TPU v7x, 128 devices: a whole 4x4x4 slice. The times are simulated.
128 devices in a mesh: rep: 16 (over y, x), ep: 8 (over z, core).
Axes of the slice: x: 4, y: 4, z: 4, core: 2. Of those that a mesh axis runs over, the one named last changes fastest.
Arguments:
- tokens: bfloat16 [16384, 2048], P(('rep', 'ep')), may hold values from -24 to 24
- experts: int32 [16384, 2], P(('rep', 'ep')), may hold values from 0 to 7, all different within a row; in each aligned block of 128 rows (0 to 127, 128 to 255, ...) at most 48 rows name the same one
- gates: bfloat16 [16384, 2], P(('rep', 'ep')), may hold values from 0.099609375 to 1
- w_gate: bfloat16 [8, 2048, 1408], P('ep'), may hold values from -0.125 to 0.125
- w_up: bfloat16 [8, 2048, 1408], P('ep'), may hold values from -0.125 to 0.125
- w_down: bfloat16 [8, 1408, 2048], P('ep'), may hold values from -0.15625 to 0.15625
- cotangent: bfloat16 [16384, 2048], P(('rep', 'ep')), may hold values from -1.1953125 to 1.1953125
Outputs:
- layer_out: bfloat16 [16384, 2048], P(('rep', 'ep'))
- input_grads: bfloat16 [16384, 2048], P(('rep', 'ep'))
- gate_grads: bfloat16 [16384, 2], P(('rep', 'ep'))
- grad_gate: float32 [8, 2048, 1408], P('ep', 'rep')
- grad_up: float32 [8, 2048, 1408], P('ep', 'rep')
- grad_down: float32 [8, 1408, 2048], P('ep', 'rep')
Inputs may be any that keep to these rules, and one draw needn't show every extreme that they name: Each row names 2 different experts; the rows of one device name no expert more than 48 times, a bound that some block reaches.
All inputs are finite; a program needn't handle non-finite values.
Results may differ from a plain program's by a relative error of at most 0.013.
Values may be sent and summed in bfloat16 or wider, within the bound.
No kernel may reach another device: no remote copies, remote signals or barrier semaphores. Data moves between devices by JAX's collectives and lax.ppermute only.
A program may use at most 128 MiB of HBM per device.

v0:
```python
import jax
import jax.numpy as jnp
from jax import lax
from jax.sharding import PartitionSpec as P


def expert_forward(gate_mat, up_mat, down_mat, rows):
    sources, piece, model_width = rows.shape
    flat_rows = rows.reshape(sources * piece, model_width)
    gate_pre = jnp.dot(flat_rows, gate_mat, preferred_element_type=jnp.float32)
    up_pre = jnp.dot(flat_rows, up_mat, preferred_element_type=jnp.float32)
    activated = gate_pre * jax.nn.sigmoid(gate_pre)
    hidden = (activated * up_pre).astype(jnp.bfloat16)
    expert_out = jnp.dot(hidden, down_mat, preferred_element_type=jnp.float32).astype(jnp.bfloat16)
    ff_width = gate_pre.shape[1]
    return (
        expert_out.reshape(sources, piece, model_width),
        rows,
        gate_pre.reshape(sources, piece, ff_width),
        up_pre.reshape(sources, piece, ff_width),
    )


def expert_backward(out_grads, gate_pre, up_pre, gate_mat, up_mat, down_mat):
    contract = (((1,), (1,)), ((), ()))
    hidden_grad = lax.dot_general(out_grads, down_mat, contract, preferred_element_type=jnp.float32)
    sigmoid_g = jax.nn.sigmoid(gate_pre)
    activated = gate_pre * sigmoid_g
    gate_delta = (hidden_grad * up_pre * sigmoid_g * (1.0 + gate_pre * (1.0 - sigmoid_g))).astype(
        jnp.bfloat16
    )
    up_delta = (hidden_grad * activated).astype(jnp.bfloat16)
    hidden = (activated * up_pre).astype(jnp.bfloat16)
    row_grads = (
        lax.dot_general(gate_delta, gate_mat, contract, preferred_element_type=jnp.float32)
        + lax.dot_general(up_delta, up_mat, contract, preferred_element_type=jnp.float32)
    ).astype(jnp.bfloat16)
    return (gate_delta, up_delta, hidden, row_grads)


def body(tokens, experts, gates, w_gate, w_up, w_down, cotangent):
    tok_rows, model_width = tokens.shape
    top_count = experts.shape[1]
    n_experts = lax.axis_size("ep")
    capacity = 3 * tok_rows * top_count // (2 * n_experts)
    pair_count = tok_rows * top_count
    gate_mat, up_mat, down_mat = (w_gate[0], w_up[0], w_down[0])
    ff_width = gate_mat.shape[1]
    flat_exp = experts.reshape(pair_count)
    onehot = (flat_exp[:, None] == jnp.arange(n_experts, dtype=jnp.int32)[None, :]).astype(
        jnp.int32
    )
    slot_rank = jnp.sum((jnp.cumsum(onehot, axis=0) - onehot) * onehot, axis=1)
    slot_index = flat_exp * capacity + slot_rank
    source = (
        jnp.zeros((n_experts * capacity,), jnp.int32)
        .at[slot_index]
        .set(jnp.arange(pair_count, dtype=jnp.int32))
    )
    filled = jnp.zeros((n_experts * capacity,), jnp.bfloat16).at[slot_index].set(1.0)
    token_src = source // top_count
    dispatch = (tokens[token_src] * filled[:, None]).reshape(n_experts, capacity, model_width)
    expert_out, rows_in, gate_pre, up_pre = expert_forward(
        gate_mat,
        up_mat,
        down_mat,
        lax.all_to_all(dispatch, "ep", split_axis=0, concat_axis=0, tiled=True),
    )
    returned = lax.all_to_all(expert_out, "ep", split_axis=0, concat_axis=0, tiled=True)
    pair_out = returned.reshape(n_experts * capacity, model_width)[slot_index]
    weights = gates.reshape(pair_count, 1).astype(jnp.float32)
    layer_out = jnp.sum(
        (weights * pair_out.astype(jnp.float32)).reshape(tok_rows, top_count, model_width), axis=1
    ).astype(jnp.bfloat16)
    flat_rows = rows_in.reshape(n_experts * capacity, model_width)
    gate_pre = gate_pre.reshape(n_experts * capacity, ff_width)
    up_pre = up_pre.reshape(n_experts * capacity, ff_width)
    gate_grads = jnp.einsum(
        "tkd,td->tk",
        pair_out.reshape(tok_rows, top_count, model_width),
        cotangent,
        preferred_element_type=jnp.float32,
    ).astype(jnp.bfloat16)
    scaled = (weights * jnp.repeat(cotangent, top_count, axis=0).astype(jnp.float32)).astype(
        jnp.bfloat16
    )
    grad_disp = (scaled[source] * filled[:, None]).reshape(n_experts, capacity, model_width)
    out_grads = lax.all_to_all(grad_disp, "ep", split_axis=0, concat_axis=0, tiled=True).reshape(
        n_experts * capacity, model_width
    )
    gate_delta, up_delta, hidden, row_grads = expert_backward(
        out_grads, gate_pre, up_pre, gate_mat, up_mat, down_mat
    )
    back_rows = lax.all_to_all(
        row_grads.reshape(n_experts, capacity, model_width),
        "ep",
        split_axis=0,
        concat_axis=0,
        tiled=True,
    )
    pair_grads = back_rows.reshape(n_experts * capacity, model_width)[slot_index]
    input_grads = jnp.sum(
        pair_grads.astype(jnp.float32).reshape(tok_rows, top_count, model_width), axis=1
    ).astype(jnp.bfloat16)
    rows_first = (((0,), (0,)), ((), ()))
    term_gate = lax.dot_general(
        flat_rows, gate_delta, rows_first, preferred_element_type=jnp.float32
    )
    term_up = lax.dot_general(flat_rows, up_delta, rows_first, preferred_element_type=jnp.float32)
    term_down = lax.dot_general(hidden, out_grads, rows_first, preferred_element_type=jnp.float32)
    grad_gate, grad_up, grad_down = (
        lax.psum_scatter(
            term_gate.astype(jnp.bfloat16), "rep", scatter_dimension=0, tiled=True
        ).astype(jnp.float32),
        lax.psum_scatter(
            term_up.astype(jnp.bfloat16), "rep", scatter_dimension=0, tiled=True
        ).astype(jnp.float32),
        lax.psum_scatter(
            term_down.astype(jnp.bfloat16), "rep", scatter_dimension=0, tiled=True
        ).astype(jnp.float32),
    )
    return (layer_out, input_grads, gate_grads, grad_gate[None], grad_up[None], grad_down[None])


def solution(mesh):
    in_specs = (
        P(("rep", "ep"), None),
        P(("rep", "ep"), None),
        P(("rep", "ep"), None),
        P("ep", None, None),
        P("ep", None, None),
        P("ep", None, None),
        P(("rep", "ep"), None),
    )
    out_specs = (
        P(("rep", "ep"), None),
        P(("rep", "ep"), None),
        P(("rep", "ep"), None),
        P("ep", "rep", None),
        P("ep", "rep", None),
        P("ep", "rep", None),
    )
    return jax.shard_map(body, mesh=mesh, in_specs=in_specs, out_specs=out_specs, check_vma=False)
```

profile of v0, /device:TPU:1, one launch (start us, length us, event | category | flops | bytes accessed | tf_op | source)
XLA Modules:
  0.0 354.4 jit_solution(1229702816602289421)
XLA Ops:
  7.2 0.0 copy-start
  7.2 0.8 copy.21
  8.0 0.1 eq.29
  8.2 0.1 eq.25
  8.3 0.7 broadcast_multiply_fusion.2
  9.0 0.6 reduce-window.6
  9.6 0.2 slice_reduce_fusion
  9.8 0.1 copy.20
  9.9 0.1 mul.80
  10.1 0.1 fusion.21
  10.2 1.4 scatter_custom_fusion
  11.6 0.8 copy.19
  12.4 0.1 reshape.120
  12.5 2.1 broadcast_in_dim.43
  14.6 2.5 convert_element_type.82
  17.1 2.2 scatter_custom_fusion.1
  19.3 0.1 mul.82
  19.4 1.8 multiply_convert_fusion.3
  21.2 2.5 gather_fusion.2
  23.6 0.0 copy-done
  23.6 3.1 gather_fusion
  26.8 2.8 broadcast_multiply_fusion
  29.6 27.1 %all_to_all.20 = bf16[8,48,2048]{2,1,0:T(8,128)(2,1)S(1)} all-to-all(bf16[8,48,2048]{2,1,0:T(8,128)(2,1)S(1)} %get-tuple-element.10), channel_id=1, replica_groups=mesh['rep'=16,'ep'=8] {'ep'}, dimensions={0} | all-to-all | bytes 3145728 | tf_op jit(solution)/shard_map/all_to_all | solution.py:67
  56.7 4.5 %all-to-all-start.2 = ((bf16[8,48,2048]{2,1,0:T(8,128)(2,1)}), bf16[8,48,2048]{2,1,0:T(8,128)(2,1)S(1)}, u32[]{:S(2)}, u32[]{:S(2)}) async-start(bf16[8,48,2048]{2,1,0:T(8,128)(2,1)} %get-tuple-element.9), calls=%async_computation.2 | async-start | bytes 3145728 | tf_op jit(solution)/shard_map/all_to_all | solution.py:88
  61.3 0.0 reduce-scatter.10.cloned.1.call-start
  61.3 6.6 %fusion.6 = f32[384,1408]{1,0:T(8,128)} fusion(bf16[384,2048]{1,0:T(8,128)(2,1)S(1)} %bitcast.70, bf16[1,2048,1408]{2,1,0:T(8,128)(2,1)} %param.11), kind=kOutput, calls=%fused_computation.15 | convolution fusion | flops 2214592512 | bytes 9502720 | tf_op jit(solution)/shard_map/dot_general | solution.py:11
  67.8 14.0 %all-to-all-done.2 = bf16[8,48,2048]{2,1,0:T(8,128)(2,1)S(1)} async-done(((bf16[8,48,2048]{2,1,0:T(8,128)(2,1)}), bf16[8,48,2048]{2,1,0:T(8,128)(2,1)S(1)}, u32[]{:S(2)}, u32[]{:S(2)}) %all-to-all-start.2) | async-done | bytes 1572896 | tf_op jit(solution)/shard_map/all_to_all | solution.py:88
  81.9 5.4 %fusion = f32[384,1408]{1,0:T(8,128)S(1)} fusion(bf16[384,2048]{1,0:T(8,128)(2,1)S(1)} %bitcast.74, bf16[1,1408,2048]{2,1,0:T(8,128)(2,1)} %param.12), kind=kOutput, calls=%fused_computation.9 | convolution fusion | flops 2214592512 | bytes 9502720 | tf_op jit(solution)/shard_map/dot_general | solution.py:26
  87.3 0.0 copy-done.7
  87.3 7.2 %multiply_convert_fusion.1 = (bf16[384,1408]{1,0:T(8,128)(2,1)}, bf16[384,1408]{1,0:T(8,128)(2,1)}, bf16[384,1408]{1,0:T(8,128)(2,1)S(1)}) fusion(f32[384,1408]{1,0:T(8,128)S(1)} %fusion, f32[384,1408]{1,0:T(8,128)S(1)} %copy-done.7, bf16[384,2048]{1,0:T(8,128)(2,1)S(1)} %bitcast.71, bf16[1,2048,1408]{2,1,0:T(8,128)(2,1)} %param.10), kind=kOutput, calls=%fused_computation.24 | convolution fusion | flops 2222702592 | bytes 14909440 | tf_op jit(solution)/shard_map/dot_general | solution.py:10
  94.5 1.0 copy-done.3
  95.5 5.0 %convolution_convert_fusion = bf16[1408,2048]{1,0:T(8,128)(2,1)} fusion(bf16[384,1408]{1,0:T(8,128)(2,1)S(1)} %get-tuple-element.8, bf16[384,2048]{1,0:T(8,128)(2,1)S(1)} %bitcast.75), kind=kOutput, calls=%fused_computation.6 | convolution fusion | flops 2217476096 | bytes 8421376 | tf_op jit(solution)/shard_map/dot_general | solution.py:110
  100.6 0.0 reduce-scatter.10.cloned.1.call-update
  100.6 0.0 reduce-scatter.8.cloned.1.call-start
  100.6 1.2 copy-done.6
  101.8 5.2 %convolution_convert_fusion.1 = bf16[2048,1408]{1,0:T(8,128)(2,1)} fusion(bf16[384,2048]{1,0:T(8,128)(2,1)S(1)} %bitcast.72, bf16[384,1408]{1,0:T(8,128)(2,1)S(1)} %copy-done.6), kind=kOutput, calls=%fused_computation.7 | convolution fusion | flops 2217476096 | bytes 8421376 | tf_op jit(solution)/shard_map/dot_general | solution.py:109
  107.0 0.0 reduce-scatter.8.cloned.1.call-update
  107.0 0.0 reduce-scatter.6.cloned.1.call-start
  107.1 1.2 copy-done.5
  108.2 5.1 %convolution_convert_fusion.2 = bf16[2048,1408]{1,0:T(8,128)(2,1)} fusion(bf16[384,2048]{1,0:T(8,128)(2,1)S(1)} %bitcast.73, bf16[384,1408]{1,0:T(8,128)(2,1)S(1)} %copy-done.5), kind=kOutput, calls=%fused_computation.8 | convolution fusion | flops 2217476096 | bytes 8421376 | tf_op jit(solution)/shard_map/dot_general | solution.py:106
  113.4 0.0 reduce-scatter.6.cloned.1.call-update
  113.4 0.0 slice-start.1
  113.4 5.2 %fusion.4 = f32[384,2048]{1,0:T(8,128)S(1)} fusion(bf16[384,1408]{1,0:T(8,128)(2,1)} %get-tuple-element.7, bf16[1,2048,1408]{2,1,0:T(8,128)(2,1)} %param.11), kind=kOutput, calls=%fused_computation.13 | convolution fusion | flops 2214592512 | bytes 9994240 | tf_op jit(solution)/shard_map/dot_general | solution.py:36
  118.6 3.8 %add_convert_fusion = bf16[384,2048]{1,0:T(8,128)(2,1)} fusion(f32[384,2048]{1,0:T(8,128)S(1)} %fusion.4, bf16[384,1408]{1,0:T(8,128)(2,1)S(1)} %copy-done.5, bf16[1,2048,1408]{2,1,0:T(8,128)(2,1)S(1)} %bitcast.84), kind=kOutput, calls=%fused_computation.21 | convolution fusion | flops 2216165376 | bytes 11567104 | tf_op jit(solution)/shard_map/dot_general | solution.py:35
  122.5 4.5 %all-to-all-start.3 = ((bf16[8,48,2048]{2,1,0:T(8,128)(2,1)}), bf16[8,48,2048]{2,1,0:T(8,128)(2,1)S(1)}, u32[]{:S(2)}, u32[]{:S(2)}) async-start(bf16[8,48,2048]{2,1,0:T(8,128)(2,1)} %bitcast.13), calls=%async_computation.3 | async-start | bytes 3145728 | tf_op jit(solution)/shard_map/all_to_all | solution.py:94
  127.0 6.5 %fusion.14 = bf16[384,2048]{1,0:T(8,128)(2,1)} fusion(bf16[384,1408]{1,0:T(8,128)(2,1)S(1)} %copy-done.4, bf16[1,1408,2048]{2,1,0:T(8,128)(2,1)} %param.12), kind=kOutput, calls=%fused_computation.22 | convolution fusion | flops 2215378944 | bytes 8421376 | tf_op jit(solution)/shard_map/dot_general | solution.py:14
  133.5 14.1 %all-to-all-done.3 = bf16[8,48,2048]{2,1,0:T(8,128)(2,1)S(1)} async-done(((bf16[8,48,2048]{2,1,0:T(8,128)(2,1)}), bf16[8,48,2048]{2,1,0:T(8,128)(2,1)S(1)}, u32[]{:S(2)}, u32[]{:S(2)}) %all-to-all-start.3) | async-done | bytes 1572896 | tf_op jit(solution)/shard_map/all_to_all | solution.py:94
  147.6 4.5 %all-to-all-start.1 = ((bf16[8,48,2048]{2,1,0:T(8,128)(2,1)}), bf16[8,48,2048]{2,1,0:T(8,128)(2,1)S(1)}, u32[]{:S(2)}, u32[]{:S(2)}) async-start(bf16[8,48,2048]{2,1,0:T(8,128)(2,1)} %bitcast.76), calls=%async_computation.1 | async-start | bytes 3145728 | tf_op jit(solution)/shard_map/all_to_all | solution.py:69
  152.1 2.4 gather_fusion.3
  154.4 1.7 gather.27
  156.2 3.6 %reduce_sum.35 = bf16[128,2048]{1,0:T(8,128)(2,1)} reduce(bf16[128,2,2048]{2,1,0:T(2,128)(2,1)S(1)} %gather.27, bf16[]{:T(256)} %constant.33.clone.1), dimensions={1}, to_apply=%region_6.7 | reduce | flops 262144 | bytes 1572866 | tf_op jit(solution)/shard_map/reduce_sum | solution.py:102
  159.8 12.9 %all-to-all-done.1 = bf16[8,48,2048]{2,1,0:T(8,128)(2,1)S(1)} async-done(((bf16[8,48,2048]{2,1,0:T(8,128)(2,1)}), bf16[8,48,2048]{2,1,0:T(8,128)(2,1)S(1)}, u32[]{:S(2)}, u32[]{:S(2)}) %all-to-all-start.1) | async-done | bytes 1572896 | tf_op jit(solution)/shard_map/all_to_all | solution.py:69
  172.7 1.4 gather_fusion.1
  174.0 0.0 copy-start.2
  174.1 0.7 gather.23
  174.8 0.3 copy-done.2
  175.1 2.3 fusion.18
  177.4 0.6 copy.25
  178.0 3.9 %multiply_reduce_fusion = bf16[128,2048]{1,0:T(8,128)(2,1)} fusion(bf16[128,2,2048]{2,1,0:T(2,128)(2,1)S(1)} %gather.23, f32[128,2]{1,0:T(8,128)S(1)} %copy.19), kind=kLoop, calls=%fused_computation.29 | loop fusion | flops 1310720 | bytes 1573888 | tf_op jit(solution)/shard_map/reduce_sum | solution.py:72
  181.9 1.9 bitcast_convert_fusion
  183.8 78.8 %reduce-scatter.8.cloned.1.call-done = bf16[128,1408]{1,0:T(8,128)(2,1)} async-done(((bf16[2048,1408]{1,0:T(8,128)(2,1)}), bf16[128,1408]{1,0:T(8,128)(2,1)}) %reduce-scatter.8.cloned.1.call-update) | async-done | bytes 360464 | tf_op jit(solution)/shard_map/reduce_scatter | solution.py:115
  262.6 1.9 bitcast_convert_fusion.1
  264.4 81.5 %reduce-scatter.6.cloned.1.call-done = bf16[128,1408]{1,0:T(8,128)(2,1)} async-done(((bf16[2048,1408]{1,0:T(8,128)(2,1)}), bf16[128,1408]{1,0:T(8,128)(2,1)}) %reduce-scatter.6.cloned.1.call-update) | async-done | bytes 360464 | tf_op jit(solution)/shard_map/reduce_scatter | solution.py:112
  346.0 1.9 bitcast_convert_fusion.2
  (22 shorter events, 0.1 us)
Async XLA Ops:
  7.2 16.5 %copy-start = (bf16[128,2048]{1,0:T(8,128)(2,1)S(1)}, bf16[128,2048]{1,0:T(8,128)(2,1)}, u32[]{:S(2)}) copy-start(bf16[128,2048]{1,0:T(8,128)(2,1)} %param.7) | copy-start | bytes 1572868
  56.7 25.1 %all-to-all-start.2 = ((bf16[8,48,2048]{2,1,0:T(8,128)(2,1)}), bf16[8,48,2048]{2,1,0:T(8,128)(2,1)S(1)}, u32[]{:S(2)}, u32[]{:S(2)}) async-start(bf16[8,48,2048]{2,1,0:T(8,128)(2,1)} %get-tuple-element.9), calls=%async_computation.2 | async-start | bytes 3145728 | tf_op jit(solution)/shard_map/all_to_all | solution.py:88
  61.3 120.6 %reduce-scatter.10.cloned.1.call-start = ((), (), s32[]{:S(2)}) async-start(), calls=%async_computation.9 | async-start | bytes 6127616
  81.9 5.4 %copy-start.7 = (f32[384,1408]{1,0:T(8,128)S(1)}, f32[384,1408]{1,0:T(8,128)}, u32[]{:S(2)}) copy-start(f32[384,1408]{1,0:T(8,128)} %fusion.6) | copy-start | bytes 6488068
  94.5 1.0 copy-start.3
  100.6 1.2 copy-start.6
  100.6 162.0 %reduce-scatter.8.cloned.1.call-start = ((), (), s32[]{:S(2)}) async-start(), calls=%async_computation.8 | async-start | bytes 6127616 | tf_op jit(solution)/shard_map/reduce_scatter | solution.py:115
  107.0 1.2 copy-start.5
  107.0 239.0 %reduce-scatter.6.cloned.1.call-start = ((), (), s32[]{:S(2)}) async-start(), calls=%async_computation.7 | async-start | bytes 6127616 | tf_op jit(solution)/shard_map/reduce_scatter | solution.py:112
  113.4 5.2 %slice-start = ((s8[5767168]{0:T(1024)(128)(4,1)}), s8[1572864]{0:T(1024)(128)(4,1)S(1)}, s32[]{:S(2)}) async-start(s8[5767168]{0:T(1024)(128)(4,1)} %bitcast.83), calls=%async_computation.10 | async-start | bytes 3145728
  113.4 5.2 %slice-start.1 = ((s8[5767168]{0:T(1024)(128)(4,1)}), s8[4194304]{0:T(1024)(128)(4,1)S(1)}, s32[]{:S(2)}) async-start(s8[5767168]{0:T(1024)(128)(4,1)} %bitcast.83), calls=%async_computation.11 | async-start | bytes 8388608
  122.4 4.6 %copy-start.4 = (bf16[384,1408]{1,0:T(8,128)(2,1)S(1)}, bf16[384,1408]{1,0:T(8,128)(2,1)}, u32[]{:S(2)}) copy-start(bf16[384,1408]{1,0:T(8,128)(2,1)} %copy-done.3) | copy-start | bytes 3244036
  122.5 25.2 %all-to-all-start.3 = ((bf16[8,48,2048]{2,1,0:T(8,128)(2,1)}), bf16[8,48,2048]{2,1,0:T(8,128)(2,1)S(1)}, u32[]{:S(2)}, u32[]{:S(2)}) async-start(bf16[8,48,2048]{2,1,0:T(8,128)(2,1)} %bitcast.13), calls=%async_computation.3 | async-start | bytes 3145728 | tf_op jit(solution)/shard_map/all_to_all | solution.py:94
  147.6 25.1 %all-to-all-start.1 = ((bf16[8,48,2048]{2,1,0:T(8,128)(2,1)}), bf16[8,48,2048]{2,1,0:T(8,128)(2,1)S(1)}, u32[]{:S(2)}, u32[]{:S(2)}) async-start(bf16[8,48,2048]{2,1,0:T(8,128)(2,1)} %bitcast.76), calls=%async_computation.1 | async-start | bytes 3145728 | tf_op jit(solution)/shard_map/all_to_all | solution.py:69
  174.0 1.0 copy-start.2
  178.0 169.8 %copy-start.1 = (bf16[128,2048]{1,0:T(8,128)(2,1)S(1)}, bf16[128,2048]{1,0:T(8,128)(2,1)}, u32[]{:S(2)}) copy-start(bf16[128,2048]{1,0:T(8,128)(2,1)} %param.7) | copy-start | bytes 1572868
Sparse Core Ops, SparseCore 0:
  100.7 78.6 reduce-scatter.9
  182.7 79.7 reduce-scatter.7
  265.9 79.9 reduce-scatter.5
where the time goes:
time: 356 us; the launch traced here: 354 us
  waiting for transfers between devices  201 us (56%)
  matrix products  52.4 us (15%)
  blocking collectives  27.1 us (8%)
  local copies, waits for them, and re-layouts  26.8 us (8%)
  other arithmetic  19.2 us (5%)
  between operations  13.9 us (4%)
  starting transfers between devices  13.6 us (4%)
    reduce_scatter x1, waiting for transfers between devices, body(): lax.psum_scatter(term_gate.astype(jnp.bfloat16), 'rep', scatter_dimension...  81.5 us
    reduce_scatter x1, waiting for transfers between devices, body(): lax.psum_scatter(term_up.astype(jnp.bfloat16), 'rep', scatter_dimension=0...  78.8 us
    all_to_all x1, blocking collectives, body(): lax.all_to_all(dispatch, 'ep', split_axis=0, concat_axis=0, tiled=True)  27.1 us
    all_to_all x1, waiting for transfers between devices, body(): lax.all_to_all(row_grads.reshape(n_experts, capacity, model_width), 'ep',...  14.1 us
    all_to_all x1, waiting for transfers between devices, body(): lax.all_to_all(grad_disp, 'ep', split_axis=0, concat_axis=0, tiled=True)  14 us
    all_to_all x1, waiting for transfers between devices, body(): lax.all_to_all(expert_out, 'ep', split_axis=0, concat_axis=0, tiled=True)  12.9 us
    dot_general x1, matrix products, expert_forward(): gate_pre = jnp.dot(flat_rows, gate_mat, preferred_element_type=jnp.float32)  7.24 us
  transfers between devices with their start and end apart: 6, of which 5 were waited for; matrix products, arithmetic and copies ran while one was open for 15% of the time, Pallas kernels for 0%

commit v1 on v0

v1 whole, which is shorter than its diff:
```python
import jax
import jax.numpy as jnp
from jax import lax
from jax.sharding import PartitionSpec as P


def body(tokens, experts, gates, w_gate, w_up, w_down, cotangent):
    tok_rows, model_width = tokens.shape
    top_count = experts.shape[1]
    n_experts = lax.axis_size("ep")
    n_rep = lax.axis_size("rep")
    capacity = 3 * tok_rows * top_count // (2 * n_experts)
    pair_count = tok_rows * top_count
    gate_mat, up_mat, down_mat = (w_gate[0], w_up[0], w_down[0])
    ff_width = gate_mat.shape[1]
    slots = n_experts * capacity

    flat_exp = experts.reshape(pair_count)
    onehot = (flat_exp[:, None] == jnp.arange(n_experts, dtype=jnp.int32)[None, :]).astype(
        jnp.int32
    )
    slot_rank = jnp.sum((jnp.cumsum(onehot, axis=0) - onehot) * onehot, axis=1)
    slot_index = flat_exp * capacity + slot_rank
    source = jnp.zeros((slots,), jnp.int32).at[slot_index].set(
        jnp.arange(pair_count, dtype=jnp.int32)
    )
    filled = jnp.zeros((slots,), jnp.bfloat16).at[slot_index].set(1.0)
    token_src = source // top_count
    weights = gates.reshape(pair_count, 1).astype(jnp.float32)
    scaled = (weights * jnp.repeat(cotangent, top_count, axis=0).astype(jnp.float32)).astype(
        jnp.bfloat16
    )

    disp = jnp.concatenate(
        [tokens[token_src] * filled[:, None], scaled[source] * filled[:, None]], axis=1
    ).reshape(n_experts, capacity, 2 * model_width)
    recv = lax.all_to_all(disp, "ep", split_axis=0, concat_axis=0, tiled=True).reshape(
        slots, 2 * model_width
    )
    rows_in = recv[:, :model_width]
    out_grads = recv[:, model_width:]

    contract = (((1,), (1,)), ((), ()))
    rows_first = (((0,), (0,)), ((), ()))
    gate_pre = jnp.dot(rows_in, gate_mat, preferred_element_type=jnp.float32)
    up_pre = jnp.dot(rows_in, up_mat, preferred_element_type=jnp.float32)
    sigmoid_g = jax.nn.sigmoid(gate_pre)
    activated = gate_pre * sigmoid_g
    hidden = (activated * up_pre).astype(jnp.bfloat16)
    hidden_grad = lax.dot_general(out_grads, down_mat, contract, preferred_element_type=jnp.float32)
    gate_delta = (hidden_grad * up_pre * sigmoid_g * (1.0 + gate_pre * (1.0 - sigmoid_g))).astype(
        jnp.bfloat16
    )
    up_delta = (hidden_grad * activated).astype(jnp.bfloat16)

    deltas = jnp.concatenate([gate_delta, up_delta], axis=1)
    term_gu = lax.dot_general(
        rows_in, deltas, rows_first, preferred_element_type=jnp.float32
    ).astype(jnp.bfloat16)
    term_down = lax.dot_general(
        hidden, out_grads, rows_first, preferred_element_type=jnp.float32
    ).astype(jnp.bfloat16)
    gu_rows = model_width // n_rep
    down_rows = ff_width // n_rep
    gu_chunk = gu_rows * 2 * ff_width // model_width
    packed = jnp.concatenate(
        [
            term_gu.reshape(n_rep, gu_chunk, model_width),
            term_down.reshape(n_rep, down_rows, model_width),
        ],
        axis=1,
    ).reshape(n_rep * (gu_chunk + down_rows), model_width)
    reduced = lax.optimization_barrier(
        lax.psum_scatter(packed, "rep", scatter_dimension=0, tiled=True)
    )
    red_gu = reduced[:gu_chunk].reshape(gu_rows, 2 * ff_width).astype(jnp.float32)
    grad_gate = red_gu[:, :ff_width]
    grad_up = red_gu[:, ff_width:]
    grad_down = reduced[gu_chunk:].astype(jnp.float32)

    expert_out = jnp.dot(hidden, down_mat, preferred_element_type=jnp.float32).astype(jnp.bfloat16)
    row_grads = (
        lax.dot_general(gate_delta, gate_mat, contract, preferred_element_type=jnp.float32)
        + lax.dot_general(up_delta, up_mat, contract, preferred_element_type=jnp.float32)
    ).astype(jnp.bfloat16)
    back = jnp.concatenate([expert_out, row_grads], axis=1).reshape(
        n_experts, capacity, 2 * model_width
    )
    returned = lax.all_to_all(back, "ep", split_axis=0, concat_axis=0, tiled=True).reshape(
        slots, 2 * model_width
    )
    pair_back = returned[slot_index]
    pair_out = pair_back[:, :model_width]
    pair_grads = pair_back[:, model_width:]
    layer_out = jnp.sum(
        (weights * pair_out.astype(jnp.float32)).reshape(tok_rows, top_count, model_width), axis=1
    ).astype(jnp.bfloat16)
    gate_grads = jnp.einsum(
        "tkd,td->tk",
        pair_out.reshape(tok_rows, top_count, model_width),
        cotangent,
        preferred_element_type=jnp.float32,
    ).astype(jnp.bfloat16)
    input_grads = jnp.sum(
        pair_grads.astype(jnp.float32).reshape(tok_rows, top_count, model_width), axis=1
    ).astype(jnp.bfloat16)
    return (layer_out, input_grads, gate_grads, grad_gate[None], grad_up[None], grad_down[None])


def solution(mesh):
    in_specs = (
        P(("rep", "ep"), None),
        P(("rep", "ep"), None),
        P(("rep", "ep"), None),
        P("ep", None, None),
        P("ep", None, None),
        P("ep", None, None),
        P(("rep", "ep"), None),
    )
    out_specs = (
        P(("rep", "ep"), None),
        P(("rep", "ep"), None),
        P(("rep", "ep"), None),
        P("ep", "rep", None),
        P("ep", "rep", None),
        P("ep", "rep", None),
    )
    return jax.shard_map(body, mesh=mesh, in_specs=in_specs, out_specs=out_specs, check_vma=False)
```

time: 356 us -> 266 us (0.75)
  waiting for transfers between devices: 201 us -> 67.1 us
  other arithmetic: 19.2 us -> 45.1 us
  local copies, waits for them, and re-layouts: 26.8 us -> 49.4 us
  blocking collectives: 27.1 us -> 44.5 us
  matrix products: 52.4 us -> 40 us
  starting transfers between devices: 13.6 us -> 4.6 us
    reduce_scatter x2 -> x0, waiting for transfers between devices: 160 us -> none  [the longest x1 81.5 us: body(): lax.psum_scatter(term_gate.astype(jnp.bfloat16), 'rep', scatter_dimension...]
    unnamed x4 -> x2, waiting for transfers between devices: 0.05 us -> 29.6 us
    concatenate x0 -> x3, other arithmetic: none -> 28.1 us  [the longest x1 25.8 us: body(): jnp.concatenate([term_gu.reshape(n_rep, gu_chunk, model_width), term_down...]
    reshape x0 -> x4, local copies, waits for them, and re-layouts: none -> 25.9 us  [the longest x1 19.6 us: body(): term_gu.reshape(n_rep, gu_chunk, model_width)]
    all_to_all x1, blocking collectives: 27.1 us -> 44.5 us  [body(): lax.all_to_all(disp, 'ep', split_axis=0, concat_axis=0, tiled=True)]
    dot_general x8 -> x7, matrix products: 45.1 us -> 31.6 us  [the longest x1 8.95 us: body(): lax.dot_general(rows_in, deltas, rows_first, preferred_element_type=jnp.f...]
    all_to_all x3 -> x1, starting transfers between devices: 13.5 us -> 4.57 us  [body(): lax.all_to_all(back, 'ep', split_axis=0, concat_axis=0, tiled=True)]
    broadcast_in_dim x2 -> x0, other arithmetic: 3.78 us -> none  [the longest x1 1.89 us: body(): grad_up[None]]
  transfers between devices with their start and end apart: 6 -> 2, of which waited for: 5 -> 2; matrix products, arithmetic and copies ran while one was open for 15% -> 15% of each run, Pallas kernels for 0% -> 0%
where the time goes in v1:
time: 266 us; the launch traced here: 265 us
  waiting for transfers between devices  67.1 us (25%)
  local copies, waits for them, and re-layouts  49.4 us (19%)
  other arithmetic  45.1 us (17%)
  blocking collectives  44.5 us (17%)
  matrix products  40 us (15%)
  between operations  14.6 us (5%)
  starting transfers between devices  4.6 us (2%)
    all_to_all x1, blocking collectives, body(): lax.all_to_all(disp, 'ep', split_axis=0, concat_axis=0, tiled=True)  44.5 us
    all_to_all x1, waiting for transfers between devices, body(): lax.all_to_all(back, 'ep', split_axis=0, concat_axis=0, tiled=True)  37.5 us
    unnamed x2, waiting for transfers between devices  29.6 us
    concatenate x1, other arithmetic, body(): jnp.concatenate([term_gu.reshape(n_rep, gu_chunk, model_width), term_down...  25.8 us
    reshape x1, local copies, waits for them, and re-layouts, body(): term_gu.reshape(n_rep, gu_chunk, model_width)  19.6 us
    dot_general x1, matrix products, body(): lax.dot_general(rows_in, deltas, rows_first, preferred_element_type=jnp.f...  8.95 us
    dot_general x1, matrix products, body(): lax.dot_general(gate_delta, gate_mat, contract, preferred_element_type=jn...  6.11 us
    dot_general x1, matrix products, body(): jnp.dot(hidden, down_mat, preferred_element_type=jnp.float32)  5.38 us
  transfers between devices with their start and end apart: 2, of which 2 were waited for; matrix products, arithmetic and copies ran while one was open for 15% of the time, Pallas kernels for 0%

profile of v1, /device:TPU:1, one launch (start us, length us, event | category | flops | bytes accessed | tf_op | source)
XLA Modules:
  0.0 265.2 jit_solution(6358231677387240398)
XLA Ops:
  7.2 0.0 copy-start
  7.2 0.0 reduce-scatter.4.cloned.1.call-start
  7.2 0.7 broadcast_multiply_fusion.2
  8.0 0.8 copy.19
  8.7 0.1 eq.29
  8.9 0.1 eq.25
  9.0 0.1 copy.18
  9.1 0.1 mul.75
  9.3 0.6 reduce-window.6
  9.9 0.2 slice_reduce_fusion
  10.1 0.1 fusion.30
  10.3 2.2 scatter_custom_fusion.1
  12.4 0.1 mul.77
  12.5 1.4 scatter_custom_fusion
  13.9 0.8 copy.17
  14.7 0.1 reshape.129
  14.8 2.1 broadcast_in_dim.36
  16.9 2.5 convert_element_type.74
  19.4 0.0 copy-done
  19.4 0.0 copy-start.4
  19.4 3.1 %gather_fusion = bf16[384,2048]{1,0:T(8,128)(2,1)} fusion(bf16[128,2048]{1,0:T(8,128)(2,1)S(1)} %copy-done, s32[1024]{0:T(1024)S(1)} %get-tuple-element.18), kind=kCustom, calls=%fused_computation | custom fusion | bytes 3147264 | tf_op jit(solution)/shard_map/gather | solution.py:35
  22.6 0.2 multiply_convert_fusion.3
  22.8 3.1 %gather_fusion.1 = bf16[384,2048]{1,0:T(8,128)(2,1)} fusion(bf16[256,2048]{1,0:T(8,128)(2,1)S(1)} %multiply_convert_fusion.3, s32[1024]{0:T(1024)S(1)} %get-tuple-element.17), kind=kCustom, calls=%fused_computation.1 | custom fusion | bytes 3147264 | tf_op jit(solution)/shard_map/gather | solution.py:35
  25.9 1.8 broadcast_multiply_fusion.1
  27.7 0.0 slice-start.1
  27.7 0.3 pad_maximum_fusion.1
  28.1 0.0 slice-start.6
  28.1 44.5 %all_to_all.10 = bf16[8,48,4096]{2,1,0:T(8,128)(2,1)S(1)} all-to-all(bf16[8,48,4096]{2,1,0:T(8,128)(2,1)S(1)} %pad_maximum_fusion.1), channel_id=1, replica_groups=mesh['rep'=16,'ep'=8] {'ep'}, dimensions={0} | all-to-all | bytes 6291456 | tf_op jit(solution)/shard_map/all_to_all | solution.py:37
  72.6 0.0 slice-done.1
  72.7 0.0 slice-start.2
  72.7 2.6 fusion
  75.3 0.0 slice-done.6
  75.3 0.0 slice-start.3
  75.3 2.6 fusion.10
  78.0 3.3 %multiply_convert_fusion.2 = (bf16[384,1408]{1,0:T(8,128)(2,1)S(1)}, bf16[384,1408]{1,0:T(8,128)(2,1)S(1)}, bf16[384,1408]{1,0:T(8,128)(2,1)S(1)}) fusion(f32[384,1408]{1,0:T(8,128)S(1)} %fusion.10, f32[384,1408]{1,0:T(8,128)S(1)} %fusion, bf16[1,2048,1408]{2,1,0:T(8,128)(2,1)S(1)} %bitcast.79, bf16[384,4096]{1,0:T(8,128)(2,1)S(1)} %bitcast.67), kind=kOutput, calls=%fused_computation.29 | convolution fusion | flops 2222702592 | bytes 14909440 | tf_op jit(solution)/shard_map/dot_general | solution.py:46
  81.3 5.0 %convolution_convert_fusion.1 = bf16[1408,2048]{1,0:T(8,128)(2,1)} fusion(bf16[384,1408]{1,0:T(8,128)(2,1)S(1)} %get-tuple-element.6, bf16[384,4096]{1,0:T(8,128)(2,1)S(1)} %bitcast.68), kind=kOutput, calls=%fused_computation.7 | convolution fusion | flops 2217476096 | bytes 8421376 | tf_op jit(solution)/shard_map/dot_general | solution.py:60
  86.3 8.9 %convolution_convert_fusion = bf16[2048,2816]{1,0:T(8,128)(2,1)} fusion(bf16[384,1408]{1,0:T(8,128)(2,1)S(1)} %get-tuple-element.8, bf16[384,1408]{1,0:T(8,128)(2,1)S(1)} %get-tuple-element.7, bf16[384,4096]{1,0:T(8,128)(2,1)S(1)} %bitcast.69), kind=kOutput, calls=%fused_computation.6 | convolution fusion | flops 4439277568 | bytes 15269888 | tf_op jit(solution)/shard_map/dot_general | solution.py:57
  95.2 19.6 %reshape.126 = bf16[16,176,2048]{2,1,0:T(8,128)(2,1)} reshape(bf16[2048,2816]{1,0:T(8,128)(2,1)} %convolution_convert_fusion) | data formatting | bytes 23068672 | tf_op jit(solution)/shard_map/reshape | solution.py:68
  114.8 25.8 %pad_maximum_fusion = bf16[16,264,2048]{2,1,0:T(8,128)(2,1)} fusion(bf16[16,88,2048]{2,1,0:T(8,128)(2,1)} %bitcast.64, bf16[16,176,2048]{2,1,0:T(8,128)(2,1)} %reshape.126), kind=kLoop, calls=%fused_computation.5 | loop fusion | flops 34603008 | bytes 34603008 | tf_op jit(solution)/shard_map/concatenate | solution.py:66
  140.6 0.0 slice-start.4
  140.7 0.0 reduce-scatter.4.cloned.1.call-update
  140.7 0.0 slice-start.5
  140.7 5.4 %fusion.14 = bf16[384,2048]{1,0:T(8,128)(2,1)S(1)} fusion(bf16[384,1408]{1,0:T(8,128)(2,1)S(1)} %get-tuple-element.6, bf16[1,1408,2048]{2,1,0:T(8,128)(2,1)} %param.12), kind=kOutput, calls=%fused_computation.23 | convolution fusion | flops 2215378944 | bytes 8421376 | tf_op jit(solution)/shard_map/dot_general | solution.py:81
  146.1 2.7 %fusion.4 = f32[384,2048]{1,0:T(8,128)S(1)} fusion(bf16[384,1408]{1,0:T(8,128)(2,1)S(1)} %copy-done.9, bf16[1,2048,1408]{2,1,0:T(8,128)(2,1)S(1)} %bitcast.81), kind=kOutput, calls=%fused_computation.12 | convolution fusion | flops 2214592512 | bytes 9994240 | tf_op jit(solution)/shard_map/dot_general | solution.py:84
  148.8 6.1 %add_convert_fusion = bf16[384,2048]{1,0:T(8,128)(2,1)S(1)} fusion(f32[384,2048]{1,0:T(8,128)S(1)} %fusion.4, bf16[384,1408]{1,0:T(8,128)(2,1)S(1)} %copy-done.7, bf16[1,2048,1408]{2,1,0:T(8,128)(2,1)} %param.10), kind=kOutput, calls=%fused_computation.22 | convolution fusion | flops 2216165376 | bytes 11567104 | tf_op jit(solution)/shard_map/dot_general | solution.py:83
  154.9 2.0 pad_maximum_fusion.2
  156.9 4.6 %all-to-all-start.1 = ((bf16[8,48,4096]{2,1,0:T(8,128)(2,1)}), bf16[8,48,4096]{2,1,0:T(8,128)(2,1)S(1)}, u32[]{:S(2)}, u32[]{:S(2)}) async-start(bf16[8,48,4096]{2,1,0:T(8,128)(2,1)} %bitcast.61), calls=%async_computation.1 | async-start | bytes 6291456 | tf_op jit(solution)/shard_map/all_to_all | solution.py:89
  161.5 37.5 %all-to-all-done.1 = bf16[8,48,4096]{2,1,0:T(8,128)(2,1)S(1)} async-done(((bf16[8,48,4096]{2,1,0:T(8,128)(2,1)}), bf16[8,48,4096]{2,1,0:T(8,128)(2,1)S(1)}, u32[]{:S(2)}, u32[]{:S(2)}) %all-to-all-start.1) | async-done | bytes 3145760 | tf_op jit(solution)/shard_map/all_to_all | solution.py:89
  199.0 3.2 %gather_fusion.2 = bf16[256,4096]{1,0:T(8,128)(2,1)} fusion(bf16[384,4096]{1,0:T(8,128)(2,1)S(1)} %bitcast.59, s32[1024]{0:T(1024)S(1)} %pad_clamp_fusion), kind=kCustom, calls=%fused_computation.2 | custom fusion | bytes 4195328 | tf_op jit(solution)/shard_map/gather | solution.py:92
  202.1 2.9 %convert_multiply_fusion = f32[256,2048]{1,0:T(8,128)} fusion(f32[256]{0:T(256)S(1)} %reshape.129, bf16[256,4096]{1,0:T(8,128)(2,1)} %gather_fusion.2), kind=kLoop, calls=%fused_computation.32 | loop fusion | flops 1048576 | bytes 3146752 | tf_op jit(solution)/shard_map/mul | solution.py:96
  205.0 3.7 %reshape.122 = f32[128,2,2048]{2,1,0:T(2,128)} reshape(f32[256,2048]{1,0:T(8,128)} %convert_multiply_fusion) | data formatting | bytes 4194304 | tf_op jit(solution)/shard_map/reshape | solution.py:96
  208.7 1.2 fusion.39
  209.9 0.7 reshape.125
  210.6 3.4 %fusion.26 = bf16[128,1,2]{2,1,0:T(2,128)(2,1)S(1)} fusion(bf16[128,2,2048]{2,1,0:T(2,128)(2,1)S(1)} %reshape.125, bf16[128,2048,1]{1,0,2:T(8,128)(2,1)} %bitcast.70), kind=kOutput, calls=%fused_computation.39 | convolution fusion | flops 1048576 | bytes 1573376 | tf_op jit(solution)/shard_map/tkd,td->tk/dot_general | solution.py:98
  214.0 0.6 copy.22
  214.6 1.8 reshape.123
  216.5 3.6 %reduce = bf16[128,2048]{1,0:T(8,128)(2,1)} reduce(bf16[128,2,2048]{2,1,0:T(2,128)(2,1)S(1)} %reshape.123, bf16[]{:T(256)} %constant.32.clone.1), dimensions={1}, to_apply=%region_6.7.clone | reduce | flops 262144 | bytes 1572866 | tf_op jit(solution)/shard_map/reduce_sum | solution.py:104
  220.1 3.8 %reduce_sum.31 = bf16[128,2048]{1,0:T(8,128)(2,1)} reduce(f32[128,2,2048]{2,1,0:T(2,128)S(1)} %copy-done.3, f32[]{:T(128)} %constant.36.clone.1), dimensions={1}, to_apply=%region_5.6 | reduce | flops 262144 | bytes 2621444 | tf_op jit(solution)/shard_map/reduce_sum | solution.py:95
  223.9 29.6 %reduce-scatter.4.cloned.1.call-done = bf16[264,2048]{1,0:T(8,128)(2,1)} async-done(((bf16[4224,2048]{1,0:T(8,128)(2,1)}), bf16[264,2048]{1,0:T(8,128)(2,1)}) %reduce-scatter.4.cloned.1.call-update) | async-done | bytes 1081360
  253.5 1.9 fusion.28
  255.4 1.3 slice_convert_fusion
  256.6 0.0 copy-start.1
  256.6 0.3 reshape.130
  257.0 1.2 slice_bitcast_fusion
  (37 shorter events, 0.1 us)
Async XLA Ops:
  7.2 12.3 %copy-start = (bf16[128,2048]{1,0:T(8,128)(2,1)S(1)}, bf16[128,2048]{1,0:T(8,128)(2,1)}, u32[]{:S(2)}) copy-start(bf16[128,2048]{1,0:T(8,128)(2,1)} %param.7) | copy-start | bytes 1572868
  7.2 246.3 %reduce-scatter.4.cloned.1.call-start = ((), (), s32[]{:S(2)}) async-start(), calls=%async_computation.3 | async-start | bytes 18382848
  19.4 3.1 %copy-start.4 = (f32[256,2048]{1,0:T(8,128)S(1)}, f32[256,2048]{1,0:T(8,128)}, u32[]{:S(2)}) copy-start(f32[256,2048]{1,0:T(8,128)} %convert_element_type.74) | copy-start | bytes 6291460
  22.8 3.1 %copy-start.5 = (bf16[384,2048]{1,0:T(8,128)(2,1)S(1)}, bf16[384,2048]{1,0:T(8,128)(2,1)}, u32[]{:S(2)}) copy-start(bf16[384,2048]{1,0:T(8,128)(2,1)} %gather_fusion) | copy-start | bytes 4718596
  25.9 46.7 %slice-start = ((s8[5767168]{0:T(1024)(128)(4,1)}), s8[4194304]{0:T(1024)(128)(4,1)S(1)}, s32[]{:S(2)}) async-start(s8[5767168]{0:T(1024)(128)(4,1)} %bitcast.76), calls=%async_computation.4 | async-start | bytes 8388608
  27.7 44.9 %slice-start.1 = ((s8[5767168]{0:T(1024)(128)(4,1)}), s8[1572864]{0:T(1024)(128)(4,1)S(1)}, s32[]{:S(2)}) async-start(s8[5767168]{0:T(1024)(128)(4,1)} %bitcast.76), calls=%async_computation.5 | async-start | bytes 3145728
  28.1 47.2 %slice-start.6 = ((s8[5767168]{0:T(1024)(128)(4,1)}), s8[4194304]{0:T(1024)(128)(4,1)S(1)}, s32[]{:S(2)}) async-start(s8[5767168]{0:T(1024)(128)(4,1)} %bitcast.82), calls=%async_computation.10 | async-start | bytes 8388608
  72.6 2.7 %slice-start.7 = ((s8[5767168]{0:T(1024)(128)(4,1)}), s8[1572864]{0:T(1024)(128)(4,1)S(1)}, s32[]{:S(2)}) async-start(s8[5767168]{0:T(1024)(128)(4,1)} %bitcast.82), calls=%async_computation.11 | async-start | bytes 3145728
  72.7 5.3 %slice-start.2 = ((s8[5767168]{0:T(1024)(128)(4,1)}), s8[1572864]{0:T(1024)(128)(4,1)S(1)}, s32[]{:S(2)}) async-start(s8[5767168]{0:T(1024)(128)(4,1)} %bitcast.78), calls=%async_computation.6 | async-start | bytes 3145728
  75.3 2.6 slice-start.3
  81.2 5.0 %copy-start.6 = (bf16[384,1408]{1,0:T(8,128)(2,1)}, bf16[384,1408]{1,0:T(8,128)(2,1)S(1)}, u32[]{:S(2)}) copy-start(bf16[384,1408]{1,0:T(8,128)(2,1)S(1)} %get-tuple-element.7) | copy-start | bytes 3244036
  81.2 5.0 %copy-start.8 = (bf16[384,1408]{1,0:T(8,128)(2,1)}, bf16[384,1408]{1,0:T(8,128)(2,1)S(1)}, u32[]{:S(2)}) copy-start(bf16[384,1408]{1,0:T(8,128)(2,1)S(1)} %get-tuple-element.8) | copy-start | bytes 3244036
  140.6 5.5 %slice-start.4 = ((s8[5767168]{0:T(1024)(128)(4,1)}), s8[1572864]{0:T(1024)(128)(4,1)S(1)}, s32[]{:S(2)}) async-start(s8[5767168]{0:T(1024)(128)(4,1)} %bitcast.80), calls=%async_computation.8 | async-start | bytes 3145728
  140.7 5.4 %slice-start.5 = ((s8[5767168]{0:T(1024)(128)(4,1)}), s8[4194304]{0:T(1024)(128)(4,1)S(1)}, s32[]{:S(2)}) async-start(s8[5767168]{0:T(1024)(128)(4,1)} %bitcast.80), calls=%async_computation.9 | async-start | bytes 8388608
  140.7 5.4 %copy-start.9 = (bf16[384,1408]{1,0:T(8,128)(2,1)S(1)}, bf16[384,1408]{1,0:T(8,128)(2,1)}, u32[]{:S(2)}) copy-start(bf16[384,1408]{1,0:T(8,128)(2,1)} %copy-done.8) | copy-start | bytes 3244036
  146.1 2.7 %copy-start.7 = (bf16[384,1408]{1,0:T(8,128)(2,1)S(1)}, bf16[384,1408]{1,0:T(8,128)(2,1)}, u32[]{:S(2)}) copy-start(bf16[384,1408]{1,0:T(8,128)(2,1)} %copy-done.6) | copy-start | bytes 3244036
  156.9 42.0 %all-to-all-start.1 = ((bf16[8,48,4096]{2,1,0:T(8,128)(2,1)}), bf16[8,48,4096]{2,1,0:T(8,128)(2,1)S(1)}, u32[]{:S(2)}, u32[]{:S(2)}) async-start(bf16[8,48,4096]{2,1,0:T(8,128)(2,1)} %bitcast.61), calls=%async_computation.1 | async-start | bytes 6291456 | tf_op jit(solution)/shard_map/all_to_all | solution.py:89
  205.0 3.7 %copy-start.2 = (bf16[256,4096]{1,0:T(8,128)(2,1)S(1)}, bf16[256,4096]{1,0:T(8,128)(2,1)}, u32[]{:S(2)}) copy-start(bf16[256,4096]{1,0:T(8,128)(2,1)} %gather_fusion.2) | copy-start | bytes 6291460
  214.0 6.1 %copy-start.3 = (f32[128,2,2048]{2,1,0:T(2,128)S(1)}, f32[128,2,2048]{2,1,0:T(2,128)}, u32[]{:S(2)}) copy-start(f32[128,2,2048]{2,1,0:T(2,128)} %reshape.122) | copy-start | bytes 6291460
  256.6 1.5 copy-start.1
Sparse Core Ops, SparseCore 0:
  140.8 112.6 reduce-scatter.3

commit v2 on v1

--- a/solution.py
+++ b/solution.py
@@ -1,7 +1,50 @@
 import jax
 import jax.numpy as jnp
 from jax import lax
+from jax.experimental import pallas as pl
 from jax.sharding import PartitionSpec as P
+
+
+def _pack_kernel(xt_ref, gd_ref, ud_ref, ht_ref, og_ref, o_ref):
+    ff = gd_ref.shape[1]
+    width = og_ref.shape[1]
+    rows = xt_ref.shape[0]
+    xt = xt_ref[...]
+    o_ref[0, :rows, :ff] = jnp.dot(xt, gd_ref[...], preferred_element_type=jnp.float32).astype(
+        o_ref.dtype
+    )
+    o_ref[0, :rows, ff:] = jnp.dot(xt, ud_ref[...], preferred_element_type=jnp.float32).astype(
+        o_ref.dtype
+    )
+    down = jnp.dot(
+        ht_ref[...].astype(jnp.bfloat16), og_ref[...], preferred_element_type=jnp.float32
+    )
+    o_ref[0, rows:, :width] = down.astype(o_ref.dtype)
+    o_ref[0, rows:, width:] = jnp.zeros((down.shape[0], 2 * ff - width), o_ref.dtype)
+
+
+def packed_weight_grads(rows_t, gate_delta, up_delta, hidden_t, recv, n_rep):
+    model_width, slots = rows_t.shape
+    ff = gate_delta.shape[1]
+    gu_rows = model_width // n_rep
+    down_rows = ff // n_rep
+    flops = 2 * slots * (model_width * 2 * ff + ff * model_width)
+    return pl.pallas_call(
+        _pack_kernel,
+        grid=(n_rep,),
+        in_specs=[
+            pl.BlockSpec((gu_rows, slots), lambda r: (r, 0)),
+            pl.BlockSpec((slots, ff), lambda r: (0, 0)),
+            pl.BlockSpec((slots, ff), lambda r: (0, 0)),
+            pl.BlockSpec((down_rows, slots), lambda r: (r, 0)),
+            pl.BlockSpec((slots, model_width), lambda r: (0, 1)),
+        ],
+        out_specs=pl.BlockSpec((1, gu_rows + down_rows, 2 * ff), lambda r: (r, 0, 0)),
+        out_shape=jax.ShapeDtypeStruct((n_rep, gu_rows + down_rows, 2 * ff), jnp.bfloat16),
+        cost_estimate=pl.CostEstimate(
+            flops=flops, transcendentals=0, bytes_accessed=2 * n_rep * (gu_rows + down_rows) * 2 * ff
+        ),
+    )(rows_t, gate_delta, up_delta, hidden_t, recv)
 
 
 def body(tokens, experts, gates, w_gate, w_up, w_down, cotangent):
@@ -53,30 +96,16 @@
     )
     up_delta = (hidden_grad * activated).astype(jnp.bfloat16)
 
-    deltas = jnp.concatenate([gate_delta, up_delta], axis=1)
-    term_gu = lax.dot_general(
-        rows_in, deltas, rows_first, preferred_element_type=jnp.float32
-    ).astype(jnp.bfloat16)
-    term_down = lax.dot_general(
-        hidden, out_grads, rows_first, preferred_element_type=jnp.float32
-    ).astype(jnp.bfloat16)
     gu_rows = model_width // n_rep
-    down_rows = ff_width // n_rep
-    gu_chunk = gu_rows * 2 * ff_width // model_width
-    packed = jnp.concatenate(
-        [
-            term_gu.reshape(n_rep, gu_chunk, model_width),
-            term_down.reshape(n_rep, down_rows, model_width),
-        ],
-        axis=1,
-    ).reshape(n_rep * (gu_chunk + down_rows), model_width)
+    packed = packed_weight_grads(
+        rows_in.T, gate_delta, up_delta, hidden.astype(jnp.float32).T, recv, n_rep
+    )
     reduced = lax.optimization_barrier(
         lax.psum_scatter(packed, "rep", scatter_dimension=0, tiled=True)
-    )
-    red_gu = reduced[:gu_chunk].reshape(gu_rows, 2 * ff_width).astype(jnp.float32)
-    grad_gate = red_gu[:, :ff_width]
-    grad_up = red_gu[:, ff_width:]
-    grad_down = reduced[gu_chunk:].astype(jnp.float32)
+    )[0]
+    grad_gate = reduced[:gu_rows, :ff_width].astype(jnp.float32)
+    grad_up = reduced[:gu_rows, ff_width:].astype(jnp.float32)
+    grad_down = reduced[gu_rows:, :model_width].astype(jnp.float32)
 
     expert_out = jnp.dot(hidden, down_mat, preferred_element_type=jnp.float32).astype(jnp.bfloat16)
     row_grads = (

time: 266 us -> 261 us (0.981)
  other arithmetic: 45.1 us -> 24.6 us
  Pallas kernels: 0 us -> 20 us
  waiting for transfers between devices: 67.1 us -> 76.2 us
  local copies, waits for them, and re-layouts: 49.4 us -> 40.6 us
  matrix products: 40 us -> 35.9 us
    concatenate x1 -> x0, other arithmetic: 25.8 us -> none  [body(): jnp.concatenate([term_gu.reshape(n_rep, gu_chunk, model_width), term_down...]
    pallas_call x0 -> x1, Pallas kernels: none -> 20 us  [packed_weight_grads(): pl.pallas_call(_pack_kernel, grid=(n_rep,), in_specs=[pl.BlockSpec((gu_ro...]
    reshape x1 -> x0, local copies, waits for them, and re-layouts: 19.6 us -> none  [body(): term_gu.reshape(n_rep, gu_chunk, model_width)]
    dot_general x2 -> x0, matrix products: 14 us -> none  [the longest x1 8.95 us: body(): lax.dot_general(rows_in, deltas, rows_first, preferred_element_type=jnp.f...]
    unnamed x2, waiting for transfers between devices: 29.6 us -> 38.8 us
    dot_general x0 -> x2, local copies, waits for them, and re-layouts: none -> 6.14 us  [the longest x1 3.11 us: body(): gate_pre = jnp.dot(rows_in, gate_mat, preferred_element_type=jnp.float32)]
    dot_general x1, matrix products: 2.59 us -> 7.51 us  [body(): gate_pre = jnp.dot(rows_in, gate_mat, preferred_element_type=jnp.float32)]
    transpose x0 -> x2, local copies, waits for them, and re-layouts: none -> 4.24 us  [body(): packed = packed_weight_grads(rows_in.T, gate_delta, up_delta, hidden.asty...]
  transfers between devices with their start and end apart: 2 -> 2, of which waited for: 2 -> 2; matrix products, arithmetic and copies ran while one was open for 15% -> 16% of each run, Pallas kernels for 0% -> 0%
where the time goes in v2:
time: 261 us; the launch traced here: 260 us
  waiting for transfers between devices  76.2 us (29%)
  blocking collectives  44 us (17%)
  local copies, waits for them, and re-layouts  40.6 us (16%)
  matrix products  35.9 us (14%)
  other arithmetic  24.6 us (9%)
  Pallas kernels  20 us (8%)
  between operations  14.3 us (5%)
  starting transfers between devices  4.67 us (2%)
    all_to_all x1, blocking collectives, body(): lax.all_to_all(disp, 'ep', split_axis=0, concat_axis=0, tiled=True)  44 us
    unnamed x2, waiting for transfers between devices  38.8 us
    all_to_all x1, waiting for transfers between devices, body(): lax.all_to_all(back, 'ep', split_axis=0, concat_axis=0, tiled=True)  37.5 us
    pallas_call x1, Pallas kernels, packed_weight_grads(): pl.pallas_call(_pack_kernel, grid=(n_rep,), in_specs=[pl.BlockSpec((gu_ro...  20 us
    dot_general x1, matrix products, body(): gate_pre = jnp.dot(rows_in, gate_mat, preferred_element_type=jnp.float32)  7.51 us
    dot_general x1, matrix products, body(): up_pre = jnp.dot(rows_in, up_mat, preferred_element_type=jnp.float32)  6.57 us
    dot_general x1, matrix products, body(): lax.dot_general(gate_delta, gate_mat, contract, preferred_element_type=jn...  5.48 us
    dot_general x1, matrix products, body(): lax.dot_general(out_grads, down_mat, contract, preferred_element_type=jnp...  5.41 us
  transfers between devices with their start and end apart: 2, of which 2 were waited for; matrix products, arithmetic and copies ran while one was open for 16% of the time, Pallas kernels for 0%

profile of v2, /device:TPU:1, one launch (start us, length us, event | category | flops | bytes accessed | tf_op | source)
XLA Modules:
  0.0 260.2 jit_solution(15835039556652926077)
XLA Ops:
  7.2 0.0 copy-start
  7.2 0.0 reduce-scatter.4.cloned.1.call-start
  7.2 0.7 broadcast_multiply_fusion.2
  8.0 0.8 copy.25
  8.7 0.1 eq.29
  8.9 0.1 eq.25
  9.0 0.1 copy.24
  9.1 0.1 mul.81
  9.3 0.6 reduce-window.6
  9.9 0.2 slice_reduce_fusion
  10.1 0.1 fusion.33
  10.3 2.2 scatter_custom_fusion.1
  12.4 0.1 mul.83
  12.5 1.4 scatter_custom_fusion
  13.9 0.8 copy.23
  14.7 0.1 reshape.114
  14.8 2.1 broadcast_in_dim.42
  16.9 2.5 convert_element_type.71
  19.4 0.0 copy-done
  19.4 0.0 copy-start.6
  19.4 3.1 %gather_fusion = bf16[384,2048]{1,0:T(8,128)(2,1)} fusion(bf16[128,2048]{1,0:T(8,128)(2,1)S(1)} %copy-done, s32[1024]{0:T(1024)S(1)} %get-tuple-element.18), kind=kCustom, calls=%fused_computation | custom fusion | bytes 3147264 | tf_op jit(solution)/shard_map/gather | solution.py:78
  22.6 0.0 copy-done.6
  22.6 0.2 multiply_convert_fusion.3
  22.7 0.0 copy-start.7
  22.7 3.1 %gather_fusion.1 = bf16[384,2048]{1,0:T(8,128)(2,1)} fusion(bf16[256,2048]{1,0:T(8,128)(2,1)S(1)} %multiply_convert_fusion.3, s32[1024]{0:T(1024)S(1)} %get-tuple-element.17), kind=kCustom, calls=%fused_computation.1 | custom fusion | bytes 3147264 | tf_op jit(solution)/shard_map/gather | solution.py:78
  25.9 0.0 copy-done.7
  25.9 1.7 broadcast_multiply_fusion.1
  27.6 0.3 pad_maximum_fusion
  27.9 44.0 %all_to_all.10 = bf16[8,48,4096]{2,1,0:T(8,128)(2,1)S(1)} all-to-all(bf16[8,48,4096]{2,1,0:T(8,128)(2,1)S(1)} %pad_maximum_fusion), channel_id=1, replica_groups=mesh['rep'=16,'ep'=8] {'ep'}, dimensions={0} | all-to-all | bytes 6291456 | tf_op jit(solution)/shard_map/all_to_all | solution.py:80
  71.9 1.4 slice_bitcast_fusion
  73.3 2.9 %copy.29.xt_ref = bf16[2048,384]{1,0:T(8,128)(2,1)} copy(bf16[2048,384]{0,1:T(8,128)(2,1)} %slice_bitcast_fusion) | data formatting | bytes 3145728 | tf_op jit(solution)/shard_map/transpose | solution.py:101
  76.2 6.6 %fusion.6 = f32[384,1408]{1,0:T(8,128)} fusion(bf16[1,2048,1408]{2,1,0:T(8,128)(2,1)} %param.11, bf16[384,4096]{1,0:T(8,128)(2,1)S(1)} %bitcast.87), kind=kOutput, calls=%fused_computation.11 | convolution fusion | flops 2214592512 | bytes 9502720 | tf_op jit(solution)/shard_map/dot_general | solution.py:89
  82.7 3.0 %copy.28 = f32[384,1408]{0,1:T(8,128)} copy(f32[384,1408]{1,0:T(8,128)} %fusion.6) | data formatting | bytes 4325376 | tf_op jit(solution)/shard_map/dot_general | solution.py:89
  85.8 5.4 %fusion = f32[384,1408]{1,0:T(8,128)S(1)} fusion(bf16[1,1408,2048]{2,1,0:T(8,128)(2,1)} %param.12, bf16[384,4096]{1,0:T(8,128)(2,1)S(1)} %bitcast.88), kind=kOutput, calls=%fused_computation.5 | convolution fusion | flops 2214592512 | bytes 9502720 | tf_op jit(solution)/shard_map/dot_general | solution.py:93
  91.2 0.0 copy-done.2
  91.2 0.0 copy-done.8
  91.2 7.5 %multiply_convert_fusion.1 = (bf16[384,1408]{1,0:T(8,128)(2,1)}, bf16[384,1408]{1,0:T(8,128)(2,1)}, f32[384,1408]{1,0:T(8,128)}) fusion(f32[384,1408]{1,0:T(8,128)S(1)} %fusion, f32[384,1408]{1,0:T(8,128)S(1)} %copy-done.8, bf16[1,2048,1408]{2,1,0:T(8,128)(2,1)} %param.10, bf16[384,4096]{1,0:T(8,128)(2,1)S(1)} %bitcast.89), kind=kOutput, calls=%fused_computation.29 | convolution fusion | flops 2221621248 | bytes 15990784 | tf_op jit(solution)/shard_map/dot_general | solution.py:88
  98.7 3.1 %copy.27 = f32[384,1408]{0,1:T(8,128)} copy(f32[384,1408]{1,0:T(8,128)} %get-tuple-element.16) | data formatting | bytes 4325376 | tf_op jit(solution)/shard_map/dot_general | solution.py:88
  101.8 0.0 copy-done.4
  101.8 3.5 %fusion.25.ht_ref = f32[1408,384]{1,0:T(8,128)} fusion(f32[384,1408]{0,1:T(8,128)S(1)} %copy-done.4, f32[384,1408]{0,1:T(8,128)} %copy.27), kind=kLoop, calls=%fused_computation.39 | loop fusion | flops 3784704 | bytes 6488064 | tf_op jit(solution)/shard_map/convert_element_type | solution.py:101
  105.3 20.0 %shard_map.118 = bf16[16,216,2816]{2,1,0:T(8,128)(2,1)} custom-call(bf16[2048,384]{1,0:T(8,128)(2,1)} %copy.29.xt_ref, bf16[384,1408]{1,0:T(8,128)(2,1)} %get-tuple-element.6.gd_ref, bf16[384,1408]{1,0:T(8,128)(2,1)} %get-tuple-element.7.ud_ref, f32[1408,384]{1,0:T(8,128)} %fusion.25.ht_ref, bf16[384,4096]{1,0:T(8,128)(2,1)} %bitcast.90), custom_call_target="tpu_custom_call" | custom-call | flops 6643777536 | bytes 19464192 | tf_op jit(solution)/shard_map/pallas_call | solution.py:32
  125.3 0.0 reduce-scatter.4.cloned.1.call-update
  125.3 1.2 copy-done.12
  126.5 4.8 %fusion.4 = f32[384,2048]{1,0:T(8,128)S(1)} fusion(bf16[384,1408]{1,0:T(8,128)(2,1)S(1)} %copy-done.12, bf16[1,2048,1408]{2,1,0:T(8,128)(2,1)} %param.11), kind=kOutput, calls=%fused_computation.9 | convolution fusion | flops 2214592512 | bytes 9994240 | tf_op jit(solution)/shard_map/dot_general | solution.py:113
  131.3 0.0 copy-done.11
  131.4 0.0 slice-start.1
  131.4 5.5 %add_convert_fusion = bf16[384,2048]{1,0:T(8,128)(2,1)S(1)} fusion(f32[384,2048]{1,0:T(8,128)S(1)} %fusion.4, bf16[384,1408]{1,0:T(8,128)(2,1)S(1)} %copy-done.11, bf16[1,2048,1408]{2,1,0:T(8,128)(2,1)} %param.10), kind=kOutput, calls=%fused_computation.19 | convolution fusion | flops 2216165376 | bytes 11567104 | tf_op jit(solution)/shard_map/dot_general | solution.py:112
  136.9 2.7 %fusion.14 = bf16[384,2048]{1,0:T(8,128)(2,1)S(1)} fusion(bf16[1,1408,2048]{2,1,0:T(8,128)(2,1)S(1)} %bitcast.103, f32[384,1408]{1,0:T(8,128)S(1)} %copy-done.9, f32[384,1408]{1,0:T(8,128)S(1)} %copy-done.10), kind=kOutput, calls=%fused_computation.20 | convolution fusion | flops 2218622976 | bytes 11665408 | tf_op jit(solution)/shard_map/dot_general | solution.py:110
  139.6 2.0 pad_maximum_fusion.1
  141.7 4.6 %all-to-all-start.1 = ((bf16[8,48,4096]{2,1,0:T(8,128)(2,1)}), bf16[8,48,4096]{2,1,0:T(8,128)(2,1)S(1)}, u32[]{:S(2)}, u32[]{:S(2)}) async-start(bf16[8,48,4096]{2,1,0:T(8,128)(2,1)} %bitcast.91), calls=%async_computation.1 | async-start | bytes 6291456 | tf_op jit(solution)/shard_map/all_to_all | solution.py:118
  146.3 37.5 %all-to-all-done.1 = bf16[8,48,4096]{2,1,0:T(8,128)(2,1)S(1)} async-done(((bf16[8,48,4096]{2,1,0:T(8,128)(2,1)}), bf16[8,48,4096]{2,1,0:T(8,128)(2,1)S(1)}, u32[]{:S(2)}, u32[]{:S(2)}) %all-to-all-start.1) | async-done | bytes 3145760 | tf_op jit(solution)/shard_map/all_to_all | solution.py:118
  183.8 3.2 %gather_fusion.2 = bf16[256,4096]{1,0:T(8,128)(2,1)} fusion(bf16[384,4096]{1,0:T(8,128)(2,1)S(1)} %bitcast.85, s32[1024]{0:T(1024)S(1)} %pad_clamp_fusion), kind=kCustom, calls=%fused_computation.2 | custom fusion | bytes 4195328 | tf_op jit(solution)/shard_map/gather | solution.py:121
  187.0 2.8 %convert_multiply_fusion = f32[256,2048]{1,0:T(8,128)} fusion(f32[256]{0:T(256)S(1)} %reshape.114, bf16[256,4096]{1,0:T(8,128)(2,1)} %gather_fusion.2), kind=kLoop, calls=%fused_computation.33 | loop fusion | flops 1048576 | bytes 3146752 | tf_op jit(solution)/shard_map/mul | solution.py:125
  189.8 3.6 %reshape.110 = f32[128,2,2048]{2,1,0:T(2,128)} reshape(f32[256,2048]{1,0:T(8,128)} %convert_multiply_fusion) | data formatting | bytes 4194304 | tf_op jit(solution)/shard_map/reshape | solution.py:125
  193.5 1.2 fusion.42
  194.7 0.7 reshape.113
  195.4 3.4 %fusion.26 = bf16[128,1,2]{2,1,0:T(2,128)(2,1)S(1)} fusion(bf16[128,2,2048]{2,1,0:T(2,128)(2,1)S(1)} %reshape.113, bf16[128,2048,1]{1,0,2:T(8,128)(2,1)} %bitcast.96), kind=kOutput, calls=%fused_computation.40 | convolution fusion | flops 1048576 | bytes 1573376 | tf_op jit(solution)/shard_map/tkd,td->tk/dot_general | solution.py:127
  198.8 0.6 copy.31
  199.4 2.7 %reshape.111 = bf16[128,2,2048]{2,1,0:T(2,128)(2,1)} reshape(bf16[256,2048]{1,0:T(8,128)(2,1)} %get-tuple-element.9) | data formatting | bytes 2097152 | tf_op jit(solution)/shard_map/reshape | solution.py:134
  202.0 4.6 %reduce = bf16[128,2048]{1,0:T(8,128)(2,1)} reduce(bf16[128,2,2048]{2,1,0:T(2,128)(2,1)} %reshape.111, bf16[]{:T(256)} %constant.32.clone.1), dimensions={1}, to_apply=%region_6.7.clone | reduce | flops 262144 | bytes 1572866 | tf_op jit(solution)/shard_map/reduce_sum | solution.py:133
  206.6 3.8 %reduce_sum.31 = bf16[128,2048]{1,0:T(8,128)(2,1)} reduce(f32[128,2,2048]{2,1,0:T(2,128)S(1)} %copy-done.5, f32[]{:T(128)} %constant.36.clone.1), dimensions={1}, to_apply=%region_5.6 | reduce | flops 262144 | bytes 2621444 | tf_op jit(solution)/shard_map/reduce_sum | solution.py:124
  210.4 38.8 %reduce-scatter.4.cloned.1.call-done = bf16[1,216,2816]{2,1,0:T(8,128)(2,1)} async-done(((bf16[16,216,2816]{2,1,0:T(8,128)(2,1)}), bf16[1,216,2816]{2,1,0:T(8,128)(2,1)}) %reduce-scatter.4.cloned.1.call-update) | async-done | bytes 1216528
  249.2 1.9 fusion.29
  251.1 2.3 fusion.30
  (28 shorter events, 0.1 us)
Async XLA Ops:
  7.2 12.3 %copy-start = (bf16[128,2048]{1,0:T(8,128)(2,1)S(1)}, bf16[128,2048]{1,0:T(8,128)(2,1)}, u32[]{:S(2)}) copy-start(bf16[128,2048]{1,0:T(8,128)(2,1)} %param.7) | copy-start | bytes 1572868
  7.2 242.0 %reduce-scatter.4.cloned.1.call-start = ((), (), s32[]{:S(2)}) async-start(), calls=%async_computation.3 | async-start | bytes 20680704
  19.4 3.1 %copy-start.6 = (f32[256,2048]{1,0:T(8,128)S(1)}, f32[256,2048]{1,0:T(8,128)}, u32[]{:S(2)}) copy-start(f32[256,2048]{1,0:T(8,128)} %convert_element_type.71) | copy-start | bytes 6291460
  22.7 3.1 %copy-start.7 = (bf16[384,2048]{1,0:T(8,128)(2,1)S(1)}, bf16[384,2048]{1,0:T(8,128)(2,1)}, u32[]{:S(2)}) copy-start(bf16[384,2048]{1,0:T(8,128)(2,1)} %gather_fusion) | copy-start | bytes 4718596
  71.9 19.3 %copy-start.2 = (bf16[8,48,4096]{2,1,0:T(8,128)(2,1)}, bf16[8,48,4096]{2,1,0:T(8,128)(2,1)S(1)}, u32[]{:S(2)}) copy-start(bf16[8,48,4096]{2,1,0:T(8,128)(2,1)S(1)} %all_to_all.10) | copy-start | bytes 9437188
  85.8 5.4 %copy-start.8 = (f32[384,1408]{1,0:T(8,128)S(1)}, f32[384,1408]{1,0:T(8,128)}, u32[]{:S(2)}) copy-start(f32[384,1408]{1,0:T(8,128)} %fusion.6) | copy-start | bytes 6488068
  98.7 3.1 %copy-start.4 = (f32[384,1408]{0,1:T(8,128)S(1)}, f32[384,1408]{0,1:T(8,128)}, u32[]{:S(2)}) copy-start(f32[384,1408]{0,1:T(8,128)} %copy.28) | copy-start | bytes 6488068
  125.3 1.2 copy-start.12
  126.5 4.8 %copy-start.11 = (bf16[384,1408]{1,0:T(8,128)(2,1)S(1)}, bf16[384,1408]{1,0:T(8,128)(2,1)}, u32[]{:S(2)}) copy-start(bf16[384,1408]{1,0:T(8,128)(2,1)} %get-tuple-element.6.gd_ref) | copy-start | bytes 3244036
  126.5 10.4 %slice-start = ((s8[5767168]{0:T(1024)(128)(4,1)}), s8[4194304]{0:T(1024)(128)(4,1)S(1)}, s32[]{:S(2)}) async-start(s8[5767168]{0:T(1024)(128)(4,1)} %bitcast.102), calls=%async_computation.4 | async-start | bytes 8388608
  131.3 5.5 %copy-start.9 = (f32[384,1408]{1,0:T(8,128)S(1)}, f32[384,1408]{1,0:T(8,128)}, u32[]{:S(2)}) copy-start(f32[384,1408]{1,0:T(8,128)} %fusion.6) | copy-start | bytes 6488068
  131.4 5.5 %copy-start.10 = (f32[384,1408]{1,0:T(8,128)S(1)}, f32[384,1408]{1,0:T(8,128)}, u32[]{:S(2)}) copy-start(f32[384,1408]{1,0:T(8,128)} %get-tuple-element.16) | copy-start | bytes 6488068
  131.4 5.5 %slice-start.1 = ((s8[5767168]{0:T(1024)(128)(4,1)}), s8[1572864]{0:T(1024)(128)(4,1)S(1)}, s32[]{:S(2)}) async-start(s8[5767168]{0:T(1024)(128)(4,1)} %bitcast.102), calls=%async_computation.5 | async-start | bytes 3145728
  141.7 42.1 %all-to-all-start.1 = ((bf16[8,48,4096]{2,1,0:T(8,128)(2,1)}), bf16[8,48,4096]{2,1,0:T(8,128)(2,1)S(1)}, u32[]{:S(2)}, u32[]{:S(2)}) async-start(bf16[8,48,4096]{2,1,0:T(8,128)(2,1)} %bitcast.91), calls=%async_computation.1 | async-start | bytes 6291456 | tf_op jit(solution)/shard_map/all_to_all | solution.py:118
  189.8 3.6 %copy-start.3 = (bf16[256,4096]{1,0:T(8,128)(2,1)S(1)}, bf16[256,4096]{1,0:T(8,128)(2,1)}, u32[]{:S(2)}) copy-start(bf16[256,4096]{1,0:T(8,128)(2,1)} %gather_fusion.2) | copy-start | bytes 6291460
  198.8 7.9 %copy-start.5 = (f32[128,2,2048]{2,1,0:T(2,128)S(1)}, f32[128,2,2048]{2,1,0:T(2,128)}, u32[]{:S(2)}) copy-start(f32[128,2,2048]{2,1,0:T(2,128)} %reshape.110) | copy-start | bytes 6291460
  206.6 46.7 %copy-start.1 = (bf16[128,2048]{1,0:T(8,128)(2,1)S(1)}, bf16[128,2048]{1,0:T(8,128)(2,1)}, u32[]{:S(2)}) copy-start(bf16[128,2048]{1,0:T(8,128)(2,1)} %param.7) | copy-start | bytes 1572868
Sparse Core Ops, SparseCore 0:
  125.4 123.6 reduce-scatter.3

commit v3 on v2

--- a/solution.py
+++ b/solution.py
@@ -2,30 +2,39 @@
 import jax.numpy as jnp
 from jax import lax
 from jax.experimental import pallas as pl
+from jax.experimental.pallas import tpu as pltpu
 from jax.sharding import PartitionSpec as P
 
 
-def _pack_kernel(xt_ref, gd_ref, ud_ref, ht_ref, og_ref, o_ref):
+def _pack_kernel(x_ref, gd_ref, ud_ref, h_ref, og_ref, o_ref, down_ref):
     ff = gd_ref.shape[1]
     width = og_ref.shape[1]
-    rows = xt_ref.shape[0]
-    xt = xt_ref[...]
-    o_ref[0, :rows, :ff] = jnp.dot(xt, gd_ref[...], preferred_element_type=jnp.float32).astype(
-        o_ref.dtype
-    )
-    o_ref[0, :rows, ff:] = jnp.dot(xt, ud_ref[...], preferred_element_type=jnp.float32).astype(
-        o_ref.dtype
-    )
-    down = jnp.dot(
-        ht_ref[...].astype(jnp.bfloat16), og_ref[...], preferred_element_type=jnp.float32
-    )
-    o_ref[0, rows:, :width] = down.astype(o_ref.dtype)
-    o_ref[0, rows:, width:] = jnp.zeros((down.shape[0], 2 * ff - width), o_ref.dtype)
+    rows = x_ref.shape[1]
+    down_rows = o_ref.shape[1] - rows
+    first = (((0,), (0,)), ((), ()))
+    r = pl.program_id(0)
+
+    @pl.when(r == 0)
+    def _():
+        down_ref[...] = lax.dot_general(
+            h_ref[...], og_ref[...], first, preferred_element_type=jnp.float32
+        )
+
+    x = x_ref[...]
+    o_ref[0, :rows, :ff] = lax.dot_general(
+        x, gd_ref[...], first, preferred_element_type=jnp.float32
+    ).astype(o_ref.dtype)
+    o_ref[0, :rows, ff:] = lax.dot_general(
+        x, ud_ref[...], first, preferred_element_type=jnp.float32
+    ).astype(o_ref.dtype)
+    start = pl.multiple_of(r * down_rows, 8)
+    o_ref[0, rows:, :width] = down_ref[pl.ds(start, down_rows), :].astype(o_ref.dtype)
+    o_ref[0, rows:, width:] = jnp.zeros((down_rows, 2 * ff - width), o_ref.dtype)
 
 
-def packed_weight_grads(rows_t, gate_delta, up_delta, hidden_t, recv, n_rep):
-    model_width, slots = rows_t.shape
-    ff = gate_delta.shape[1]
+def packed_weight_grads(recv, gate_delta, up_delta, hidden, n_rep):
+    slots, ff = gate_delta.shape
+    model_width = recv.shape[1] // 2
     gu_rows = model_width // n_rep
     down_rows = ff // n_rep
     flops = 2 * slots * (model_width * 2 * ff + ff * model_width)
@@ -33,18 +42,20 @@
         _pack_kernel,
         grid=(n_rep,),
         in_specs=[
-            pl.BlockSpec((gu_rows, slots), lambda r: (r, 0)),
+            pl.BlockSpec((slots, gu_rows), lambda r: (0, r)),
             pl.BlockSpec((slots, ff), lambda r: (0, 0)),
             pl.BlockSpec((slots, ff), lambda r: (0, 0)),
-            pl.BlockSpec((down_rows, slots), lambda r: (r, 0)),
+            pl.BlockSpec((slots, ff), lambda r: (0, 0)),
             pl.BlockSpec((slots, model_width), lambda r: (0, 1)),
         ],
         out_specs=pl.BlockSpec((1, gu_rows + down_rows, 2 * ff), lambda r: (r, 0, 0)),
         out_shape=jax.ShapeDtypeStruct((n_rep, gu_rows + down_rows, 2 * ff), jnp.bfloat16),
+        scratch_shapes=[pltpu.VMEM((ff, model_width), jnp.float32)],
+        compiler_params=pltpu.CompilerParams(dimension_semantics=("arbitrary",)),
         cost_estimate=pl.CostEstimate(
             flops=flops, transcendentals=0, bytes_accessed=2 * n_rep * (gu_rows + down_rows) * 2 * ff
         ),
-    )(rows_t, gate_delta, up_delta, hidden_t, recv)
+    )(recv, gate_delta, up_delta, hidden, recv)
 
 
 def body(tokens, experts, gates, w_gate, w_up, w_down, cotangent):
@@ -70,12 +81,11 @@
     filled = jnp.zeros((slots,), jnp.bfloat16).at[slot_index].set(1.0)
     token_src = source // top_count
     weights = gates.reshape(pair_count, 1).astype(jnp.float32)
-    scaled = (weights * jnp.repeat(cotangent, top_count, axis=0).astype(jnp.float32)).astype(
-        jnp.bfloat16
-    )
+    slot_weight = weights[source] * filled[:, None].astype(jnp.float32)
+    scaled_rows = (slot_weight * cotangent[token_src].astype(jnp.float32)).astype(jnp.bfloat16)
 
     disp = jnp.concatenate(
-        [tokens[token_src] * filled[:, None], scaled[source] * filled[:, None]], axis=1
+        [tokens[token_src] * filled[:, None], scaled_rows], axis=1
     ).reshape(n_experts, capacity, 2 * model_width)
     recv = lax.all_to_all(disp, "ep", split_axis=0, concat_axis=0, tiled=True).reshape(
         slots, 2 * model_width
@@ -97,9 +107,7 @@
     up_delta = (hidden_grad * activated).astype(jnp.bfloat16)
 
     gu_rows = model_width // n_rep
-    packed = packed_weight_grads(
-        rows_in.T, gate_delta, up_delta, hidden.astype(jnp.float32).T, recv, n_rep
-    )
+    packed = packed_weight_grads(recv, gate_delta, up_delta, hidden, n_rep)
     reduced = lax.optimization_barrier(
         lax.psum_scatter(packed, "rep", scatter_dimension=0, tiled=True)
     )[0]

time: 261 us -> 236 us (0.904)
  matrix products: 35.9 us -> 26.7 us
  local copies, waits for them, and re-layouts: 40.6 us -> 32.3 us
  other arithmetic: 24.6 us -> 17.5 us
    dot_general x2 -> x0, local copies, waits for them, and re-layouts: 6.14 us -> none  [the longest x1 3.11 us: body(): gate_pre = jnp.dot(rows_in, gate_mat, preferred_element_type=jnp.float32)]
    dot_general x1, matrix products: 7.51 us -> 2.6 us  [body(): gate_pre = jnp.dot(rows_in, gate_mat, preferred_element_type=jnp.float32)]
    transpose x2 -> x0, local copies, waits for them, and re-layouts: 4.24 us -> none  [body(): packed = packed_weight_grads(rows_in.T, gate_delta, up_delta, hidden.asty...]
    convert_element_type x2 -> x1, other arithmetic: 3.66 us -> 0.32 us  [body(): (slot_weight * cotangent[token_src].astype(jnp.float32)).astype(jnp.bfloa...]
    gather x1, local copies, waits for them, and re-layouts: 3.24 us -> 6.23 us  [body(): pair_back = returned[slot_index]]
    dot_general x1, matrix products: 5.48 us -> 2.63 us  [body(): lax.dot_general(gate_delta, gate_mat, contract, preferred_element_type=jn...]
    dot_general x1, matrix products: 2.69 us -> 5.48 us  [body(): jnp.dot(hidden, down_mat, preferred_element_type=jnp.float32)]
    dot_general x1, matrix products: 5.41 us -> 2.64 us  [body(): lax.dot_general(out_grads, down_mat, contract, preferred_element_type=jnp...]
  transfers between devices with their start and end apart: 2 -> 2, of which waited for: 2 -> 2; matrix products, arithmetic and copies ran while one was open for 16% -> 18% of each run, Pallas kernels for 0% -> 0%
where the time goes in v3:
time: 236 us; the launch traced here: 235 us
  waiting for transfers between devices  73.8 us (31%)
  blocking collectives  44.3 us (19%)
  local copies, waits for them, and re-layouts  32.3 us (14%)
  matrix products  26.7 us (11%)
  Pallas kernels  20.5 us (9%)
  other arithmetic  17.5 us (7%)
  between operations  14.4 us (6%)
  starting transfers between devices  5.53 us (2%)
    all_to_all x1, blocking collectives, body(): lax.all_to_all(disp, 'ep', split_axis=0, concat_axis=0, tiled=True)  44.3 us
    all_to_all x1, waiting for transfers between devices, body(): lax.all_to_all(back, 'ep', split_axis=0, concat_axis=0, tiled=True)  37.6 us
    unnamed x2, waiting for transfers between devices  36.2 us
    pallas_call x1, Pallas kernels, packed_weight_grads(): pl.pallas_call(_pack_kernel, grid=(n_rep,), in_specs=[pl.BlockSpec((slots...  20.5 us
    gather x1, local copies, waits for them, and re-layouts, body(): pair_back = returned[slot_index]  6.23 us
    all_to_all x1, starting transfers between devices, body(): lax.all_to_all(back, 'ep', split_axis=0, concat_axis=0, tiled=True)  5.49 us
    dot_general x1, matrix products, body(): jnp.dot(hidden, down_mat, preferred_element_type=jnp.float32)  5.48 us
    dot_general x1, matrix products, body(): lax.dot_general(up_delta, up_mat, contract, preferred_element_type=jnp.fl...  5.04 us
  transfers between devices with their start and end apart: 2, of which 2 were waited for; matrix products, arithmetic and copies ran while one was open for 18% of the time, Pallas kernels for 0%

profile of v3, /device:TPU:1, one launch (start us, length us, event | category | flops | bytes accessed | tf_op | source)
XLA Modules:
  0.0 234.8 jit_solution(13077297194677215373)
XLA Ops:
  7.2 0.0 copy-start
  7.2 0.0 reduce-scatter.4.cloned.1.call-start
  7.2 0.8 copy.19
  8.1 0.1 eq.29
  8.2 0.1 eq.25
  8.3 0.7 broadcast_multiply_fusion.1
  9.0 0.6 reduce-window.6
  9.6 0.2 slice_reduce_fusion
  9.9 0.1 copy.18
  10.0 0.1 mul.77
  10.1 0.1 fusion.28
  10.2 1.4 scatter_custom_fusion
  11.7 0.8 copy.17
  12.4 0.1 reshape.127
  12.6 2.2 scatter_custom_fusion.1
  14.7 0.1 mul.79
  14.8 2.8 %gather_fusion.1 = f32[384]{0:T(512)S(1)} fusion(f32[256]{0:T(256)S(1)} %reshape.127, s32[1024]{0:T(1024)S(1)} %get-tuple-element.15), kind=kCustom, calls=%fused_computation.1 | custom fusion | bytes 4608 | tf_op jit(solution)/shard_map/gather | solution.py:84
  17.7 0.1 mul.83
  17.8 0.0 copy-start.1
  17.8 2.5 %gather_fusion.2 = bf16[384,2048]{1,0:T(8,128)(2,1)S(1)} fusion(bf16[128,2048]{1,0:T(8,128)(2,1)S(1)} %copy-done, s32[1024]{0:T(1024)S(1)} %get-tuple-element.16), kind=kCustom, calls=%fused_computation.2 | custom fusion | bytes 3147264 | tf_op jit(solution)/shard_map/gather | solution.py:85
  20.2 0.0 copy-done.1
  20.2 3.2 %gather_fusion = bf16[384,2048]{1,0:T(8,128)(2,1)} fusion(bf16[128,2048]{1,0:T(8,128)(2,1)S(1)} %copy-done.1, s32[1024]{0:T(1024)S(1)} %get-tuple-element.16), kind=kCustom, calls=%fused_computation | custom fusion | bytes 3147264 | tf_op jit(solution)/shard_map/gather | solution.py:88
  23.4 0.3 fusion.12
  23.7 1.1 copy-done.4
  24.8 0.2 broadcast_multiply_fusion
  25.0 0.0 slice-start.3
  25.0 0.2 pad_maximum_fusion
  25.2 0.0 slice-start.4
  25.2 44.3 %all_to_all.10 = bf16[8,48,4096]{2,1,0:T(8,128)(2,1)S(1)} all-to-all(bf16[8,48,4096]{2,1,0:T(8,128)(2,1)S(1)} %pad_maximum_fusion), channel_id=1, replica_groups=mesh['rep'=16,'ep'=8] {'ep'}, dimensions={0} | all-to-all | bytes 6291456 | tf_op jit(solution)/shard_map/all_to_all | solution.py:90
  69.5 0.0 slice-done.3
  69.5 0.0 slice-start.5
  69.5 0.0 slice-start
  69.5 2.6 %fusion = f32[384,1408]{1,0:T(8,128)S(1)} fusion(bf16[1,1408,2048]{2,1,0:T(8,128)(2,1)S(1)} %bitcast.81, bf16[384,4096]{1,0:T(8,128)(2,1)S(1)} %bitcast.63), kind=kOutput, calls=%fused_computation.6 | convolution fusion | flops 2214592512 | bytes 9502720 | tf_op jit(solution)/shard_map/dot_general | solution.py:103
  72.2 0.0 slice-start.1
  72.2 2.6 %fusion.10 = f32[384,1408]{1,0:T(8,128)S(1)} fusion(bf16[1,2048,1408]{2,1,0:T(8,128)(2,1)S(1)} %bitcast.83, bf16[384,4096]{1,0:T(8,128)(2,1)S(1)} %bitcast.64), kind=kOutput, calls=%fused_computation.16 | convolution fusion | flops 2214592512 | bytes 9502720 | tf_op jit(solution)/shard_map/dot_general | solution.py:98
  74.8 0.0 copy-done.2
  74.8 0.0 slice-done
  74.8 0.0 slice-done.1
  74.9 4.6 %multiply_convert_fusion.2 = (bf16[384,1408]{1,0:T(8,128)(2,1)}, bf16[384,1408]{1,0:T(8,128)(2,1)}, bf16[384,1408]{1,0:T(8,128)(2,1)}) fusion(f32[384,1408]{1,0:T(8,128)S(1)} %fusion.10, f32[384,1408]{1,0:T(8,128)S(1)} %fusion, bf16[1,2048,1408]{2,1,0:T(8,128)(2,1)S(1)} %bitcast.79, bf16[384,4096]{1,0:T(8,128)(2,1)S(1)} %bitcast.65), kind=kOutput, calls=%fused_computation.26 | convolution fusion | flops 2222702592 | bytes 14909440 | tf_op jit(solution)/shard_map/dot_general | solution.py:99
  79.4 20.5 %shard_map.118 = bf16[16,216,2816]{2,1,0:T(8,128)(2,1)} custom-call(bf16[384,4096]{1,0:T(8,128)(2,1)} %bitcast.66, bf16[384,1408]{1,0:T(8,128)(2,1)} %get-tuple-element.7.gd_ref, bf16[384,1408]{1,0:T(8,128)(2,1)} %get-tuple-element.8.ud_ref, bf16[384,1408]{1,0:T(8,128)(2,1)} %get-tuple-element.6.h_ref, bf16[384,4096]{1,0:T(8,128)(2,1)} %bitcast.67), custom_call_target="tpu_custom_call" | custom-call | flops 6643777536 | bytes 19464192 | tf_op jit(solution)/shard_map/pallas_call | solution.py:41
  99.9 0.0 reduce-scatter.4.cloned.1.call-update
  99.9 1.2 copy-done.8
  101.2 5.0 %fusion.4 = f32[384,2048]{1,0:T(8,128)S(1)} fusion(bf16[384,1408]{1,0:T(8,128)(2,1)S(1)} %copy-done.8, bf16[1,2048,1408]{2,1,0:T(8,128)(2,1)} %param.11), kind=kOutput, calls=%fused_computation.10 | convolution fusion | flops 2214592512 | bytes 9994240 | tf_op jit(solution)/shard_map/dot_general | solution.py:121
  106.2 0.0 copy-done.7
  106.2 0.0 copy-start.6
  106.2 0.0 slice-start.7
  106.2 5.5 %fusion.15 = bf16[384,2048]{1,0:T(8,128)(2,1)S(1)} fusion(bf16[384,1408]{1,0:T(8,128)(2,1)S(1)} %copy-done.7, bf16[1,1408,2048]{2,1,0:T(8,128)(2,1)} %param.12), kind=kOutput, calls=%fused_computation.23 | convolution fusion | flops 2215378944 | bytes 8421376 | tf_op jit(solution)/shard_map/dot_general | solution.py:118
  111.8 2.6 %add_convert_fusion = bf16[384,2048]{1,0:T(8,128)(2,1)S(1)} fusion(f32[384,2048]{1,0:T(8,128)S(1)} %fusion.4, bf16[384,1408]{1,0:T(8,128)(2,1)S(1)} %copy-done.6, bf16[1,2048,1408]{2,1,0:T(8,128)(2,1)S(1)} %bitcast.85), kind=kOutput, calls=%fused_computation.22 | convolution fusion | flops 2216165376 | bytes 11567104 | tf_op jit(solution)/shard_map/dot_general | solution.py:120
  114.4 2.1 pad_maximum_fusion.1
  116.5 5.5 %all-to-all-start.1 = ((bf16[8,48,4096]{2,1,0:T(8,128)(2,1)}), bf16[8,48,4096]{2,1,0:T(8,128)(2,1)}, u32[]{:S(2)}, u32[]{:S(2)}) async-start(bf16[8,48,4096]{2,1,0:T(8,128)(2,1)} %bitcast.68), calls=%async_computation.1 | async-start | bytes 6291456 | tf_op jit(solution)/shard_map/all_to_all | solution.py:126
  122.0 37.6 %all-to-all-done.1 = bf16[8,48,4096]{2,1,0:T(8,128)(2,1)} async-done(((bf16[8,48,4096]{2,1,0:T(8,128)(2,1)}), bf16[8,48,4096]{2,1,0:T(8,128)(2,1)}, u32[]{:S(2)}, u32[]{:S(2)}) %all-to-all-start.1) | async-done | bytes 3145760 | tf_op jit(solution)/shard_map/all_to_all | solution.py:126
  159.5 6.2 %gather_fusion.3 = bf16[256,4096]{1,0:T(8,128)(2,1)S(1)} fusion(bf16[384,4096]{1,0:T(8,128)(2,1)} %bitcast.11, s32[1024]{0:T(1024)S(1)} %pad_clamp_fusion), kind=kCustom, calls=%fused_computation.3 | custom fusion | bytes 4195328 | tf_op jit(solution)/shard_map/gather | solution.py:129
  165.8 1.5 convert_multiply_fusion.1
  167.3 3.6 %reshape.123 = f32[128,2,2048]{2,1,0:T(2,128)} reshape(f32[256,2048]{1,0:T(8,128)} %convert_multiply_fusion.1) | data formatting | bytes 4194304 | tf_op jit(solution)/shard_map/reshape | solution.py:133
  170.9 1.5 fusion.36
  172.4 1.8 reshape.124
  174.2 3.7 %reduce = bf16[128,2048]{1,0:T(8,128)(2,1)} reduce(bf16[128,2,2048]{2,1,0:T(2,128)(2,1)S(1)} %reshape.124, bf16[]{:T(256)} %constant.32.clone.1), dimensions={1}, to_apply=%region_6.7.clone | reduce | flops 262144 | bytes 1572866 | tf_op jit(solution)/shard_map/reduce_sum | solution.py:141
  177.9 1.5 reshape.126
  179.4 3.7 %fusion.22 = bf16[128,1,2]{2,1,0:T(2,128)(2,1)S(1)} fusion(bf16[128,2,2048]{2,1,0:T(2,128)(2,1)} %reshape.126, bf16[128,2048,1]{1,0,2:T(8,128)(2,1)S(1)} %bitcast.62), kind=kOutput, calls=%fused_computation.33 | convolution fusion | flops 1048576 | bytes 1573376 | tf_op jit(solution)/shard_map/tkd,td->tk/dot_general | solution.py:135
  183.2 0.6 copy.22
  183.8 3.9 %reduce_sum.31 = bf16[128,2048]{1,0:T(8,128)(2,1)} reduce(f32[128,2,2048]{2,1,0:T(2,128)S(1)} %copy-done.3, f32[]{:T(128)} %constant.36.clone.1), dimensions={1}, to_apply=%region_5.6 | reduce | flops 262144 | bytes 2621444 | tf_op jit(solution)/shard_map/reduce_sum | solution.py:132
  187.6 36.2 %reduce-scatter.4.cloned.1.call-done = bf16[1,216,2816]{2,1,0:T(8,128)(2,1)} async-done(((bf16[16,216,2816]{2,1,0:T(8,128)(2,1)}), bf16[1,216,2816]{2,1,0:T(8,128)(2,1)}) %reduce-scatter.4.cloned.1.call-update) | async-done | bytes 1216528
  223.8 2.3 fusion.25
  226.1 1.9 fusion.24
  (31 shorter events, 0.1 us)
Async XLA Ops:
  7.2 10.6 %copy-start = (bf16[128,2048]{1,0:T(8,128)(2,1)S(1)}, bf16[128,2048]{1,0:T(8,128)(2,1)}, u32[]{:S(2)}) copy-start(bf16[128,2048]{1,0:T(8,128)(2,1)} %param.13) | copy-start | bytes 1572868
  7.2 216.6 %reduce-scatter.4.cloned.1.call-start = ((), (), s32[]{:S(2)}) async-start(), calls=%async_computation.3 | async-start | bytes 20680704
  17.8 2.5 %copy-start.1 = (bf16[128,2048]{1,0:T(8,128)(2,1)S(1)}, bf16[128,2048]{1,0:T(8,128)(2,1)}, u32[]{:S(2)}) copy-start(bf16[128,2048]{1,0:T(8,128)(2,1)} %param.7) | copy-start | bytes 1572868
  23.4 1.4 copy-start.4
  24.8 44.7 %slice-start.2 = ((s8[5767168]{0:T(1024)(128)(4,1)}), s8[4194304]{0:T(1024)(128)(4,1)S(1)}, s32[]{:S(2)}) async-start(s8[5767168]{0:T(1024)(128)(4,1)} %bitcast.80), calls=%async_computation.6 | async-start | bytes 8388608
  25.0 44.5 %slice-start.3 = ((s8[5767168]{0:T(1024)(128)(4,1)}), s8[1572864]{0:T(1024)(128)(4,1)S(1)}, s32[]{:S(2)}) async-start(s8[5767168]{0:T(1024)(128)(4,1)} %bitcast.80), calls=%async_computation.7 | async-start | bytes 3145728
  25.2 47.0 %slice-start.4 = ((s8[5767168]{0:T(1024)(128)(4,1)}), s8[4194304]{0:T(1024)(128)(4,1)S(1)}, s32[]{:S(2)}) async-start(s8[5767168]{0:T(1024)(128)(4,1)} %bitcast.82), calls=%async_computation.8 | async-start | bytes 8388608
  69.5 5.3 %copy-start.2 = (bf16[8,48,4096]{2,1,0:T(8,128)(2,1)}, bf16[8,48,4096]{2,1,0:T(8,128)(2,1)S(1)}, u32[]{:S(2)}) copy-start(bf16[8,48,4096]{2,1,0:T(8,128)(2,1)S(1)} %all_to_all.10) | copy-start | bytes 9437188
  69.5 2.7 %slice-start.5 = ((s8[5767168]{0:T(1024)(128)(4,1)}), s8[1572864]{0:T(1024)(128)(4,1)S(1)}, s32[]{:S(2)}) async-start(s8[5767168]{0:T(1024)(128)(4,1)} %bitcast.82), calls=%async_computation.9 | async-start | bytes 3145728
  69.5 5.3 %slice-start = ((s8[5767168]{0:T(1024)(128)(4,1)}), s8[4194304]{0:T(1024)(128)(4,1)S(1)}, s32[]{:S(2)}) async-start(s8[5767168]{0:T(1024)(128)(4,1)} %bitcast.78), calls=%async_computation.4 | async-start | bytes 8388608
  72.2 2.6 %slice-start.1 = ((s8[5767168]{0:T(1024)(128)(4,1)}), s8[1572864]{0:T(1024)(128)(4,1)S(1)}, s32[]{:S(2)}) async-start(s8[5767168]{0:T(1024)(128)(4,1)} %bitcast.78), calls=%async_computation.5 | async-start | bytes 3145728
  99.9 1.2 copy-start.8
  101.2 5.1 %copy-start.7 = (bf16[384,1408]{1,0:T(8,128)(2,1)S(1)}, bf16[384,1408]{1,0:T(8,128)(2,1)}, u32[]{:S(2)}) copy-start(bf16[384,1408]{1,0:T(8,128)(2,1)} %get-tuple-element.6.h_ref) | copy-start | bytes 3244036
  101.2 10.6 %slice-start.6 = ((s8[5767168]{0:T(1024)(128)(4,1)}), s8[4194304]{0:T(1024)(128)(4,1)S(1)}, s32[]{:S(2)}) async-start(s8[5767168]{0:T(1024)(128)(4,1)} %bitcast.84), calls=%async_computation.10 | async-start | bytes 8388608
  106.2 5.5 %copy-start.6 = (bf16[384,1408]{1,0:T(8,128)(2,1)S(1)}, bf16[384,1408]{1,0:T(8,128)(2,1)}, u32[]{:S(2)}) copy-start(bf16[384,1408]{1,0:T(8,128)(2,1)} %get-tuple-element.7.gd_ref) | copy-start | bytes 3244036
  106.2 5.5 %slice-start.7 = ((s8[5767168]{0:T(1024)(128)(4,1)}), s8[1572864]{0:T(1024)(128)(4,1)S(1)}, s32[]{:S(2)}) async-start(s8[5767168]{0:T(1024)(128)(4,1)} %bitcast.84), calls=%async_computation.11 | async-start | bytes 3145728
  116.5 43.1 %all-to-all-start.1 = ((bf16[8,48,4096]{2,1,0:T(8,128)(2,1)}), bf16[8,48,4096]{2,1,0:T(8,128)(2,1)}, u32[]{:S(2)}, u32[]{:S(2)}) async-start(bf16[8,48,4096]{2,1,0:T(8,128)(2,1)} %bitcast.68), calls=%async_computation.1 | async-start | bytes 6291456 | tf_op jit(solution)/shard_map/all_to_all | solution.py:126
  172.4 5.6 %copy-start.5 = (bf16[256,2048]{1,0:T(8,128)(2,1)S(1)}, bf16[256,2048]{1,0:T(8,128)(2,1)}, u32[]{:S(2)}) copy-start(bf16[256,2048]{1,0:T(8,128)(2,1)} %get-tuple-element.9) | copy-start | bytes 3145732
  179.4 4.3 %copy-start.3 = (f32[128,2,2048]{2,1,0:T(2,128)S(1)}, f32[128,2,2048]{2,1,0:T(2,128)}, u32[]{:S(2)}) copy-start(f32[128,2,2048]{2,1,0:T(2,128)} %reshape.123) | copy-start | bytes 6291460
Sparse Core Ops, SparseCore 0:
  100.1 123.6 reduce-scatter.3

commit v4 on v3

--- a/solution.py
+++ b/solution.py
@@ -6,11 +6,16 @@
 from jax.sharding import PartitionSpec as P
 
 
+TILE_ROWS = 16
+LANES = 128
+
+
 def _pack_kernel(x_ref, gd_ref, ud_ref, h_ref, og_ref, o_ref, down_ref):
     ff = gd_ref.shape[1]
     width = og_ref.shape[1]
     rows = x_ref.shape[1]
-    down_rows = o_ref.shape[1] - rows
+    down_rows = down_ref.shape[0] // pl.num_programs(0)
+    over = 2 * ff - width
     first = (((0,), (0,)), ((), ()))
     r = pl.program_id(0)
 
@@ -21,15 +26,21 @@
         )
 
     x = x_ref[...]
-    o_ref[0, :rows, :ff] = lax.dot_general(
-        x, gd_ref[...], first, preferred_element_type=jnp.float32
-    ).astype(o_ref.dtype)
-    o_ref[0, :rows, ff:] = lax.dot_general(
-        x, ud_ref[...], first, preferred_element_type=jnp.float32
-    ).astype(o_ref.dtype)
+    g = lax.dot_general(x, gd_ref[...], first, preferred_element_type=jnp.float32)
+    u = lax.dot_general(x, ud_ref[...], first, preferred_element_type=jnp.float32)
+    o_ref[0, :rows, :ff] = g.astype(o_ref.dtype)
+    o_ref[0, :rows, ff:] = u[:, : width - ff].astype(o_ref.dtype)
+    col_tiles = over // LANES
+    for i in range(rows // TILE_ROWS):
+        for j in range(col_tiles):
+            q, p = divmod(i * col_tiles + j, width // LANES)
+            src = u[i * TILE_ROWS : (i + 1) * TILE_ROWS, width - ff + j * LANES :][:, :LANES]
+            o_ref[0, rows + q * TILE_ROWS : rows + (q + 1) * TILE_ROWS, p * LANES : (p + 1) * LANES] = (
+                src.astype(o_ref.dtype)
+            )
+    extra = rows * over // width
     start = pl.multiple_of(r * down_rows, 8)
-    o_ref[0, rows:, :width] = down_ref[pl.ds(start, down_rows), :].astype(o_ref.dtype)
-    o_ref[0, rows:, width:] = jnp.zeros((down_rows, 2 * ff - width), o_ref.dtype)
+    o_ref[0, rows + extra :, :] = down_ref[pl.ds(start, down_rows), :].astype(o_ref.dtype)
 
 
 def packed_weight_grads(recv, gate_delta, up_delta, hidden, n_rep):
@@ -37,6 +48,8 @@
     model_width = recv.shape[1] // 2
     gu_rows = model_width // n_rep
     down_rows = ff // n_rep
+    extra = gu_rows * (2 * ff - model_width) // model_width
+    chunk = gu_rows + extra + down_rows
     flops = 2 * slots * (model_width * 2 * ff + ff * model_width)
     return pl.pallas_call(
         _pack_kernel,
@@ -48,14 +61,31 @@
             pl.BlockSpec((slots, ff), lambda r: (0, 0)),
             pl.BlockSpec((slots, model_width), lambda r: (0, 1)),
         ],
-        out_specs=pl.BlockSpec((1, gu_rows + down_rows, 2 * ff), lambda r: (r, 0, 0)),
-        out_shape=jax.ShapeDtypeStruct((n_rep, gu_rows + down_rows, 2 * ff), jnp.bfloat16),
+        out_specs=pl.BlockSpec((1, chunk, model_width), lambda r: (r, 0, 0)),
+        out_shape=jax.ShapeDtypeStruct((n_rep, chunk, model_width), jnp.bfloat16),
         scratch_shapes=[pltpu.VMEM((ff, model_width), jnp.float32)],
         compiler_params=pltpu.CompilerParams(dimension_semantics=("arbitrary",)),
         cost_estimate=pl.CostEstimate(
-            flops=flops, transcendentals=0, bytes_accessed=2 * n_rep * (gu_rows + down_rows) * 2 * ff
+            flops=flops, transcendentals=0, bytes_accessed=2 * n_rep * chunk * model_width
         ),
     )(recv, gate_delta, up_delta, hidden, recv)
+
+
+def unpack_weight_grads(red, gu_rows, ff):
+    width = red.shape[1]
+    over = 2 * ff - width
+    extra = gu_rows * over // width
+    gate = red[:gu_rows, :ff]
+    up_head = red[:gu_rows, ff:]
+    tiles = red[gu_rows : gu_rows + extra].reshape(
+        extra // TILE_ROWS, TILE_ROWS, width // LANES, LANES
+    )
+    tiles = tiles.transpose(0, 2, 1, 3).reshape(
+        gu_rows // TILE_ROWS, over // LANES, TILE_ROWS, LANES
+    )
+    up_tail = tiles.transpose(0, 2, 1, 3).reshape(gu_rows, over)
+    up = jnp.concatenate([up_head, up_tail], axis=1)
+    return gate, up, red[gu_rows + extra :]
 
 
 def body(tokens, experts, gates, w_gate, w_up, w_down, cotangent):
@@ -111,9 +141,9 @@
     reduced = lax.optimization_barrier(
         lax.psum_scatter(packed, "rep", scatter_dimension=0, tiled=True)
     )[0]
-    grad_gate = reduced[:gu_rows, :ff_width].astype(jnp.float32)
-    grad_up = reduced[:gu_rows, ff_width:].astype(jnp.float32)
-    grad_down = reduced[gu_rows:, :model_width].astype(jnp.float32)
+    grad_gate, grad_up, grad_down = (
+        part.astype(jnp.float32) for part in unpack_weight_grads(reduced, gu_rows, ff_width)
+    )
 
     expert_out = jnp.dot(hidden, down_mat, preferred_element_type=jnp.float32).astype(jnp.bfloat16)
     row_grads = (

time: 236 us -> 227 us (0.962)
  waiting for transfers between devices: 73.8 us -> 63 us
    unnamed x2, waiting for transfers between devices: 36.2 us -> 25.4 us
    convert_element_type x0 -> x2, other arithmetic: none -> 2.81 us  [body(): part.astype(jnp.float32)]
  transfers between devices with their start and end apart: 2 -> 2, of which waited for: 2 -> 2; matrix products, arithmetic and copies ran while one was open for 18% -> 19% of each run, Pallas kernels for 0% -> 0%
where the time goes in v4:
time: 227 us; the launch traced here: 226 us
  waiting for transfers between devices  63 us (28%)
  blocking collectives  44.3 us (20%)
  local copies, waits for them, and re-layouts  34.4 us (15%)
  matrix products  26.6 us (12%)
  Pallas kernels  20.3 us (9%)
  other arithmetic  17.7 us (8%)
  between operations  14.4 us (6%)
  starting transfers between devices  5.52 us (2%)
    all_to_all x1, blocking collectives, body(): lax.all_to_all(disp, 'ep', split_axis=0, concat_axis=0, tiled=True)  44.3 us
    all_to_all x1, waiting for transfers between devices, body(): lax.all_to_all(back, 'ep', split_axis=0, concat_axis=0, tiled=True)  37.6 us
    unnamed x2, waiting for transfers between devices  25.4 us
    pallas_call x1, Pallas kernels, packed_weight_grads(): pl.pallas_call(_pack_kernel, grid=(n_rep,), in_specs=[pl.BlockSpec((slots...  20.3 us
    gather x1, local copies, waits for them, and re-layouts, body(): pair_back = returned[slot_index]  6.18 us
    all_to_all x1, starting transfers between devices, body(): lax.all_to_all(back, 'ep', split_axis=0, concat_axis=0, tiled=True)  5.49 us
    dot_general x1, matrix products, body(): jnp.dot(hidden, down_mat, preferred_element_type=jnp.float32)  5.48 us
    dot_general x1, matrix products, body(): lax.dot_general(up_delta, up_mat, contract, preferred_element_type=jnp.fl...  5.06 us
  transfers between devices with their start and end apart: 2, of which 2 were waited for; matrix products, arithmetic and copies ran while one was open for 19% of the time, Pallas kernels for 0%

profile of v4, /device:TPU:1, one launch (start us, length us, event | category | flops | bytes accessed | tf_op | source)
XLA Modules:
  0.0 226.3 jit_solution(419425952090347970)
XLA Ops:
  7.2 0.0 copy-start
  7.2 0.0 reduce-scatter.4.cloned.1.call-start
  7.2 0.8 copy.26
  8.1 0.1 eq.29
  8.2 0.1 eq.25
  8.3 0.7 broadcast_multiply_fusion.1
  9.0 0.6 reduce-window.6
  9.6 0.2 slice_reduce_fusion
  9.9 0.1 copy.25
  10.0 0.1 mul.77
  10.1 0.1 fusion.26
  10.2 1.4 scatter_custom_fusion
  11.7 0.8 copy.24
  12.4 0.1 reshape.169
  12.6 2.2 scatter_custom_fusion.1
  14.7 0.1 mul.79
  14.8 2.8 %gather_fusion.1 = f32[384]{0:T(512)S(1)} fusion(f32[256]{0:T(256)S(1)} %reshape.169, s32[1024]{0:T(1024)S(1)} %get-tuple-element.13), kind=kCustom, calls=%fused_computation.1 | custom fusion | bytes 4608 | tf_op jit(solution)/shard_map/gather | solution.py:114
  17.7 0.1 mul.83
  17.7 0.0 copy-done
  17.7 0.0 copy-start.1
  17.8 2.5 %gather_fusion.2 = bf16[384,2048]{1,0:T(8,128)(2,1)S(1)} fusion(bf16[128,2048]{1,0:T(8,128)(2,1)S(1)} %copy-done, s32[1024]{0:T(1024)S(1)} %get-tuple-element.14), kind=kCustom, calls=%fused_computation.2 | custom fusion | bytes 3147264 | tf_op jit(solution)/shard_map/gather | solution.py:115
  20.2 3.1 %gather_fusion = bf16[384,2048]{1,0:T(8,128)(2,1)} fusion(bf16[128,2048]{1,0:T(8,128)(2,1)S(1)} %copy-done.1, s32[1024]{0:T(1024)S(1)} %get-tuple-element.14), kind=kCustom, calls=%fused_computation | custom fusion | bytes 3147264 | tf_op jit(solution)/shard_map/gather | solution.py:118
  23.4 0.3 fusion.12
  23.7 1.1 copy-done.4
  24.8 0.2 broadcast_multiply_fusion
  25.0 0.0 slice-start.3
  25.0 0.2 pad_maximum_fusion
  25.2 0.0 slice-start.4
  25.2 44.3 %all_to_all.10 = bf16[8,48,4096]{2,1,0:T(8,128)(2,1)S(1)} all-to-all(bf16[8,48,4096]{2,1,0:T(8,128)(2,1)S(1)} %pad_maximum_fusion), channel_id=1, replica_groups=mesh['rep'=16,'ep'=8] {'ep'}, dimensions={0} | all-to-all | bytes 6291456 | tf_op jit(solution)/shard_map/all_to_all | solution.py:120
  69.5 0.0 slice-start.5
  69.5 0.0 slice-start
  69.5 2.6 %fusion = f32[384,1408]{1,0:T(8,128)S(1)} fusion(bf16[1,1408,2048]{2,1,0:T(8,128)(2,1)S(1)} %bitcast.87, bf16[384,4096]{1,0:T(8,128)(2,1)S(1)} %bitcast.67), kind=kOutput, calls=%fused_computation.6 | convolution fusion | flops 2214592512 | bytes 9502720 | tf_op jit(solution)/shard_map/dot_general | solution.py:133
  72.2 0.0 slice-start.1
  72.2 2.6 %fusion.10 = f32[384,1408]{1,0:T(8,128)S(1)} fusion(bf16[1,2048,1408]{2,1,0:T(8,128)(2,1)S(1)} %bitcast.89, bf16[384,4096]{1,0:T(8,128)(2,1)S(1)} %bitcast.68), kind=kOutput, calls=%fused_computation.16 | convolution fusion | flops 2214592512 | bytes 9502720 | tf_op jit(solution)/shard_map/dot_general | solution.py:128
  74.8 4.5 %multiply_convert_fusion.2 = (bf16[384,1408]{1,0:T(8,128)(2,1)}, bf16[384,1408]{1,0:T(8,128)(2,1)}, bf16[384,1408]{1,0:T(8,128)(2,1)}) fusion(f32[384,1408]{1,0:T(8,128)S(1)} %fusion.10, f32[384,1408]{1,0:T(8,128)S(1)} %fusion, bf16[1,2048,1408]{2,1,0:T(8,128)(2,1)S(1)} %bitcast.85, bf16[384,4096]{1,0:T(8,128)(2,1)S(1)} %bitcast.69), kind=kOutput, calls=%fused_computation.26 | convolution fusion | flops 2222702592 | bytes 14909440 | tf_op jit(solution)/shard_map/dot_general | solution.py:129
  79.4 20.3 %shard_map.118 = bf16[16,264,2048]{2,1,0:T(8,128)(2,1)} custom-call(bf16[384,4096]{1,0:T(8,128)(2,1)} %bitcast.70, bf16[384,1408]{1,0:T(8,128)(2,1)} %get-tuple-element.7.gd_ref, bf16[384,1408]{1,0:T(8,128)(2,1)} %get-tuple-element.8.ud_ref, bf16[384,1408]{1,0:T(8,128)(2,1)} %get-tuple-element.6.h_ref, bf16[384,4096]{1,0:T(8,128)(2,1)} %bitcast.71), custom_call_target="tpu_custom_call" | custom-call | flops 6643777536 | bytes 17301504 | tf_op jit(solution)/shard_map/pallas_call | solution.py:54
  99.7 0.0 reduce-scatter.4.cloned.1.call-update
  99.7 1.2 copy-done.8
  100.9 5.1 %fusion.4 = f32[384,2048]{1,0:T(8,128)S(1)} fusion(bf16[384,1408]{1,0:T(8,128)(2,1)S(1)} %copy-done.8, bf16[1,2048,1408]{2,1,0:T(8,128)(2,1)} %param.11), kind=kOutput, calls=%fused_computation.10 | convolution fusion | flops 2214592512 | bytes 9994240 | tf_op jit(solution)/shard_map/dot_general | solution.py:151
  106.0 0.0 slice-start.7
  106.0 5.5 %fusion.15 = bf16[384,2048]{1,0:T(8,128)(2,1)S(1)} fusion(bf16[384,1408]{1,0:T(8,128)(2,1)S(1)} %copy-done.7, bf16[1,1408,2048]{2,1,0:T(8,128)(2,1)} %param.12), kind=kOutput, calls=%fused_computation.23 | convolution fusion | flops 2215378944 | bytes 8421376 | tf_op jit(solution)/shard_map/dot_general | solution.py:148
  111.5 2.6 %add_convert_fusion = bf16[384,2048]{1,0:T(8,128)(2,1)S(1)} fusion(f32[384,2048]{1,0:T(8,128)S(1)} %fusion.4, bf16[384,1408]{1,0:T(8,128)(2,1)S(1)} %copy-done.6, bf16[1,2048,1408]{2,1,0:T(8,128)(2,1)S(1)} %bitcast.91), kind=kOutput, calls=%fused_computation.22 | convolution fusion | flops 2216165376 | bytes 11567104 | tf_op jit(solution)/shard_map/dot_general | solution.py:150
  114.2 2.0 pad_maximum_fusion.1
  116.2 5.5 %all-to-all-start.1 = ((bf16[8,48,4096]{2,1,0:T(8,128)(2,1)}), bf16[8,48,4096]{2,1,0:T(8,128)(2,1)}, u32[]{:S(2)}, u32[]{:S(2)}) async-start(bf16[8,48,4096]{2,1,0:T(8,128)(2,1)} %bitcast.72), calls=%async_computation.1 | async-start | bytes 6291456 | tf_op jit(solution)/shard_map/all_to_all | solution.py:156
  121.7 37.6 %all-to-all-done.1 = bf16[8,48,4096]{2,1,0:T(8,128)(2,1)} async-done(((bf16[8,48,4096]{2,1,0:T(8,128)(2,1)}), bf16[8,48,4096]{2,1,0:T(8,128)(2,1)}, u32[]{:S(2)}, u32[]{:S(2)}) %all-to-all-start.1) | async-done | bytes 3145760 | tf_op jit(solution)/shard_map/all_to_all | solution.py:156
  159.2 6.2 %gather_fusion.3 = bf16[256,4096]{1,0:T(8,128)(2,1)S(1)} fusion(bf16[384,4096]{1,0:T(8,128)(2,1)} %bitcast.11, s32[1024]{0:T(1024)S(1)} %pad_clamp_fusion), kind=kCustom, calls=%fused_computation.3 | custom fusion | bytes 4195328 | tf_op jit(solution)/shard_map/gather | solution.py:159
  165.4 1.5 convert_multiply_fusion.1
  166.9 3.5 %reshape.163 = f32[128,2,2048]{2,1,0:T(2,128)} reshape(f32[256,2048]{1,0:T(8,128)} %convert_multiply_fusion.1) | data formatting | bytes 4194304 | tf_op jit(solution)/shard_map/reshape | solution.py:163
  170.4 1.5 fusion.34
  171.9 1.9 reshape.164
  173.8 3.6 %reduce = bf16[128,2048]{1,0:T(8,128)(2,1)} reduce(bf16[128,2,2048]{2,1,0:T(2,128)(2,1)S(1)} %reshape.164, bf16[]{:T(256)} %constant.32.clone.1), dimensions={1}, to_apply=%region_6.7.clone | reduce | flops 262144 | bytes 1572866 | tf_op jit(solution)/shard_map/reduce_sum | solution.py:171
  177.4 1.5 reshape.166
  178.9 3.7 %fusion.22 = bf16[128,1,2]{2,1,0:T(2,128)(2,1)S(1)} fusion(bf16[128,2,2048]{2,1,0:T(2,128)(2,1)} %reshape.166, bf16[128,2048,1]{1,0,2:T(8,128)(2,1)S(1)} %bitcast.66), kind=kOutput, calls=%fused_computation.33 | convolution fusion | flops 1048576 | bytes 1573376 | tf_op jit(solution)/shard_map/tkd,td->tk/dot_general | solution.py:165
  182.6 0.6 copy.31
  183.3 3.8 %reduce_sum.31 = bf16[128,2048]{1,0:T(8,128)(2,1)} reduce(f32[128,2,2048]{2,1,0:T(2,128)S(1)} %copy-done.3, f32[]{:T(128)} %constant.36.clone.1), dimensions={1}, to_apply=%region_5.6 | reduce | flops 262144 | bytes 2621444 | tf_op jit(solution)/shard_map/reduce_sum | solution.py:162
  187.0 25.4 %reduce-scatter.4.cloned.1.call-done = bf16[1,264,2048]{2,1,0:T(8,128)(2,1)} async-done(((bf16[16,264,2048]{2,1,0:T(8,128)(2,1)}), bf16[1,264,2048]{2,1,0:T(8,128)(2,1)}) %reduce-scatter.4.cloned.1.call-update) | async-done | bytes 1081360
  212.4 0.9 slice_bitcast_fusion.1
  213.4 0.9 slice_bitcast_fusion.2
  214.3 1.9 fusion.24
  216.2 1.9 slice_convert_fusion
  218.2 0.1 copy.28
  218.2 0.1 copy.29
  218.3 0.2 concatenate.24
  218.6 0.9 maximum_convert_fusion
  (39 shorter events, 0.2 us)
Async XLA Ops:
  7.2 10.6 %copy-start = (bf16[128,2048]{1,0:T(8,128)(2,1)S(1)}, bf16[128,2048]{1,0:T(8,128)(2,1)}, u32[]{:S(2)}) copy-start(bf16[128,2048]{1,0:T(8,128)(2,1)} %param.13) | copy-start | bytes 1572868
  7.2 205.3 %reduce-scatter.4.cloned.1.call-start = ((), (), s32[]{:S(2)}) async-start(), calls=%async_computation.3 | async-start | bytes 18382848
  17.7 2.5 %copy-start.1 = (bf16[128,2048]{1,0:T(8,128)(2,1)S(1)}, bf16[128,2048]{1,0:T(8,128)(2,1)}, u32[]{:S(2)}) copy-start(bf16[128,2048]{1,0:T(8,128)(2,1)} %param.7) | copy-start | bytes 1572868
  23.4 1.4 copy-start.4
  24.8 44.7 %slice-start.2 = ((s8[5767168]{0:T(1024)(128)(4,1)}), s8[4194304]{0:T(1024)(128)(4,1)S(1)}, s32[]{:S(2)}) async-start(s8[5767168]{0:T(1024)(128)(4,1)} %bitcast.86), calls=%async_computation.6 | async-start | bytes 8388608
  25.0 44.5 %slice-start.3 = ((s8[5767168]{0:T(1024)(128)(4,1)}), s8[1572864]{0:T(1024)(128)(4,1)S(1)}, s32[]{:S(2)}) async-start(s8[5767168]{0:T(1024)(128)(4,1)} %bitcast.86), calls=%async_computation.7 | async-start | bytes 3145728
  25.2 47.0 %slice-start.4 = ((s8[5767168]{0:T(1024)(128)(4,1)}), s8[4194304]{0:T(1024)(128)(4,1)S(1)}, s32[]{:S(2)}) async-start(s8[5767168]{0:T(1024)(128)(4,1)} %bitcast.88), calls=%async_computation.8 | async-start | bytes 8388608
  69.5 5.3 %copy-start.2 = (bf16[8,48,4096]{2,1,0:T(8,128)(2,1)}, bf16[8,48,4096]{2,1,0:T(8,128)(2,1)S(1)}, u32[]{:S(2)}) copy-start(bf16[8,48,4096]{2,1,0:T(8,128)(2,1)S(1)} %all_to_all.10) | copy-start | bytes 9437188
  69.5 2.7 %slice-start.5 = ((s8[5767168]{0:T(1024)(128)(4,1)}), s8[1572864]{0:T(1024)(128)(4,1)S(1)}, s32[]{:S(2)}) async-start(s8[5767168]{0:T(1024)(128)(4,1)} %bitcast.88), calls=%async_computation.9 | async-start | bytes 3145728
  69.5 5.3 %slice-start = ((s8[5767168]{0:T(1024)(128)(4,1)}), s8[4194304]{0:T(1024)(128)(4,1)S(1)}, s32[]{:S(2)}) async-start(s8[5767168]{0:T(1024)(128)(4,1)} %bitcast.84), calls=%async_computation.4 | async-start | bytes 8388608
  72.2 2.6 %slice-start.1 = ((s8[5767168]{0:T(1024)(128)(4,1)}), s8[1572864]{0:T(1024)(128)(4,1)S(1)}, s32[]{:S(2)}) async-start(s8[5767168]{0:T(1024)(128)(4,1)} %bitcast.84), calls=%async_computation.5 | async-start | bytes 3145728
  99.7 1.2 copy-start.8
  100.9 5.1 %copy-start.7 = (bf16[384,1408]{1,0:T(8,128)(2,1)S(1)}, bf16[384,1408]{1,0:T(8,128)(2,1)}, u32[]{:S(2)}) copy-start(bf16[384,1408]{1,0:T(8,128)(2,1)} %get-tuple-element.6.h_ref) | copy-start | bytes 3244036
  100.9 10.6 %slice-start.6 = ((s8[5767168]{0:T(1024)(128)(4,1)}), s8[4194304]{0:T(1024)(128)(4,1)S(1)}, s32[]{:S(2)}) async-start(s8[5767168]{0:T(1024)(128)(4,1)} %bitcast.90), calls=%async_computation.10 | async-start | bytes 8388608
  106.0 5.5 %copy-start.6 = (bf16[384,1408]{1,0:T(8,128)(2,1)S(1)}, bf16[384,1408]{1,0:T(8,128)(2,1)}, u32[]{:S(2)}) copy-start(bf16[384,1408]{1,0:T(8,128)(2,1)} %get-tuple-element.7.gd_ref) | copy-start | bytes 3244036
  106.0 5.5 %slice-start.7 = ((s8[5767168]{0:T(1024)(128)(4,1)}), s8[1572864]{0:T(1024)(128)(4,1)S(1)}, s32[]{:S(2)}) async-start(s8[5767168]{0:T(1024)(128)(4,1)} %bitcast.90), calls=%async_computation.11 | async-start | bytes 3145728
  116.2 43.1 %all-to-all-start.1 = ((bf16[8,48,4096]{2,1,0:T(8,128)(2,1)}), bf16[8,48,4096]{2,1,0:T(8,128)(2,1)}, u32[]{:S(2)}, u32[]{:S(2)}) async-start(bf16[8,48,4096]{2,1,0:T(8,128)(2,1)} %bitcast.72), calls=%async_computation.1 | async-start | bytes 6291456 | tf_op jit(solution)/shard_map/all_to_all | solution.py:156
  171.9 5.5 %copy-start.5 = (bf16[256,2048]{1,0:T(8,128)(2,1)S(1)}, bf16[256,2048]{1,0:T(8,128)(2,1)}, u32[]{:S(2)}) copy-start(bf16[256,2048]{1,0:T(8,128)(2,1)} %get-tuple-element.9) | copy-start | bytes 3145732
  178.9 4.3 %copy-start.3 = (f32[128,2,2048]{2,1,0:T(2,128)S(1)}, f32[128,2,2048]{2,1,0:T(2,128)}, u32[]{:S(2)}) copy-start(f32[128,2,2048]{2,1,0:T(2,128)} %reshape.163) | copy-start | bytes 6291460
Sparse Core Ops, SparseCore 0:
  99.8 112.5 reduce-scatter.3

commit v5 on v4

--- a/solution.py
+++ b/solution.py
@@ -13,8 +13,9 @@
 def _pack_kernel(x_ref, gd_ref, ud_ref, h_ref, og_ref, o_ref, down_ref):
     ff = gd_ref.shape[1]
     width = og_ref.shape[1]
-    rows = x_ref.shape[1]
-    down_rows = down_ref.shape[0] // pl.num_programs(0)
+    group, chunk, _ = o_ref.shape
+    rows = x_ref.shape[1] // group
+    down_rows = down_ref.shape[0] // (group * pl.num_programs(0))
     over = 2 * ff - width
     first = (((0,), (0,)), ((), ()))
     r = pl.program_id(0)
@@ -26,21 +27,27 @@
         )
 
     x = x_ref[...]
-    g = lax.dot_general(x, gd_ref[...], first, preferred_element_type=jnp.float32)
-    u = lax.dot_general(x, ud_ref[...], first, preferred_element_type=jnp.float32)
-    o_ref[0, :rows, :ff] = g.astype(o_ref.dtype)
-    o_ref[0, :rows, ff:] = u[:, : width - ff].astype(o_ref.dtype)
+    g_all = lax.dot_general(x, gd_ref[...], first, preferred_element_type=jnp.float32)
+    u_all = lax.dot_general(x, ud_ref[...], first, preferred_element_type=jnp.float32)
     col_tiles = over // LANES
-    for i in range(rows // TILE_ROWS):
-        for j in range(col_tiles):
-            q, p = divmod(i * col_tiles + j, width // LANES)
-            src = u[i * TILE_ROWS : (i + 1) * TILE_ROWS, width - ff + j * LANES :][:, :LANES]
-            o_ref[0, rows + q * TILE_ROWS : rows + (q + 1) * TILE_ROWS, p * LANES : (p + 1) * LANES] = (
-                src.astype(o_ref.dtype)
-            )
     extra = rows * over // width
-    start = pl.multiple_of(r * down_rows, 8)
-    o_ref[0, rows + extra :, :] = down_ref[pl.ds(start, down_rows), :].astype(o_ref.dtype)
+    for c in range(group):
+        g = g_all[c * rows : (c + 1) * rows]
+        u = u_all[c * rows : (c + 1) * rows]
+        o_ref[c, :rows, :ff] = g.astype(o_ref.dtype)
+        o_ref[c, :rows, ff:] = u[:, : width - ff].astype(o_ref.dtype)
+        for i in range(rows // TILE_ROWS):
+            for j in range(col_tiles):
+                q, p = divmod(i * col_tiles + j, width // LANES)
+                src = u[i * TILE_ROWS : (i + 1) * TILE_ROWS, width - ff + j * LANES :][:, :LANES]
+                o_ref[
+                    c, rows + q * TILE_ROWS : rows + (q + 1) * TILE_ROWS, p * LANES : (p + 1) * LANES
+                ] = src.astype(o_ref.dtype)
+        start = pl.multiple_of((r * group + c) * down_rows, 8)
+        o_ref[c, rows + extra :, :] = down_ref[pl.ds(start, down_rows), :].astype(o_ref.dtype)
+
+
+GROUP = 4
 
 
 def packed_weight_grads(recv, gate_delta, up_delta, hidden, n_rep):
@@ -51,17 +58,18 @@
     extra = gu_rows * (2 * ff - model_width) // model_width
     chunk = gu_rows + extra + down_rows
     flops = 2 * slots * (model_width * 2 * ff + ff * model_width)
+    group = GROUP if n_rep % GROUP == 0 else 1
     return pl.pallas_call(
         _pack_kernel,
-        grid=(n_rep,),
+        grid=(n_rep // group,),
         in_specs=[
-            pl.BlockSpec((slots, gu_rows), lambda r: (0, r)),
+            pl.BlockSpec((slots, group * gu_rows), lambda r: (0, r)),
             pl.BlockSpec((slots, ff), lambda r: (0, 0)),
             pl.BlockSpec((slots, ff), lambda r: (0, 0)),
             pl.BlockSpec((slots, ff), lambda r: (0, 0)),
             pl.BlockSpec((slots, model_width), lambda r: (0, 1)),
         ],
-        out_specs=pl.BlockSpec((1, chunk, model_width), lambda r: (r, 0, 0)),
+        out_specs=pl.BlockSpec((group, chunk, model_width), lambda r: (r, 0, 0)),
         out_shape=jax.ShapeDtypeStruct((n_rep, chunk, model_width), jnp.bfloat16),
         scratch_shapes=[pltpu.VMEM((ff, model_width), jnp.float32)],
         compiler_params=pltpu.CompilerParams(dimension_semantics=("arbitrary",)),

time: 227 us -> 222 us (0.978)
  Pallas kernels: 20.3 us -> 15.3 us
    pallas_call x1, Pallas kernels: 20.3 us -> 15.3 us  [packed_weight_grads(): pl.pallas_call(_pack_kernel, grid=(n_rep // group,), in_specs=[pl.BlockSp...]
where the time goes in v5:
time: 222 us; the launch traced here: 221 us
  waiting for transfers between devices  63 us (28%)
  blocking collectives  44.3 us (20%)
  local copies, waits for them, and re-layouts  34.4 us (15%)
  matrix products  26.6 us (12%)
  other arithmetic  17.7 us (8%)
  Pallas kernels  15.3 us (7%)
  between operations  14.4 us (6%)
  starting transfers between devices  5.53 us (2%)
    all_to_all x1, blocking collectives, body(): lax.all_to_all(disp, 'ep', split_axis=0, concat_axis=0, tiled=True)  44.3 us
    all_to_all x1, waiting for transfers between devices, body(): lax.all_to_all(back, 'ep', split_axis=0, concat_axis=0, tiled=True)  37.6 us
    unnamed x2, waiting for transfers between devices  25.4 us
    pallas_call x1, Pallas kernels, packed_weight_grads(): pl.pallas_call(_pack_kernel, grid=(n_rep // group,), in_specs=[pl.BlockSp...  15.3 us
    gather x1, local copies, waits for them, and re-layouts, body(): pair_back = returned[slot_index]  6.18 us
    all_to_all x1, starting transfers between devices, body(): lax.all_to_all(back, 'ep', split_axis=0, concat_axis=0, tiled=True)  5.49 us
    dot_general x1, matrix products, body(): jnp.dot(hidden, down_mat, preferred_element_type=jnp.float32)  5.48 us
    dot_general x1, matrix products, body(): lax.dot_general(up_delta, up_mat, contract, preferred_element_type=jnp.fl...  5.06 us
  transfers between devices with their start and end apart: 2, of which 2 were waited for; matrix products, arithmetic and copies ran while one was open for 19% of the time, Pallas kernels for 0%

profile of v5, /device:TPU:1, one launch (start us, length us, event | category | flops | bytes accessed | tf_op | source)
XLA Modules:
  0.0 221.3 jit_solution(9865645811233900739)
XLA Ops:
  7.2 0.0 copy-start
  7.2 0.0 reduce-scatter.4.cloned.1.call-start
  7.2 0.8 copy.26
  8.1 0.1 eq.29
  8.2 0.1 eq.25
  8.3 0.7 broadcast_multiply_fusion.1
  9.0 0.6 reduce-window.6
  9.6 0.2 slice_reduce_fusion
  9.9 0.1 copy.25
  10.0 0.1 mul.77
  10.1 0.1 fusion.26
  10.2 1.4 scatter_custom_fusion
  11.7 0.8 copy.24
  12.4 0.1 reshape.169
  12.6 2.2 scatter_custom_fusion.1
  14.7 0.1 mul.79
  14.8 2.8 %gather_fusion.1 = f32[384]{0:T(512)S(1)} fusion(f32[256]{0:T(256)S(1)} %reshape.169, s32[1024]{0:T(1024)S(1)} %get-tuple-element.13), kind=kCustom, calls=%fused_computation.1 | custom fusion | bytes 4608 | tf_op jit(solution)/shard_map/gather | solution.py:122
  17.7 0.1 mul.83
  17.7 0.0 copy-start.1
  17.8 2.5 %gather_fusion.2 = bf16[384,2048]{1,0:T(8,128)(2,1)S(1)} fusion(bf16[128,2048]{1,0:T(8,128)(2,1)S(1)} %copy-done, s32[1024]{0:T(1024)S(1)} %get-tuple-element.14), kind=kCustom, calls=%fused_computation.2 | custom fusion | bytes 3147264 | tf_op jit(solution)/shard_map/gather | solution.py:123
  20.2 3.1 %gather_fusion = bf16[384,2048]{1,0:T(8,128)(2,1)} fusion(bf16[128,2048]{1,0:T(8,128)(2,1)S(1)} %copy-done.1, s32[1024]{0:T(1024)S(1)} %get-tuple-element.14), kind=kCustom, calls=%fused_computation | custom fusion | bytes 3147264 | tf_op jit(solution)/shard_map/gather | solution.py:126
  23.4 0.3 fusion.12
  23.7 1.1 copy-done.4
  24.8 0.2 broadcast_multiply_fusion
  25.0 0.0 slice-start.3
  25.0 0.2 pad_maximum_fusion
  25.2 0.0 slice-start.4
  25.2 44.3 %all_to_all.10 = bf16[8,48,4096]{2,1,0:T(8,128)(2,1)S(1)} all-to-all(bf16[8,48,4096]{2,1,0:T(8,128)(2,1)S(1)} %pad_maximum_fusion), channel_id=1, replica_groups=mesh['rep'=16,'ep'=8] {'ep'}, dimensions={0} | all-to-all | bytes 6291456 | tf_op jit(solution)/shard_map/all_to_all | solution.py:128
  69.5 0.0 slice-done.2
  69.5 0.0 slice-start.5
  69.5 0.0 slice-start
  69.5 2.6 %fusion = f32[384,1408]{1,0:T(8,128)S(1)} fusion(bf16[1,1408,2048]{2,1,0:T(8,128)(2,1)S(1)} %bitcast.87, bf16[384,4096]{1,0:T(8,128)(2,1)S(1)} %bitcast.67), kind=kOutput, calls=%fused_computation.6 | convolution fusion | flops 2214592512 | bytes 9502720 | tf_op jit(solution)/shard_map/dot_general | solution.py:141
  72.2 0.0 slice-start.1
  72.2 2.6 %fusion.10 = f32[384,1408]{1,0:T(8,128)S(1)} fusion(bf16[1,2048,1408]{2,1,0:T(8,128)(2,1)S(1)} %bitcast.89, bf16[384,4096]{1,0:T(8,128)(2,1)S(1)} %bitcast.68), kind=kOutput, calls=%fused_computation.16 | convolution fusion | flops 2214592512 | bytes 9502720 | tf_op jit(solution)/shard_map/dot_general | solution.py:136
  74.8 4.5 %multiply_convert_fusion.2 = (bf16[384,1408]{1,0:T(8,128)(2,1)}, bf16[384,1408]{1,0:T(8,128)(2,1)}, bf16[384,1408]{1,0:T(8,128)(2,1)}) fusion(f32[384,1408]{1,0:T(8,128)S(1)} %fusion.10, f32[384,1408]{1,0:T(8,128)S(1)} %fusion, bf16[1,2048,1408]{2,1,0:T(8,128)(2,1)S(1)} %bitcast.85, bf16[384,4096]{1,0:T(8,128)(2,1)S(1)} %bitcast.69), kind=kOutput, calls=%fused_computation.26 | convolution fusion | flops 2222702592 | bytes 14909440 | tf_op jit(solution)/shard_map/dot_general | solution.py:137
  79.4 15.3 %shard_map.118 = bf16[16,264,2048]{2,1,0:T(8,128)(2,1)} custom-call(bf16[384,4096]{1,0:T(8,128)(2,1)} %bitcast.70, bf16[384,1408]{1,0:T(8,128)(2,1)} %get-tuple-element.7.gd_ref, bf16[384,1408]{1,0:T(8,128)(2,1)} %get-tuple-element.8.ud_ref, bf16[384,1408]{1,0:T(8,128)(2,1)} %get-tuple-element.6.h_ref, bf16[384,4096]{1,0:T(8,128)(2,1)} %bitcast.71), custom_call_target="tpu_custom_call" | custom-call | flops 6643777536 | bytes 17301504 | tf_op jit(solution)/shard_map/pallas_call | solution.py:62
  94.7 0.0 reduce-scatter.4.cloned.1.call-update
  94.7 1.2 copy-done.8
  95.9 5.1 %fusion.4 = f32[384,2048]{1,0:T(8,128)S(1)} fusion(bf16[384,1408]{1,0:T(8,128)(2,1)S(1)} %copy-done.8, bf16[1,2048,1408]{2,1,0:T(8,128)(2,1)} %param.11), kind=kOutput, calls=%fused_computation.10 | convolution fusion | flops 2214592512 | bytes 9994240 | tf_op jit(solution)/shard_map/dot_general | solution.py:159
  101.0 0.0 slice-start.7
  101.0 5.5 %fusion.15 = bf16[384,2048]{1,0:T(8,128)(2,1)S(1)} fusion(bf16[384,1408]{1,0:T(8,128)(2,1)S(1)} %copy-done.7, bf16[1,1408,2048]{2,1,0:T(8,128)(2,1)} %param.12), kind=kOutput, calls=%fused_computation.23 | convolution fusion | flops 2215378944 | bytes 8421376 | tf_op jit(solution)/shard_map/dot_general | solution.py:156
  106.6 2.6 %add_convert_fusion = bf16[384,2048]{1,0:T(8,128)(2,1)S(1)} fusion(f32[384,2048]{1,0:T(8,128)S(1)} %fusion.4, bf16[384,1408]{1,0:T(8,128)(2,1)S(1)} %copy-done.6, bf16[1,2048,1408]{2,1,0:T(8,128)(2,1)S(1)} %bitcast.91), kind=kOutput, calls=%fused_computation.22 | convolution fusion | flops 2216165376 | bytes 11567104 | tf_op jit(solution)/shard_map/dot_general | solution.py:158
  109.2 2.0 pad_maximum_fusion.1
  111.2 5.5 %all-to-all-start.1 = ((bf16[8,48,4096]{2,1,0:T(8,128)(2,1)}), bf16[8,48,4096]{2,1,0:T(8,128)(2,1)}, u32[]{:S(2)}, u32[]{:S(2)}) async-start(bf16[8,48,4096]{2,1,0:T(8,128)(2,1)} %bitcast.72), calls=%async_computation.1 | async-start | bytes 6291456 | tf_op jit(solution)/shard_map/all_to_all | solution.py:164
  116.7 37.6 %all-to-all-done.1 = bf16[8,48,4096]{2,1,0:T(8,128)(2,1)} async-done(((bf16[8,48,4096]{2,1,0:T(8,128)(2,1)}), bf16[8,48,4096]{2,1,0:T(8,128)(2,1)}, u32[]{:S(2)}, u32[]{:S(2)}) %all-to-all-start.1) | async-done | bytes 3145760 | tf_op jit(solution)/shard_map/all_to_all | solution.py:164
  154.3 6.2 %gather_fusion.3 = bf16[256,4096]{1,0:T(8,128)(2,1)S(1)} fusion(bf16[384,4096]{1,0:T(8,128)(2,1)} %bitcast.11, s32[1024]{0:T(1024)S(1)} %pad_clamp_fusion), kind=kCustom, calls=%fused_computation.3 | custom fusion | bytes 4195328 | tf_op jit(solution)/shard_map/gather | solution.py:167
  160.4 1.5 convert_multiply_fusion.1
  162.0 3.5 %reshape.163 = f32[128,2,2048]{2,1,0:T(2,128)} reshape(f32[256,2048]{1,0:T(8,128)} %convert_multiply_fusion.1) | data formatting | bytes 4194304 | tf_op jit(solution)/shard_map/reshape | solution.py:171
  165.5 1.5 fusion.34
  167.0 1.9 reshape.164
  168.8 3.6 %reduce = bf16[128,2048]{1,0:T(8,128)(2,1)} reduce(bf16[128,2,2048]{2,1,0:T(2,128)(2,1)S(1)} %reshape.164, bf16[]{:T(256)} %constant.32.clone.1), dimensions={1}, to_apply=%region_6.7.clone | reduce | flops 262144 | bytes 1572866 | tf_op jit(solution)/shard_map/reduce_sum | solution.py:179
  172.5 1.5 reshape.166
  174.0 3.7 %fusion.22 = bf16[128,1,2]{2,1,0:T(2,128)(2,1)S(1)} fusion(bf16[128,2,2048]{2,1,0:T(2,128)(2,1)} %reshape.166, bf16[128,2048,1]{1,0,2:T(8,128)(2,1)S(1)} %bitcast.66), kind=kOutput, calls=%fused_computation.33 | convolution fusion | flops 1048576 | bytes 1573376 | tf_op jit(solution)/shard_map/tkd,td->tk/dot_general | solution.py:173
  177.7 0.6 copy.31
  178.3 3.8 %reduce_sum.31 = bf16[128,2048]{1,0:T(8,128)(2,1)} reduce(f32[128,2,2048]{2,1,0:T(2,128)S(1)} %copy-done.3, f32[]{:T(128)} %constant.36.clone.1), dimensions={1}, to_apply=%region_5.6 | reduce | flops 262144 | bytes 2621444 | tf_op jit(solution)/shard_map/reduce_sum | solution.py:170
  182.1 25.4 %reduce-scatter.4.cloned.1.call-done = bf16[1,264,2048]{2,1,0:T(8,128)(2,1)} async-done(((bf16[16,264,2048]{2,1,0:T(8,128)(2,1)}), bf16[1,264,2048]{2,1,0:T(8,128)(2,1)}) %reduce-scatter.4.cloned.1.call-update) | async-done | bytes 1081360
  207.5 0.9 slice_bitcast_fusion.1
  208.4 0.9 slice_bitcast_fusion.2
  209.3 1.9 fusion.24
  211.2 1.9 slice_convert_fusion
  213.2 0.1 copy.28
  213.3 0.1 copy.29
  213.3 0.2 concatenate.24
  213.6 0.9 maximum_convert_fusion
  (39 shorter events, 0.2 us)
Async XLA Ops:
  7.2 10.6 %copy-start = (bf16[128,2048]{1,0:T(8,128)(2,1)S(1)}, bf16[128,2048]{1,0:T(8,128)(2,1)}, u32[]{:S(2)}) copy-start(bf16[128,2048]{1,0:T(8,128)(2,1)} %param.13) | copy-start | bytes 1572868
  7.2 200.3 %reduce-scatter.4.cloned.1.call-start = ((), (), s32[]{:S(2)}) async-start(), calls=%async_computation.3 | async-start | bytes 18382848
  17.7 2.5 %copy-start.1 = (bf16[128,2048]{1,0:T(8,128)(2,1)S(1)}, bf16[128,2048]{1,0:T(8,128)(2,1)}, u32[]{:S(2)}) copy-start(bf16[128,2048]{1,0:T(8,128)(2,1)} %param.7) | copy-start | bytes 1572868
  23.4 1.4 copy-start.4
  24.8 44.7 %slice-start.2 = ((s8[5767168]{0:T(1024)(128)(4,1)}), s8[4194304]{0:T(1024)(128)(4,1)S(1)}, s32[]{:S(2)}) async-start(s8[5767168]{0:T(1024)(128)(4,1)} %bitcast.86), calls=%async_computation.6 | async-start | bytes 8388608
  25.0 44.5 %slice-start.3 = ((s8[5767168]{0:T(1024)(128)(4,1)}), s8[1572864]{0:T(1024)(128)(4,1)S(1)}, s32[]{:S(2)}) async-start(s8[5767168]{0:T(1024)(128)(4,1)} %bitcast.86), calls=%async_computation.7 | async-start | bytes 3145728
  25.2 47.0 %slice-start.4 = ((s8[5767168]{0:T(1024)(128)(4,1)}), s8[4194304]{0:T(1024)(128)(4,1)S(1)}, s32[]{:S(2)}) async-start(s8[5767168]{0:T(1024)(128)(4,1)} %bitcast.88), calls=%async_computation.8 | async-start | bytes 8388608
  69.5 5.3 %copy-start.2 = (bf16[8,48,4096]{2,1,0:T(8,128)(2,1)}, bf16[8,48,4096]{2,1,0:T(8,128)(2,1)S(1)}, u32[]{:S(2)}) copy-start(bf16[8,48,4096]{2,1,0:T(8,128)(2,1)S(1)} %all_to_all.10) | copy-start | bytes 9437188
  69.5 2.7 %slice-start.5 = ((s8[5767168]{0:T(1024)(128)(4,1)}), s8[1572864]{0:T(1024)(128)(4,1)S(1)}, s32[]{:S(2)}) async-start(s8[5767168]{0:T(1024)(128)(4,1)} %bitcast.88), calls=%async_computation.9 | async-start | bytes 3145728
  69.5 5.3 %slice-start = ((s8[5767168]{0:T(1024)(128)(4,1)}), s8[4194304]{0:T(1024)(128)(4,1)S(1)}, s32[]{:S(2)}) async-start(s8[5767168]{0:T(1024)(128)(4,1)} %bitcast.84), calls=%async_computation.4 | async-start | bytes 8388608
  72.2 2.6 %slice-start.1 = ((s8[5767168]{0:T(1024)(128)(4,1)}), s8[1572864]{0:T(1024)(128)(4,1)S(1)}, s32[]{:S(2)}) async-start(s8[5767168]{0:T(1024)(128)(4,1)} %bitcast.84), calls=%async_computation.5 | async-start | bytes 3145728
  94.7 1.2 copy-start.8
  95.9 5.1 %copy-start.7 = (bf16[384,1408]{1,0:T(8,128)(2,1)S(1)}, bf16[384,1408]{1,0:T(8,128)(2,1)}, u32[]{:S(2)}) copy-start(bf16[384,1408]{1,0:T(8,128)(2,1)} %get-tuple-element.6.h_ref) | copy-start | bytes 3244036
  95.9 10.6 %slice-start.6 = ((s8[5767168]{0:T(1024)(128)(4,1)}), s8[4194304]{0:T(1024)(128)(4,1)S(1)}, s32[]{:S(2)}) async-start(s8[5767168]{0:T(1024)(128)(4,1)} %bitcast.90), calls=%async_computation.10 | async-start | bytes 8388608
  101.0 5.5 %copy-start.6 = (bf16[384,1408]{1,0:T(8,128)(2,1)S(1)}, bf16[384,1408]{1,0:T(8,128)(2,1)}, u32[]{:S(2)}) copy-start(bf16[384,1408]{1,0:T(8,128)(2,1)} %get-tuple-element.7.gd_ref) | copy-start | bytes 3244036
  101.0 5.5 %slice-start.7 = ((s8[5767168]{0:T(1024)(128)(4,1)}), s8[1572864]{0:T(1024)(128)(4,1)S(1)}, s32[]{:S(2)}) async-start(s8[5767168]{0:T(1024)(128)(4,1)} %bitcast.90), calls=%async_computation.11 | async-start | bytes 3145728
  111.2 43.1 %all-to-all-start.1 = ((bf16[8,48,4096]{2,1,0:T(8,128)(2,1)}), bf16[8,48,4096]{2,1,0:T(8,128)(2,1)}, u32[]{:S(2)}, u32[]{:S(2)}) async-start(bf16[8,48,4096]{2,1,0:T(8,128)(2,1)} %bitcast.72), calls=%async_computation.1 | async-start | bytes 6291456 | tf_op jit(solution)/shard_map/all_to_all | solution.py:164
  167.0 5.5 %copy-start.5 = (bf16[256,2048]{1,0:T(8,128)(2,1)S(1)}, bf16[256,2048]{1,0:T(8,128)(2,1)}, u32[]{:S(2)}) copy-start(bf16[256,2048]{1,0:T(8,128)(2,1)} %get-tuple-element.9) | copy-start | bytes 3145732
  173.9 4.3 %copy-start.3 = (f32[128,2,2048]{2,1,0:T(2,128)S(1)}, f32[128,2,2048]{2,1,0:T(2,128)}, u32[]{:S(2)}) copy-start(f32[128,2,2048]{2,1,0:T(2,128)} %reshape.163) | copy-start | bytes 6291460
Sparse Core Ops, SparseCore 0:
  94.8 112.5 reduce-scatter.3

commit v6 on v5

--- a/solution.py
+++ b/solution.py
@@ -50,9 +50,9 @@
 GROUP = 4
 
 
-def packed_weight_grads(recv, gate_delta, up_delta, hidden, n_rep):
+def packed_weight_grads(rows_in, gate_delta, up_delta, hidden, out_grads, n_rep):
     slots, ff = gate_delta.shape
-    model_width = recv.shape[1] // 2
+    model_width = rows_in.shape[1]
     gu_rows = model_width // n_rep
     down_rows = ff // n_rep
     extra = gu_rows * (2 * ff - model_width) // model_width
@@ -67,7 +67,7 @@
             pl.BlockSpec((slots, ff), lambda r: (0, 0)),
             pl.BlockSpec((slots, ff), lambda r: (0, 0)),
             pl.BlockSpec((slots, ff), lambda r: (0, 0)),
-            pl.BlockSpec((slots, model_width), lambda r: (0, 1)),
+            pl.BlockSpec((slots, model_width), lambda r: (0, 0)),
         ],
         out_specs=pl.BlockSpec((group, chunk, model_width), lambda r: (r, 0, 0)),
         out_shape=jax.ShapeDtypeStruct((n_rep, chunk, model_width), jnp.bfloat16),
@@ -76,7 +76,7 @@
         cost_estimate=pl.CostEstimate(
             flops=flops, transcendentals=0, bytes_accessed=2 * n_rep * chunk * model_width
         ),
-    )(recv, gate_delta, up_delta, hidden, recv)
+    )(rows_in, gate_delta, up_delta, hidden, out_grads)
 
 
 def unpack_weight_grads(red, gu_rows, ff):
@@ -122,14 +122,14 @@
     slot_weight = weights[source] * filled[:, None].astype(jnp.float32)
     scaled_rows = (slot_weight * cotangent[token_src].astype(jnp.float32)).astype(jnp.bfloat16)
 
-    disp = jnp.concatenate(
-        [tokens[token_src] * filled[:, None], scaled_rows], axis=1
-    ).reshape(n_experts, capacity, 2 * model_width)
-    recv = lax.all_to_all(disp, "ep", split_axis=0, concat_axis=0, tiled=True).reshape(
-        slots, 2 * model_width
-    )
-    rows_in = recv[:, :model_width]
-    out_grads = recv[:, model_width:]
+    tok_disp = (tokens[token_src] * filled[:, None]).reshape(n_experts, capacity, model_width)
+    rows_in = lax.all_to_all(tok_disp, "ep", split_axis=0, concat_axis=0, tiled=True).reshape(
+        slots, model_width
+    )
+    grad_disp = scaled_rows.reshape(n_experts, capacity, model_width)
+    out_grads = lax.all_to_all(grad_disp, "ep", split_axis=0, concat_axis=0, tiled=True).reshape(
+        slots, model_width
+    )
 
     contract = (((1,), (1,)), ((), ()))
     rows_first = (((0,), (0,)), ((), ()))
@@ -145,7 +145,7 @@
     up_delta = (hidden_grad * activated).astype(jnp.bfloat16)
 
     gu_rows = model_width // n_rep
-    packed = packed_weight_grads(recv, gate_delta, up_delta, hidden, n_rep)
+    packed = packed_weight_grads(rows_in, gate_delta, up_delta, hidden, out_grads, n_rep)
     reduced = lax.optimization_barrier(
         lax.psum_scatter(packed, "rep", scatter_dimension=0, tiled=True)
     )[0]

time: 222 us -> 230 us (1.036)
  blocking collectives: 44.3 us -> 0 us
  waiting for transfers between devices: 63 us -> 93.5 us
  starting transfers between devices: 5.53 us -> 16.7 us
  matrix products: 26.6 us -> 36.9 us
  other arithmetic: 17.7 us -> 20.1 us
    all_to_all x1 -> x0, blocking collectives: 44.3 us -> none  [body(): lax.all_to_all(disp, 'ep', split_axis=0, concat_axis=0, tiled=True)]
    all_to_all x0 -> x2, waiting for transfers between devices: none -> 30.3 us  [the longest x1 16.8 us: body(): lax.all_to_all(grad_disp, 'ep', split_axis=0, concat_axis=0, tiled=True)]
    all_to_all x0 -> x2, starting transfers between devices: none -> 11.4 us  [the longest x1 6.93 us: body(): lax.all_to_all(grad_disp, 'ep', split_axis=0, concat_axis=0, tiled=True)]
    dot_general x1, matrix products: 2.64 us -> 7.11 us  [body(): lax.dot_general(out_grads, down_mat, contract, preferred_element_type=jnp...]
    dot_general x1, matrix products: 2.59 us -> 5.87 us  [body(): gate_pre = jnp.dot(rows_in, gate_mat, preferred_element_type=jnp.float32)]
    dot_general x1, matrix products: 4.53 us -> 7.33 us  [body(): up_pre = jnp.dot(rows_in, up_mat, preferred_element_type=jnp.float32)]
  transfers between devices with their start and end apart: 2 -> 4, of which waited for: 2 -> 4; matrix products, arithmetic and copies ran while one was open for 19% -> 23% of each run, Pallas kernels for 0% -> 0%
where the time goes in v6:
time: 230 us; the launch traced here: 229 us
  waiting for transfers between devices  93.5 us (41%)
  matrix products  36.9 us (16%)
  local copies, waits for them, and re-layouts  32.6 us (14%)
  other arithmetic  20.1 us (9%)
  starting transfers between devices  16.7 us (7%)
  Pallas kernels  15.3 us (7%)
  between operations  14.3 us (6%)
    all_to_all x1, waiting for transfers between devices, body(): lax.all_to_all(back, 'ep', split_axis=0, concat_axis=0, tiled=True)  37.6 us
    unnamed x2, waiting for transfers between devices  25.6 us
    all_to_all x1, waiting for transfers between devices, body(): lax.all_to_all(grad_disp, 'ep', split_axis=0, concat_axis=0, tiled=True)  16.8 us
    pallas_call x1, Pallas kernels, packed_weight_grads(): pl.pallas_call(_pack_kernel, grid=(n_rep // group,), in_specs=[pl.BlockSp...  15.3 us
    all_to_all x1, waiting for transfers between devices, body(): lax.all_to_all(tok_disp, 'ep', split_axis=0, concat_axis=0, tiled=True)  13.5 us
    dot_general x1, matrix products, body(): up_pre = jnp.dot(rows_in, up_mat, preferred_element_type=jnp.float32)  7.33 us
    dot_general x1, matrix products, body(): lax.dot_general(out_grads, down_mat, contract, preferred_element_type=jnp...  7.11 us
    all_to_all x1, starting transfers between devices, body(): lax.all_to_all(grad_disp, 'ep', split_axis=0, concat_axis=0, tiled=True)  6.93 us
  transfers between devices with their start and end apart: 4, of which 4 were waited for; matrix products, arithmetic and copies ran while one was open for 23% of the time, Pallas kernels for 0%

profile of v6, /device:TPU:1, one launch (start us, length us, event | category | flops | bytes accessed | tf_op | source)
XLA Modules:
  0.0 229.4 jit_solution(1859047802518250375)
XLA Ops:
  7.2 0.0 copy-start
  7.2 0.8 copy.26
  8.0 0.1 eq.29
  8.2 0.1 eq.25
  8.3 0.7 broadcast_multiply_fusion.1
  9.0 0.6 reduce-window.6
  9.6 0.2 slice_reduce_fusion
  9.8 0.1 copy.25
  9.9 0.1 mul.77
  10.1 0.1 fusion.23
  10.2 1.4 scatter_custom_fusion
  11.6 0.8 copy.24
  12.4 0.1 reshape.172
  12.5 2.8 %gather_fusion.1 = f32[384]{0:T(512)S(1)} fusion(f32[256]{0:T(256)S(1)} %reshape.172, s32[1024]{0:T(1024)S(1)} %get-tuple-element.13), kind=kCustom, calls=%fused_computation.1 | custom fusion | bytes 4608 | tf_op jit(solution)/shard_map/gather | solution.py:122
  15.4 2.2 scatter_custom_fusion.1
  17.6 0.1 mul.85
  17.6 0.0 copy-done
  17.6 2.5 %gather_fusion.2 = bf16[384,2048]{1,0:T(8,128)(2,1)S(1)} fusion(bf16[128,2048]{1,0:T(8,128)(2,1)S(1)} %copy-done, s32[1024]{0:T(1024)S(1)} %get-tuple-element.14), kind=kCustom, calls=%fused_computation.2 | custom fusion | bytes 3147264 | tf_op jit(solution)/shard_map/gather | solution.py:123
  20.1 1.5 fusion.12
  21.6 6.9 %all-to-all-start.1 = ((bf16[8,48,2048]{2,1,0:T(8,128)(2,1)}), bf16[8,48,2048]{2,1,0:T(8,128)(2,1)}, u32[]{:S(2)}, u32[]{:S(2)}) async-start(bf16[8,48,2048]{2,1,0:T(8,128)(2,1)} %fusion.12), calls=%async_computation.1 | async-start | bytes 3145728 | tf_op jit(solution)/shard_map/all_to_all | solution.py:130
  28.5 0.1 mul.79
  28.6 2.5 %gather_fusion = bf16[384,2048]{1,0:T(8,128)(2,1)S(1)} fusion(bf16[128,2048]{1,0:T(8,128)(2,1)S(1)} %copy-done.1, s32[1024]{0:T(1024)S(1)} %get-tuple-element.14), kind=kCustom, calls=%fused_computation | custom fusion | bytes 3147264 | tf_op jit(solution)/shard_map/gather | solution.py:125
  31.1 1.3 broadcast_multiply_fusion
  32.4 16.8 %all-to-all-done.1 = bf16[8,48,2048]{2,1,0:T(8,128)(2,1)} async-done(((bf16[8,48,2048]{2,1,0:T(8,128)(2,1)}), bf16[8,48,2048]{2,1,0:T(8,128)(2,1)}, u32[]{:S(2)}, u32[]{:S(2)}) %all-to-all-start.1) | async-done | bytes 1572896 | tf_op jit(solution)/shard_map/all_to_all | solution.py:130
  49.2 4.5 %all-to-all-start = ((bf16[8,48,2048]{2,1,0:T(8,128)(2,1)}), bf16[8,48,2048]{2,1,0:T(8,128)(2,1)S(1)}, u32[]{:S(2)}, u32[]{:S(2)}) async-start(bf16[8,48,2048]{2,1,0:T(8,128)(2,1)} %broadcast_multiply_fusion), calls=%async_computation | async-start | bytes 3145728 | tf_op jit(solution)/shard_map/all_to_all | solution.py:126
  53.7 7.1 %fusion = f32[384,1408]{1,0:T(8,128)} fusion(bf16[384,2048]{1,0:T(8,128)(2,1)} %bitcast.10.og_ref, bf16[1,1408,2048]{2,1,0:T(8,128)(2,1)} %param.12), kind=kOutput, calls=%fused_computation.6 | convolution fusion | flops 2214592512 | bytes 9502720 | tf_op jit(solution)/shard_map/dot_general | solution.py:141
  60.8 13.5 %all-to-all-done = bf16[8,48,2048]{2,1,0:T(8,128)(2,1)S(1)} async-done(((bf16[8,48,2048]{2,1,0:T(8,128)(2,1)}), bf16[8,48,2048]{2,1,0:T(8,128)(2,1)S(1)}, u32[]{:S(2)}, u32[]{:S(2)}) %all-to-all-start) | async-done | bytes 1572896 | tf_op jit(solution)/shard_map/all_to_all | solution.py:126
  74.3 5.9 %fusion.10 = f32[384,1408]{1,0:T(8,128)S(1)} fusion(bf16[384,2048]{1,0:T(8,128)(2,1)S(1)} %bitcast.74, bf16[1,2048,1408]{2,1,0:T(8,128)(2,1)} %param.10), kind=kOutput, calls=%fused_computation.16 | convolution fusion | flops 2214592512 | bytes 9502720 | tf_op jit(solution)/shard_map/dot_general | solution.py:136
  80.2 7.3 %multiply_convert_fusion.2 = (bf16[384,1408]{1,0:T(8,128)(2,1)}, bf16[384,1408]{1,0:T(8,128)(2,1)}, bf16[384,1408]{1,0:T(8,128)(2,1)}) fusion(f32[384,1408]{1,0:T(8,128)S(1)} %fusion.10, f32[384,1408]{1,0:T(8,128)S(1)} %copy-done.8, bf16[384,2048]{1,0:T(8,128)(2,1)S(1)} %bitcast.75, bf16[1,2048,1408]{2,1,0:T(8,128)(2,1)} %param.11), kind=kOutput, calls=%fused_computation.25 | convolution fusion | flops 2222702592 | bytes 14909440 | tf_op jit(solution)/shard_map/dot_general | solution.py:137
  87.5 15.3 %shard_map.118 = bf16[16,264,2048]{2,1,0:T(8,128)(2,1)} custom-call(bf16[384,2048]{1,0:T(8,128)(2,1)} %bitcast.76, bf16[384,1408]{1,0:T(8,128)(2,1)} %get-tuple-element.7.gd_ref, bf16[384,1408]{1,0:T(8,128)(2,1)} %get-tuple-element.8.ud_ref, bf16[384,1408]{1,0:T(8,128)(2,1)} %get-tuple-element.6.h_ref, bf16[384,2048]{1,0:T(8,128)(2,1)} %bitcast.10.og_ref), custom_call_target="tpu_custom_call" | custom-call | flops 6643777536 | bytes 17301504 | tf_op jit(solution)/shard_map/pallas_call | solution.py:62
  102.8 0.0 reduce-scatter.4.cloned.1.call-update
  102.9 1.2 copy-done.7
  104.1 4.8 %fusion.4 = f32[384,2048]{1,0:T(8,128)S(1)} fusion(bf16[384,1408]{1,0:T(8,128)(2,1)S(1)} %copy-done.7, bf16[1,2048,1408]{2,1,0:T(8,128)(2,1)} %param.11), kind=kOutput, calls=%fused_computation.10 | convolution fusion | flops 2214592512 | bytes 9994240 | tf_op jit(solution)/shard_map/dot_general | solution.py:159
  108.9 0.0 copy-done.6
  108.9 0.0 slice-start.1
  108.9 0.0 copy-start.5
  108.9 5.5 %fusion.15 = bf16[384,2048]{1,0:T(8,128)(2,1)S(1)} fusion(bf16[384,1408]{1,0:T(8,128)(2,1)S(1)} %copy-done.6, bf16[1,1408,2048]{2,1,0:T(8,128)(2,1)} %param.12), kind=kOutput, calls=%fused_computation.22 | convolution fusion | flops 2215378944 | bytes 8421376 | tf_op jit(solution)/shard_map/dot_general | solution.py:156
  114.4 0.0 slice-done
  114.4 0.0 slice-done.1
  114.4 0.0 copy-done.5
  114.5 2.6 %add_convert_fusion = bf16[384,2048]{1,0:T(8,128)(2,1)S(1)} fusion(f32[384,2048]{1,0:T(8,128)S(1)} %fusion.4, bf16[384,1408]{1,0:T(8,128)(2,1)S(1)} %copy-done.5, bf16[1,2048,1408]{2,1,0:T(8,128)(2,1)S(1)} %bitcast.87), kind=kOutput, calls=%fused_computation.21 | convolution fusion | flops 2216165376 | bytes 11567104 | tf_op jit(solution)/shard_map/dot_general | solution.py:158
  117.1 2.0 pad_maximum_fusion
  119.1 5.3 %all-to-all-start.2 = ((bf16[8,48,4096]{2,1,0:T(8,128)(2,1)}), bf16[8,48,4096]{2,1,0:T(8,128)(2,1)}, u32[]{:S(2)}, u32[]{:S(2)}) async-start(bf16[8,48,4096]{2,1,0:T(8,128)(2,1)} %bitcast.71), calls=%async_computation.2 | async-start | bytes 6291456 | tf_op jit(solution)/shard_map/all_to_all | solution.py:164
  124.4 37.6 %all-to-all-done.2 = bf16[8,48,4096]{2,1,0:T(8,128)(2,1)} async-done(((bf16[8,48,4096]{2,1,0:T(8,128)(2,1)}), bf16[8,48,4096]{2,1,0:T(8,128)(2,1)}, u32[]{:S(2)}, u32[]{:S(2)}) %all-to-all-start.2) | async-done | bytes 3145760 | tf_op jit(solution)/shard_map/all_to_all | solution.py:164
  162.0 6.2 %gather_fusion.3 = bf16[256,4096]{1,0:T(8,128)(2,1)S(1)} fusion(bf16[384,4096]{1,0:T(8,128)(2,1)} %bitcast.12, s32[1024]{0:T(1024)S(1)} %pad_clamp_fusion), kind=kCustom, calls=%fused_computation.3 | custom fusion | bytes 4195328 | tf_op jit(solution)/shard_map/gather | solution.py:167
  168.2 1.6 convert_multiply_fusion.1
  169.7 3.5 %reshape.166 = f32[128,2,2048]{2,1,0:T(2,128)} reshape(f32[256,2048]{1,0:T(8,128)} %convert_multiply_fusion.1) | data formatting | bytes 4194304 | tf_op jit(solution)/shard_map/reshape | solution.py:171
  173.2 1.5 fusion.31
  174.7 1.8 reshape.167
  176.6 3.7 %reduce = bf16[128,2048]{1,0:T(8,128)(2,1)} reduce(bf16[128,2,2048]{2,1,0:T(2,128)(2,1)S(1)} %reshape.167, bf16[]{:T(256)} %constant.32.clone.1), dimensions={1}, to_apply=%region_6.7.clone | reduce | flops 262144 | bytes 1572866 | tf_op jit(solution)/shard_map/reduce_sum | solution.py:179
  180.3 0.0 copy-done.3
  180.3 1.5 reshape.169
  181.8 3.7 %fusion.19 = bf16[128,1,2]{2,1,0:T(2,128)(2,1)S(1)} fusion(bf16[128,2,2048]{2,1,0:T(2,128)(2,1)} %reshape.169, bf16[128,2048,1]{1,0,2:T(8,128)(2,1)S(1)} %bitcast.70), kind=kOutput, calls=%fused_computation.29 | convolution fusion | flops 1048576 | bytes 1573376 | tf_op jit(solution)/shard_map/tkd,td->tk/dot_general | solution.py:173
  185.5 0.6 copy.31
  186.1 3.9 %reduce_sum.31 = bf16[128,2048]{1,0:T(8,128)(2,1)} reduce(f32[128,2,2048]{2,1,0:T(2,128)S(1)} %copy-done.2, f32[]{:T(128)} %constant.36.clone.1), dimensions={1}, to_apply=%region_5.6 | reduce | flops 262144 | bytes 2621444 | tf_op jit(solution)/shard_map/reduce_sum | solution.py:170
  189.9 25.6 %reduce-scatter.4.cloned.1.call-done = bf16[1,264,2048]{2,1,0:T(8,128)(2,1)} async-done(((bf16[16,264,2048]{2,1,0:T(8,128)(2,1)}), bf16[1,264,2048]{2,1,0:T(8,128)(2,1)}) %reduce-scatter.4.cloned.1.call-update) | async-done | bytes 1081360
  215.6 0.9 slice_bitcast_fusion.1
  216.5 0.9 slice_bitcast_fusion.2
  217.4 1.9 fusion.21
  219.3 1.9 slice_convert_fusion
  221.3 0.1 copy.28
  221.4 0.1 copy.29
  221.4 0.2 concatenate.19
  221.7 0.9 maximum_convert_fusion
  (26 shorter events, 0.2 us)
Async XLA Ops:
  7.2 10.5 %copy-start = (bf16[128,2048]{1,0:T(8,128)(2,1)S(1)}, bf16[128,2048]{1,0:T(8,128)(2,1)}, u32[]{:S(2)}) copy-start(bf16[128,2048]{1,0:T(8,128)(2,1)} %param.13) | copy-start | bytes 1572868
  21.6 7.0 %copy-start.1 = (bf16[128,2048]{1,0:T(8,128)(2,1)S(1)}, bf16[128,2048]{1,0:T(8,128)(2,1)}, u32[]{:S(2)}) copy-start(bf16[128,2048]{1,0:T(8,128)(2,1)} %param.7) | copy-start | bytes 1572868
  21.6 27.6 %all-to-all-start.1 = ((bf16[8,48,2048]{2,1,0:T(8,128)(2,1)}), bf16[8,48,2048]{2,1,0:T(8,128)(2,1)}, u32[]{:S(2)}, u32[]{:S(2)}) async-start(bf16[8,48,2048]{2,1,0:T(8,128)(2,1)} %fusion.12), calls=%async_computation.1 | async-start | bytes 3145728 | tf_op jit(solution)/shard_map/all_to_all | solution.py:130
  49.2 25.1 %all-to-all-start = ((bf16[8,48,2048]{2,1,0:T(8,128)(2,1)}), bf16[8,48,2048]{2,1,0:T(8,128)(2,1)S(1)}, u32[]{:S(2)}, u32[]{:S(2)}) async-start(bf16[8,48,2048]{2,1,0:T(8,128)(2,1)} %broadcast_multiply_fusion), calls=%async_computation | async-start | bytes 3145728 | tf_op jit(solution)/shard_map/all_to_all | solution.py:126
  53.7 161.9 %reduce-scatter.4.cloned.1.call-start = ((), (), s32[]{:S(2)}) async-start(), calls=%async_computation.4 | async-start | bytes 18382848
  74.3 5.9 %copy-start.4 = (bf16[8,48,2048]{2,1,0:T(8,128)(2,1)}, bf16[8,48,2048]{2,1,0:T(8,128)(2,1)S(1)}, u32[]{:S(2)}) copy-start(bf16[8,48,2048]{2,1,0:T(8,128)(2,1)S(1)} %all-to-all-done) | copy-start | bytes 4718596
  74.3 5.9 %copy-start.8 = (f32[384,1408]{1,0:T(8,128)S(1)}, f32[384,1408]{1,0:T(8,128)}, u32[]{:S(2)}) copy-start(f32[384,1408]{1,0:T(8,128)} %fusion) | copy-start | bytes 6488068
  102.8 1.2 copy-start.7
  104.1 4.8 %copy-start.6 = (bf16[384,1408]{1,0:T(8,128)(2,1)S(1)}, bf16[384,1408]{1,0:T(8,128)(2,1)}, u32[]{:S(2)}) copy-start(bf16[384,1408]{1,0:T(8,128)(2,1)} %get-tuple-element.6.h_ref) | copy-start | bytes 3244036
  104.1 10.3 %slice-start = ((s8[5767168]{0:T(1024)(128)(4,1)}), s8[4194304]{0:T(1024)(128)(4,1)S(1)}, s32[]{:S(2)}) async-start(s8[5767168]{0:T(1024)(128)(4,1)} %bitcast.86), calls=%async_computation.5 | async-start | bytes 8388608
  108.9 5.5 %slice-start.1 = ((s8[5767168]{0:T(1024)(128)(4,1)}), s8[1572864]{0:T(1024)(128)(4,1)S(1)}, s32[]{:S(2)}) async-start(s8[5767168]{0:T(1024)(128)(4,1)} %bitcast.86), calls=%async_computation.6 | async-start | bytes 3145728
  108.9 5.5 %copy-start.5 = (bf16[384,1408]{1,0:T(8,128)(2,1)S(1)}, bf16[384,1408]{1,0:T(8,128)(2,1)}, u32[]{:S(2)}) copy-start(bf16[384,1408]{1,0:T(8,128)(2,1)} %get-tuple-element.7.gd_ref) | copy-start | bytes 3244036
  119.1 42.9 %all-to-all-start.2 = ((bf16[8,48,4096]{2,1,0:T(8,128)(2,1)}), bf16[8,48,4096]{2,1,0:T(8,128)(2,1)}, u32[]{:S(2)}, u32[]{:S(2)}) async-start(bf16[8,48,4096]{2,1,0:T(8,128)(2,1)} %bitcast.71), calls=%async_computation.2 | async-start | bytes 6291456 | tf_op jit(solution)/shard_map/all_to_all | solution.py:164
  174.7 5.6 %copy-start.3 = (bf16[256,2048]{1,0:T(8,128)(2,1)S(1)}, bf16[256,2048]{1,0:T(8,128)(2,1)}, u32[]{:S(2)}) copy-start(bf16[256,2048]{1,0:T(8,128)(2,1)} %get-tuple-element.9) | copy-start | bytes 3145732
  181.8 4.3 %copy-start.2 = (f32[128,2,2048]{2,1,0:T(2,128)S(1)}, f32[128,2,2048]{2,1,0:T(2,128)}, u32[]{:S(2)}) copy-start(f32[128,2,2048]{2,1,0:T(2,128)} %reshape.166) | copy-start | bytes 6291460
Sparse Core Ops, SparseCore 0:
  103.0 112.5 reduce-scatter.3

commit v7 on v5

--- a/solution.py
+++ b/solution.py
@@ -113,17 +113,21 @@
     )
     slot_rank = jnp.sum((jnp.cumsum(onehot, axis=0) - onehot) * onehot, axis=1)
     slot_index = flat_exp * capacity + slot_rank
-    source = jnp.zeros((slots,), jnp.int32).at[slot_index].set(
-        jnp.arange(pair_count, dtype=jnp.int32)
-    )
-    filled = jnp.zeros((slots,), jnp.bfloat16).at[slot_index].set(1.0)
-    token_src = source // top_count
+    hit = (
+        slot_index.reshape(tok_rows, top_count, 1)
+        == jnp.arange(slots, dtype=jnp.int32)[None, None, :]
+    )
+    select = jnp.sum(hit, axis=1).astype(jnp.bfloat16)
+    gate_select = jnp.sum(jnp.where(hit, gates[:, :, None], 0), axis=1).astype(jnp.bfloat16)
+    rows_first = (((0,), (0,)), ((), ()))
+    tok_rows_out = lax.dot_general(select, tokens, rows_first, preferred_element_type=jnp.float32)
+    scaled_rows = lax.dot_general(
+        gate_select, cotangent, rows_first, preferred_element_type=jnp.float32
+    )
     weights = gates.reshape(pair_count, 1).astype(jnp.float32)
-    slot_weight = weights[source] * filled[:, None].astype(jnp.float32)
-    scaled_rows = (slot_weight * cotangent[token_src].astype(jnp.float32)).astype(jnp.bfloat16)
 
     disp = jnp.concatenate(
-        [tokens[token_src] * filled[:, None], scaled_rows], axis=1
+        [tok_rows_out.astype(jnp.bfloat16), scaled_rows.astype(jnp.bfloat16)], axis=1
     ).reshape(n_experts, capacity, 2 * model_width)
     recv = lax.all_to_all(disp, "ep", split_axis=0, concat_axis=0, tiled=True).reshape(
         slots, 2 * model_width
@@ -132,7 +136,6 @@
     out_grads = recv[:, model_width:]
 
     contract = (((1,), (1,)), ((), ()))
-    rows_first = (((0,), (0,)), ((), ()))
     gate_pre = jnp.dot(rows_in, gate_mat, preferred_element_type=jnp.float32)
     up_pre = jnp.dot(rows_in, up_mat, preferred_element_type=jnp.float32)
     sigmoid_g = jax.nn.sigmoid(gate_pre)

time: 222 us -> 210 us (0.946)
  local copies, waits for them, and re-layouts: 34.4 us -> 21.4 us
    gather x3 -> x0, local copies, waits for them, and re-layouts: 8.4 us -> none  [the longest x1 3.14 us: body(): tokens[token_src] * filled[:, None]]
    scatter x2 -> x0, local copies, waits for them, and re-layouts: 3.56 us -> none  [the longest x1 2.16 us: body(): filled = jnp.zeros((slots,), jnp.bfloat16).at[slot_index].set(1.0)]
    dot_general x0 -> x2, matrix products: none -> 2.23 us  [the longest x1 1.64 us: body(): lax.dot_general(select, tokens, rows_first, preferred_element_type=jnp.fl...]
  transfers between devices with their start and end apart: 2 -> 2, of which waited for: 2 -> 2; matrix products, arithmetic and copies ran while one was open for 19% -> 22% of each run, Pallas kernels for 0% -> 0%
where the time goes in v7:
time: 210 us; the launch traced here: 209 us
  waiting for transfers between devices  60.8 us (29%)
  blocking collectives  44.3 us (21%)
  matrix products  28.8 us (14%)
  local copies, waits for them, and re-layouts  21.4 us (10%)
  other arithmetic  18.4 us (9%)
  Pallas kernels  15.3 us (7%)
  between operations  14.4 us (7%)
  starting transfers between devices  5.62 us (3%)
    all_to_all x1, blocking collectives, body(): lax.all_to_all(disp, 'ep', split_axis=0, concat_axis=0, tiled=True)  44.3 us
    all_to_all x1, waiting for transfers between devices, body(): lax.all_to_all(back, 'ep', split_axis=0, concat_axis=0, tiled=True)  37.1 us
    unnamed x2, waiting for transfers between devices  23.7 us
    pallas_call x1, Pallas kernels, packed_weight_grads(): pl.pallas_call(_pack_kernel, grid=(n_rep // group,), in_specs=[pl.BlockSp...  15.3 us
    gather x1, local copies, waits for them, and re-layouts, body(): pair_back = returned[slot_index]  6.18 us
    all_to_all x1, starting transfers between devices, body(): lax.all_to_all(back, 'ep', split_axis=0, concat_axis=0, tiled=True)  5.58 us
    dot_general x1, matrix products, body(): jnp.dot(hidden, down_mat, preferred_element_type=jnp.float32)  5.48 us
    dot_general x1, matrix products, body(): lax.dot_general(up_delta, up_mat, contract, preferred_element_type=jnp.fl...  5 us
  transfers between devices with their start and end apart: 2, of which 2 were waited for; matrix products, arithmetic and copies ran while one was open for 22% of the time, Pallas kernels for 0%

profile of v7, /device:TPU:1, one launch (start us, length us, event | category | flops | bytes accessed | tf_op | source)
XLA Modules:
  0.0 209.1 jit_solution(4343630967447838921)
XLA Ops:
  7.2 0.0 copy-start
  7.2 0.0 reduce-scatter.4.cloned.1.call-start
  7.2 0.8 copy.36
  8.1 0.1 eq.42
  8.2 0.1 eq.38
  8.4 0.6 reduce-window.6
  8.9 0.2 slice_reduce_fusion
  9.2 0.1 fusion.28
  9.3 0.1 reduce_sum.53
  9.5 0.1 copy.39
  9.5 0.1 convert_reduce_fusion
  9.7 0.8 fusion.25
  10.5 1.6 convolution_convert_fusion.1
  12.1 0.0 copy-done
  12.1 0.0 slice-start.2
  12.1 0.6 convolution_convert_fusion
  12.7 0.0 slice-start.3
  12.7 0.2 pad_maximum_fusion
  12.9 0.0 slice-start.4
  13.0 44.3 %all_to_all.10 = bf16[8,48,4096]{2,1,0:T(8,128)(2,1)S(1)} all-to-all(bf16[8,48,4096]{2,1,0:T(8,128)(2,1)S(1)} %bitcast.74), channel_id=1, replica_groups=mesh['rep'=16,'ep'=8] {'ep'}, dimensions={0} | all-to-all | bytes 6291456 | tf_op jit(solution)/shard_map/all_to_all | solution.py:132
  57.2 0.0 slice-done.2
  57.2 0.0 slice-done.3
  57.2 0.0 slice-start.5
  57.3 0.0 slice-start
  57.3 2.6 %fusion = f32[384,1408]{1,0:T(8,128)S(1)} fusion(bf16[1,1408,2048]{2,1,0:T(8,128)(2,1)S(1)} %bitcast.85, bf16[384,4096]{1,0:T(8,128)(2,1)S(1)} %bitcast.68), kind=kOutput, calls=%fused_computation.1 | convolution fusion | flops 2214592512 | bytes 9502720 | tf_op jit(solution)/shard_map/dot_general | solution.py:144
  59.9 0.0 slice-done.4
  59.9 0.0 slice-done.5
  59.9 0.0 slice-start.1
  60.0 2.6 %fusion.10 = f32[384,1408]{1,0:T(8,128)S(1)} fusion(bf16[1,2048,1408]{2,1,0:T(8,128)(2,1)S(1)} %bitcast.87, bf16[384,4096]{1,0:T(8,128)(2,1)S(1)} %bitcast.69), kind=kOutput, calls=%fused_computation.11 | convolution fusion | flops 2214592512 | bytes 9502720 | tf_op jit(solution)/shard_map/dot_general | solution.py:139
  62.6 0.0 copy-done.1
  62.6 0.0 slice-done
  62.6 4.6 %multiply_convert_fusion.2 = (bf16[384,1408]{1,0:T(8,128)(2,1)}, bf16[384,1408]{1,0:T(8,128)(2,1)}, bf16[384,1408]{1,0:T(8,128)(2,1)}) fusion(f32[384,1408]{1,0:T(8,128)S(1)} %fusion.10, f32[384,1408]{1,0:T(8,128)S(1)} %fusion, bf16[1,2048,1408]{2,1,0:T(8,128)(2,1)S(1)} %bitcast.83, bf16[384,4096]{1,0:T(8,128)(2,1)S(1)} %bitcast.70), kind=kOutput, calls=%fused_computation.21 | convolution fusion | flops 2222702592 | bytes 14909440 | tf_op jit(solution)/shard_map/dot_general | solution.py:140
  67.1 15.3 %shard_map.118 = bf16[16,264,2048]{2,1,0:T(8,128)(2,1)} custom-call(bf16[384,4096]{1,0:T(8,128)(2,1)} %bitcast.71, bf16[384,1408]{1,0:T(8,128)(2,1)} %get-tuple-element.7.gd_ref, bf16[384,1408]{1,0:T(8,128)(2,1)} %get-tuple-element.8.ud_ref, bf16[384,1408]{1,0:T(8,128)(2,1)} %get-tuple-element.6.h_ref, bf16[384,4096]{1,0:T(8,128)(2,1)} %bitcast.72), custom_call_target="tpu_custom_call" | custom-call | flops 6643777536 | bytes 17301504 | tf_op jit(solution)/shard_map/pallas_call | solution.py:62
  82.5 0.0 reduce-scatter.4.cloned.1.call-update
  82.5 1.2 copy-done.6
  83.7 5.0 %fusion.4 = f32[384,2048]{1,0:T(8,128)S(1)} fusion(bf16[384,1408]{1,0:T(8,128)(2,1)S(1)} %copy-done.6, bf16[1,2048,1408]{2,1,0:T(8,128)(2,1)} %param.11), kind=kOutput, calls=%fused_computation.5 | convolution fusion | flops 2214592512 | bytes 9994240 | tf_op jit(solution)/shard_map/dot_general | solution.py:162
  88.7 0.0 slice-start.7
  88.7 5.5 %fusion.14 = bf16[384,2048]{1,0:T(8,128)(2,1)S(1)} fusion(bf16[384,1408]{1,0:T(8,128)(2,1)S(1)} %copy-done.5, bf16[1,1408,2048]{2,1,0:T(8,128)(2,1)} %param.12), kind=kOutput, calls=%fused_computation.16 | convolution fusion | flops 2215378944 | bytes 8421376 | tf_op jit(solution)/shard_map/dot_general | solution.py:159
  94.3 2.6 %add_convert_fusion = bf16[384,2048]{1,0:T(8,128)(2,1)S(1)} fusion(f32[384,2048]{1,0:T(8,128)S(1)} %fusion.4, bf16[384,1408]{1,0:T(8,128)(2,1)S(1)} %copy-done.4, bf16[1,2048,1408]{2,1,0:T(8,128)(2,1)S(1)} %bitcast.89), kind=kOutput, calls=%fused_computation.15 | convolution fusion | flops 2216165376 | bytes 11567104 | tf_op jit(solution)/shard_map/dot_general | solution.py:161
  96.9 2.0 pad_maximum_fusion.1
  98.9 5.6 %all-to-all-start.1 = ((bf16[8,48,4096]{2,1,0:T(8,128)(2,1)}), bf16[8,48,4096]{2,1,0:T(8,128)(2,1)}, u32[]{:S(2)}, u32[]{:S(2)}) async-start(bf16[8,48,4096]{2,1,0:T(8,128)(2,1)} %bitcast.73), calls=%async_computation.1 | async-start | bytes 6291456 | tf_op jit(solution)/shard_map/all_to_all | solution.py:167
  104.5 0.1 copy.35
  104.6 0.1 mul.61
  104.7 0.1 reshape.151
  104.9 37.1 %all-to-all-done.1 = bf16[8,48,4096]{2,1,0:T(8,128)(2,1)} async-done(((bf16[8,48,4096]{2,1,0:T(8,128)(2,1)}), bf16[8,48,4096]{2,1,0:T(8,128)(2,1)}, u32[]{:S(2)}, u32[]{:S(2)}) %all-to-all-start.1) | async-done | bytes 3145760 | tf_op jit(solution)/shard_map/all_to_all | solution.py:167
  142.1 6.2 %gather_fusion = bf16[256,4096]{1,0:T(8,128)(2,1)S(1)} fusion(bf16[384,4096]{1,0:T(8,128)(2,1)} %bitcast.8, s32[1024]{0:T(1024)S(1)} %pad_clamp_fusion), kind=kCustom, calls=%fused_computation | custom fusion | bytes 4195328 | tf_op jit(solution)/shard_map/gather | solution.py:170
  148.2 1.5 convert_multiply_fusion
  149.8 3.5 %reshape.145 = f32[128,2,2048]{2,1,0:T(2,128)} reshape(f32[256,2048]{1,0:T(8,128)} %convert_multiply_fusion) | data formatting | bytes 4194304 | tf_op jit(solution)/shard_map/reshape | solution.py:174
  153.3 1.5 fusion.31
  154.8 2.6 %reshape.146 = bf16[128,2,2048]{2,1,0:T(2,128)(2,1)} reshape(bf16[256,2048]{1,0:T(8,128)(2,1)} %get-tuple-element.10) | data formatting | bytes 2097152 | tf_op jit(solution)/shard_map/reshape | solution.py:183
  157.4 1.5 reshape.148
  158.9 3.7 %fusion.21 = bf16[128,1,2]{2,1,0:T(2,128)(2,1)S(1)} fusion(bf16[128,2,2048]{2,1,0:T(2,128)(2,1)} %reshape.148, bf16[128,2048,1]{1,0,2:T(8,128)(2,1)S(1)} %bitcast.67), kind=kOutput, calls=%fused_computation.28 | convolution fusion | flops 1048576 | bytes 1573376 | tf_op jit(solution)/shard_map/tkd,td->tk/dot_general | solution.py:176
  162.6 0.6 copy.43
  163.2 3.8 %reduce_sum.57 = bf16[128,2048]{1,0:T(8,128)(2,1)} reduce(f32[128,2,2048]{2,1,0:T(2,128)S(1)} %copy-done.2, f32[]{:T(128)} %constant.17.clone.1), dimensions={1}, to_apply=%region_5.6 | reduce | flops 262144 | bytes 2621444 | tf_op jit(solution)/shard_map/reduce_sum | solution.py:173
  167.0 4.6 %reduce.1 = bf16[128,2048]{1,0:T(8,128)(2,1)} reduce(bf16[128,2,2048]{2,1,0:T(2,128)(2,1)} %reshape.146, bf16[]{:T(256)} %constant.14.clone.1), dimensions={1}, to_apply=%region_6.7.clone | reduce | flops 262144 | bytes 1572866 | tf_op jit(solution)/shard_map/reduce_sum | solution.py:182
  171.6 23.6 %reduce-scatter.4.cloned.1.call-done = bf16[1,264,2048]{2,1,0:T(8,128)(2,1)} async-done(((bf16[16,264,2048]{2,1,0:T(8,128)(2,1)}), bf16[1,264,2048]{2,1,0:T(8,128)(2,1)}) %reduce-scatter.4.cloned.1.call-update) | async-done | bytes 1081360
  195.2 0.9 slice_bitcast_fusion.1
  196.2 0.9 slice_bitcast_fusion.2
  197.1 1.9 fusion.24
  199.0 1.9 slice_convert_fusion
  201.0 0.1 copy.40
  201.0 0.1 copy.41
  201.1 0.2 concatenate.23
  201.3 0.9 maximum_convert_fusion
  (28 shorter events, 0.1 us)
Async XLA Ops:
  7.2 4.9 %copy-start = (bf16[128,2048]{1,0:T(8,128)(2,1)S(1)}, bf16[128,2048]{1,0:T(8,128)(2,1)}, u32[]{:S(2)}) copy-start(bf16[128,2048]{1,0:T(8,128)(2,1)} %param.13) | copy-start | bytes 1572868
  7.2 188.0 %reduce-scatter.4.cloned.1.call-start = ((), (), s32[]{:S(2)}) async-start(), calls=%async_computation.3 | async-start | bytes 18382848
  12.1 45.1 %slice-start.2 = ((s8[5767168]{0:T(1024)(128)(4,1)}), s8[4194304]{0:T(1024)(128)(4,1)S(1)}, s32[]{:S(2)}) async-start(s8[5767168]{0:T(1024)(128)(4,1)} %bitcast.84), calls=%async_computation.6 | async-start | bytes 8388608
  12.7 44.5 %slice-start.3 = ((s8[5767168]{0:T(1024)(128)(4,1)}), s8[1572864]{0:T(1024)(128)(4,1)S(1)}, s32[]{:S(2)}) async-start(s8[5767168]{0:T(1024)(128)(4,1)} %bitcast.84), calls=%async_computation.7 | async-start | bytes 3145728
  12.9 47.0 %slice-start.4 = ((s8[5767168]{0:T(1024)(128)(4,1)}), s8[4194304]{0:T(1024)(128)(4,1)S(1)}, s32[]{:S(2)}) async-start(s8[5767168]{0:T(1024)(128)(4,1)} %bitcast.86), calls=%async_computation.8 | async-start | bytes 8388608
  57.2 5.3 %copy-start.1 = (bf16[8,48,4096]{2,1,0:T(8,128)(2,1)}, bf16[8,48,4096]{2,1,0:T(8,128)(2,1)S(1)}, u32[]{:S(2)}) copy-start(bf16[8,48,4096]{2,1,0:T(8,128)(2,1)S(1)} %all_to_all.10) | copy-start | bytes 9437188
  57.2 2.7 %slice-start.5 = ((s8[5767168]{0:T(1024)(128)(4,1)}), s8[1572864]{0:T(1024)(128)(4,1)S(1)}, s32[]{:S(2)}) async-start(s8[5767168]{0:T(1024)(128)(4,1)} %bitcast.86), calls=%async_computation.9 | async-start | bytes 3145728
  57.3 5.3 %slice-start = ((s8[5767168]{0:T(1024)(128)(4,1)}), s8[4194304]{0:T(1024)(128)(4,1)S(1)}, s32[]{:S(2)}) async-start(s8[5767168]{0:T(1024)(128)(4,1)} %bitcast.82), calls=%async_computation.4 | async-start | bytes 8388608
  59.9 2.6 %slice-start.1 = ((s8[5767168]{0:T(1024)(128)(4,1)}), s8[1572864]{0:T(1024)(128)(4,1)S(1)}, s32[]{:S(2)}) async-start(s8[5767168]{0:T(1024)(128)(4,1)} %bitcast.82), calls=%async_computation.5 | async-start | bytes 3145728
  82.4 1.2 copy-start.6
  83.7 5.0 %copy-start.5 = (bf16[384,1408]{1,0:T(8,128)(2,1)S(1)}, bf16[384,1408]{1,0:T(8,128)(2,1)}, u32[]{:S(2)}) copy-start(bf16[384,1408]{1,0:T(8,128)(2,1)} %get-tuple-element.6.h_ref) | copy-start | bytes 3244036
  83.7 10.5 %slice-start.6 = ((s8[5767168]{0:T(1024)(128)(4,1)}), s8[4194304]{0:T(1024)(128)(4,1)S(1)}, s32[]{:S(2)}) async-start(s8[5767168]{0:T(1024)(128)(4,1)} %bitcast.88), calls=%async_computation.10 | async-start | bytes 8388608
  88.7 5.5 %copy-start.4 = (bf16[384,1408]{1,0:T(8,128)(2,1)S(1)}, bf16[384,1408]{1,0:T(8,128)(2,1)}, u32[]{:S(2)}) copy-start(bf16[384,1408]{1,0:T(8,128)(2,1)} %get-tuple-element.7.gd_ref) | copy-start | bytes 3244036
  88.7 5.5 %slice-start.7 = ((s8[5767168]{0:T(1024)(128)(4,1)}), s8[1572864]{0:T(1024)(128)(4,1)S(1)}, s32[]{:S(2)}) async-start(s8[5767168]{0:T(1024)(128)(4,1)} %bitcast.88), calls=%async_computation.11 | async-start | bytes 3145728
  98.9 5.6 %copy-start.7 = (bf16[128,2]{0,1:T(2,128)(2,1)S(1)}, bf16[128,2]{0,1:T(2,128)(2,1)}, u32[]{:S(2)}) copy-start(bf16[128,2]{0,1:T(2,128)(2,1)} %param.9) | copy-start | bytes 1540
  98.9 43.2 %all-to-all-start.1 = ((bf16[8,48,4096]{2,1,0:T(8,128)(2,1)}), bf16[8,48,4096]{2,1,0:T(8,128)(2,1)}, u32[]{:S(2)}, u32[]{:S(2)}) async-start(bf16[8,48,4096]{2,1,0:T(8,128)(2,1)} %bitcast.73), calls=%async_computation.1 | async-start | bytes 6291456 | tf_op jit(solution)/shard_map/all_to_all | solution.py:167
  154.8 2.6 %copy-start.3 = (bf16[256,2048]{1,0:T(8,128)(2,1)S(1)}, bf16[256,2048]{1,0:T(8,128)(2,1)}, u32[]{:S(2)}) copy-start(bf16[256,2048]{1,0:T(8,128)(2,1)} %get-tuple-element.9) | copy-start | bytes 3145732
  158.9 4.3 %copy-start.2 = (f32[128,2,2048]{2,1,0:T(2,128)S(1)}, f32[128,2,2048]{2,1,0:T(2,128)}, u32[]{:S(2)}) copy-start(f32[128,2,2048]{2,1,0:T(2,128)} %reshape.145) | copy-start | bytes 6291460
Sparse Core Ops, SparseCore 0:
  82.6 112.5 reduce-scatter.3

commit v8 on v7

--- a/solution.py
+++ b/solution.py
@@ -47,7 +47,7 @@
         o_ref[c, rows + extra :, :] = down_ref[pl.ds(start, down_rows), :].astype(o_ref.dtype)
 
 
-GROUP = 4
+GROUP = 8
 
 
 def packed_weight_grads(recv, gate_delta, up_delta, hidden, n_rep):

time: 210 us -> 211 us (level)
  transfers between devices with their start and end apart: 2 -> 2, of which waited for: 2 -> 2; matrix products, arithmetic and copies ran while one was open for 22% -> 21% of each run, Pallas kernels for 0% -> 0%
where the time goes in v8:
time: 211 us; the launch traced here: 210 us
  waiting for transfers between devices  60.8 us (29%)
  blocking collectives  44.3 us (21%)
  matrix products  28.8 us (14%)
  local copies, waits for them, and re-layouts  21.4 us (10%)
  other arithmetic  18.4 us (9%)
  Pallas kernels  16.3 us (8%)
  between operations  14.4 us (7%)
  starting transfers between devices  5.62 us (3%)
    all_to_all x1, blocking collectives, body(): lax.all_to_all(disp, 'ep', split_axis=0, concat_axis=0, tiled=True)  44.3 us
    all_to_all x1, waiting for transfers between devices, body(): lax.all_to_all(back, 'ep', split_axis=0, concat_axis=0, tiled=True)  37.1 us
    unnamed x2, waiting for transfers between devices  23.7 us
    pallas_call x1, Pallas kernels, packed_weight_grads(): pl.pallas_call(_pack_kernel, grid=(n_rep // group,), in_specs=[pl.BlockSp...  16.3 us
    gather x1, local copies, waits for them, and re-layouts, body(): pair_back = returned[slot_index]  6.18 us
    all_to_all x1, starting transfers between devices, body(): lax.all_to_all(back, 'ep', split_axis=0, concat_axis=0, tiled=True)  5.58 us
    dot_general x1, matrix products, body(): jnp.dot(hidden, down_mat, preferred_element_type=jnp.float32)  5.48 us
    dot_general x1, matrix products, body(): lax.dot_general(up_delta, up_mat, contract, preferred_element_type=jnp.fl...  5 us
  transfers between devices with their start and end apart: 2, of which 2 were waited for; matrix products, arithmetic and copies ran while one was open for 21% of the time, Pallas kernels for 0%

profile of v8, /device:TPU:1, one launch (start us, length us, event | category | flops | bytes accessed | tf_op | source)
XLA Modules:
  0.0 210.1 jit_solution(8168135907859767937)
XLA Ops:
  7.2 0.0 copy-start
  7.2 0.0 reduce-scatter.4.cloned.1.call-start
  7.2 0.8 copy.36
  8.1 0.1 eq.42
  8.2 0.1 eq.38
  8.4 0.6 reduce-window.6
  8.9 0.2 slice_reduce_fusion
  9.2 0.1 fusion.28
  9.3 0.1 reduce_sum.53
  9.5 0.1 copy.39
  9.5 0.1 convert_reduce_fusion
  9.7 0.8 fusion.25
  10.5 1.6 convolution_convert_fusion.1
  12.1 0.0 copy-done
  12.1 0.0 slice-start.2
  12.1 0.6 convolution_convert_fusion
  12.7 0.0 slice-start.3
  12.7 0.2 pad_maximum_fusion
  12.9 0.0 slice-start.4
  13.0 44.3 %all_to_all.10 = bf16[8,48,4096]{2,1,0:T(8,128)(2,1)S(1)} all-to-all(bf16[8,48,4096]{2,1,0:T(8,128)(2,1)S(1)} %bitcast.74), channel_id=1, replica_groups=mesh['rep'=16,'ep'=8] {'ep'}, dimensions={0} | all-to-all | bytes 6291456 | tf_op jit(solution)/shard_map/all_to_all | solution.py:132
  57.2 0.0 slice-done.2
  57.2 0.0 slice-done.3
  57.2 0.0 slice-start.5
  57.3 0.0 slice-start
  57.3 2.6 %fusion = f32[384,1408]{1,0:T(8,128)S(1)} fusion(bf16[1,1408,2048]{2,1,0:T(8,128)(2,1)S(1)} %bitcast.85, bf16[384,4096]{1,0:T(8,128)(2,1)S(1)} %bitcast.68), kind=kOutput, calls=%fused_computation.1 | convolution fusion | flops 2214592512 | bytes 9502720 | tf_op jit(solution)/shard_map/dot_general | solution.py:144
  59.9 0.0 slice-done.4
  59.9 0.0 slice-done.5
  59.9 0.0 slice-start.1
  60.0 2.6 %fusion.10 = f32[384,1408]{1,0:T(8,128)S(1)} fusion(bf16[1,2048,1408]{2,1,0:T(8,128)(2,1)S(1)} %bitcast.87, bf16[384,4096]{1,0:T(8,128)(2,1)S(1)} %bitcast.69), kind=kOutput, calls=%fused_computation.11 | convolution fusion | flops 2214592512 | bytes 9502720 | tf_op jit(solution)/shard_map/dot_general | solution.py:139
  62.6 0.0 copy-done.1
  62.6 4.6 %multiply_convert_fusion.2 = (bf16[384,1408]{1,0:T(8,128)(2,1)}, bf16[384,1408]{1,0:T(8,128)(2,1)}, bf16[384,1408]{1,0:T(8,128)(2,1)}) fusion(f32[384,1408]{1,0:T(8,128)S(1)} %fusion.10, f32[384,1408]{1,0:T(8,128)S(1)} %fusion, bf16[1,2048,1408]{2,1,0:T(8,128)(2,1)S(1)} %bitcast.83, bf16[384,4096]{1,0:T(8,128)(2,1)S(1)} %bitcast.70), kind=kOutput, calls=%fused_computation.21 | convolution fusion | flops 2222702592 | bytes 14909440 | tf_op jit(solution)/shard_map/dot_general | solution.py:140
  67.1 16.3 %shard_map.118 = bf16[16,264,2048]{2,1,0:T(8,128)(2,1)} custom-call(bf16[384,4096]{1,0:T(8,128)(2,1)} %bitcast.71, bf16[384,1408]{1,0:T(8,128)(2,1)} %get-tuple-element.7.gd_ref, bf16[384,1408]{1,0:T(8,128)(2,1)} %get-tuple-element.8.ud_ref, bf16[384,1408]{1,0:T(8,128)(2,1)} %get-tuple-element.6.h_ref, bf16[384,4096]{1,0:T(8,128)(2,1)} %bitcast.72), custom_call_target="tpu_custom_call" | custom-call | flops 6643777536 | bytes 17301504 | tf_op jit(solution)/shard_map/pallas_call | solution.py:62
  83.5 0.0 reduce-scatter.4.cloned.1.call-update
  83.5 1.2 copy-done.6
  84.7 5.0 %fusion.4 = f32[384,2048]{1,0:T(8,128)S(1)} fusion(bf16[384,1408]{1,0:T(8,128)(2,1)S(1)} %copy-done.6, bf16[1,2048,1408]{2,1,0:T(8,128)(2,1)} %param.11), kind=kOutput, calls=%fused_computation.5 | convolution fusion | flops 2214592512 | bytes 9994240 | tf_op jit(solution)/shard_map/dot_general | solution.py:162
  89.7 0.0 slice-start.7
  89.8 5.5 %fusion.14 = bf16[384,2048]{1,0:T(8,128)(2,1)S(1)} fusion(bf16[384,1408]{1,0:T(8,128)(2,1)S(1)} %copy-done.5, bf16[1,1408,2048]{2,1,0:T(8,128)(2,1)} %param.12), kind=kOutput, calls=%fused_computation.16 | convolution fusion | flops 2215378944 | bytes 8421376 | tf_op jit(solution)/shard_map/dot_general | solution.py:159
  95.3 2.6 %add_convert_fusion = bf16[384,2048]{1,0:T(8,128)(2,1)S(1)} fusion(f32[384,2048]{1,0:T(8,128)S(1)} %fusion.4, bf16[384,1408]{1,0:T(8,128)(2,1)S(1)} %copy-done.4, bf16[1,2048,1408]{2,1,0:T(8,128)(2,1)S(1)} %bitcast.89), kind=kOutput, calls=%fused_computation.15 | convolution fusion | flops 2216165376 | bytes 11567104 | tf_op jit(solution)/shard_map/dot_general | solution.py:161
  97.9 2.0 pad_maximum_fusion.1
  99.9 5.6 %all-to-all-start.1 = ((bf16[8,48,4096]{2,1,0:T(8,128)(2,1)}), bf16[8,48,4096]{2,1,0:T(8,128)(2,1)}, u32[]{:S(2)}, u32[]{:S(2)}) async-start(bf16[8,48,4096]{2,1,0:T(8,128)(2,1)} %bitcast.73), calls=%async_computation.1 | async-start | bytes 6291456 | tf_op jit(solution)/shard_map/all_to_all | solution.py:167
  105.5 0.0 copy-done.7
  105.5 0.1 copy.35
  105.6 0.1 mul.61
  105.8 0.1 reshape.151
  105.9 37.1 %all-to-all-done.1 = bf16[8,48,4096]{2,1,0:T(8,128)(2,1)} async-done(((bf16[8,48,4096]{2,1,0:T(8,128)(2,1)}), bf16[8,48,4096]{2,1,0:T(8,128)(2,1)}, u32[]{:S(2)}, u32[]{:S(2)}) %all-to-all-start.1) | async-done | bytes 3145760 | tf_op jit(solution)/shard_map/all_to_all | solution.py:167
  143.1 6.2 %gather_fusion = bf16[256,4096]{1,0:T(8,128)(2,1)S(1)} fusion(bf16[384,4096]{1,0:T(8,128)(2,1)} %bitcast.8, s32[1024]{0:T(1024)S(1)} %pad_clamp_fusion), kind=kCustom, calls=%fused_computation | custom fusion | bytes 4195328 | tf_op jit(solution)/shard_map/gather | solution.py:170
  149.3 1.5 convert_multiply_fusion
  150.8 3.5 %reshape.145 = f32[128,2,2048]{2,1,0:T(2,128)} reshape(f32[256,2048]{1,0:T(8,128)} %convert_multiply_fusion) | data formatting | bytes 4194304 | tf_op jit(solution)/shard_map/reshape | solution.py:174
  154.3 1.5 fusion.31
  155.8 2.6 %reshape.146 = bf16[128,2,2048]{2,1,0:T(2,128)(2,1)} reshape(bf16[256,2048]{1,0:T(8,128)(2,1)} %get-tuple-element.10) | data formatting | bytes 2097152 | tf_op jit(solution)/shard_map/reshape | solution.py:183
  158.5 1.5 reshape.148
  160.0 3.7 %fusion.21 = bf16[128,1,2]{2,1,0:T(2,128)(2,1)S(1)} fusion(bf16[128,2,2048]{2,1,0:T(2,128)(2,1)} %reshape.148, bf16[128,2048,1]{1,0,2:T(8,128)(2,1)S(1)} %bitcast.67), kind=kOutput, calls=%fused_computation.28 | convolution fusion | flops 1048576 | bytes 1573376 | tf_op jit(solution)/shard_map/tkd,td->tk/dot_general | solution.py:176
  163.7 0.6 copy.43
  164.3 3.8 %reduce_sum.57 = bf16[128,2048]{1,0:T(8,128)(2,1)} reduce(f32[128,2,2048]{2,1,0:T(2,128)S(1)} %copy-done.2, f32[]{:T(128)} %constant.17.clone.1), dimensions={1}, to_apply=%region_5.6 | reduce | flops 262144 | bytes 2621444 | tf_op jit(solution)/shard_map/reduce_sum | solution.py:173
  168.0 4.6 %reduce.1 = bf16[128,2048]{1,0:T(8,128)(2,1)} reduce(bf16[128,2,2048]{2,1,0:T(2,128)(2,1)} %reshape.146, bf16[]{:T(256)} %constant.14.clone.1), dimensions={1}, to_apply=%region_6.7.clone | reduce | flops 262144 | bytes 1572866 | tf_op jit(solution)/shard_map/reduce_sum | solution.py:182
  172.6 23.6 %reduce-scatter.4.cloned.1.call-done = bf16[1,264,2048]{2,1,0:T(8,128)(2,1)} async-done(((bf16[16,264,2048]{2,1,0:T(8,128)(2,1)}), bf16[1,264,2048]{2,1,0:T(8,128)(2,1)}) %reduce-scatter.4.cloned.1.call-update) | async-done | bytes 1081360
  196.3 0.9 slice_bitcast_fusion.1
  197.2 0.9 slice_bitcast_fusion.2
  198.1 1.9 fusion.24
  200.0 1.9 slice_convert_fusion
  202.0 0.1 copy.40
  202.0 0.1 copy.41
  202.1 0.2 concatenate.23
  202.4 0.9 maximum_convert_fusion
  (28 shorter events, 0.1 us)
Async XLA Ops:
  7.2 4.9 %copy-start = (bf16[128,2048]{1,0:T(8,128)(2,1)S(1)}, bf16[128,2048]{1,0:T(8,128)(2,1)}, u32[]{:S(2)}) copy-start(bf16[128,2048]{1,0:T(8,128)(2,1)} %param.13) | copy-start | bytes 1572868
  7.2 189.1 %reduce-scatter.4.cloned.1.call-start = ((), (), s32[]{:S(2)}) async-start(), calls=%async_computation.3 | async-start | bytes 18382848
  12.1 45.1 %slice-start.2 = ((s8[5767168]{0:T(1024)(128)(4,1)}), s8[4194304]{0:T(1024)(128)(4,1)S(1)}, s32[]{:S(2)}) async-start(s8[5767168]{0:T(1024)(128)(4,1)} %bitcast.84), calls=%async_computation.6 | async-start | bytes 8388608
  12.7 44.5 %slice-start.3 = ((s8[5767168]{0:T(1024)(128)(4,1)}), s8[1572864]{0:T(1024)(128)(4,1)S(1)}, s32[]{:S(2)}) async-start(s8[5767168]{0:T(1024)(128)(4,1)} %bitcast.84), calls=%async_computation.7 | async-start | bytes 3145728
  12.9 47.0 %slice-start.4 = ((s8[5767168]{0:T(1024)(128)(4,1)}), s8[4194304]{0:T(1024)(128)(4,1)S(1)}, s32[]{:S(2)}) async-start(s8[5767168]{0:T(1024)(128)(4,1)} %bitcast.86), calls=%async_computation.8 | async-start | bytes 8388608
  57.2 5.3 %copy-start.1 = (bf16[8,48,4096]{2,1,0:T(8,128)(2,1)}, bf16[8,48,4096]{2,1,0:T(8,128)(2,1)S(1)}, u32[]{:S(2)}) copy-start(bf16[8,48,4096]{2,1,0:T(8,128)(2,1)S(1)} %all_to_all.10) | copy-start | bytes 9437188
  57.2 2.7 %slice-start.5 = ((s8[5767168]{0:T(1024)(128)(4,1)}), s8[1572864]{0:T(1024)(128)(4,1)S(1)}, s32[]{:S(2)}) async-start(s8[5767168]{0:T(1024)(128)(4,1)} %bitcast.86), calls=%async_computation.9 | async-start | bytes 3145728
  57.3 5.3 %slice-start = ((s8[5767168]{0:T(1024)(128)(4,1)}), s8[4194304]{0:T(1024)(128)(4,1)S(1)}, s32[]{:S(2)}) async-start(s8[5767168]{0:T(1024)(128)(4,1)} %bitcast.82), calls=%async_computation.4 | async-start | bytes 8388608
  59.9 2.6 %slice-start.1 = ((s8[5767168]{0:T(1024)(128)(4,1)}), s8[1572864]{0:T(1024)(128)(4,1)S(1)}, s32[]{:S(2)}) async-start(s8[5767168]{0:T(1024)(128)(4,1)} %bitcast.82), calls=%async_computation.5 | async-start | bytes 3145728
  83.5 1.2 copy-start.6
  84.7 5.0 %copy-start.5 = (bf16[384,1408]{1,0:T(8,128)(2,1)S(1)}, bf16[384,1408]{1,0:T(8,128)(2,1)}, u32[]{:S(2)}) copy-start(bf16[384,1408]{1,0:T(8,128)(2,1)} %get-tuple-element.6.h_ref) | copy-start | bytes 3244036
  84.7 10.5 %slice-start.6 = ((s8[5767168]{0:T(1024)(128)(4,1)}), s8[4194304]{0:T(1024)(128)(4,1)S(1)}, s32[]{:S(2)}) async-start(s8[5767168]{0:T(1024)(128)(4,1)} %bitcast.88), calls=%async_computation.10 | async-start | bytes 8388608
  89.7 5.5 %copy-start.4 = (bf16[384,1408]{1,0:T(8,128)(2,1)S(1)}, bf16[384,1408]{1,0:T(8,128)(2,1)}, u32[]{:S(2)}) copy-start(bf16[384,1408]{1,0:T(8,128)(2,1)} %get-tuple-element.7.gd_ref) | copy-start | bytes 3244036
  89.7 5.5 %slice-start.7 = ((s8[5767168]{0:T(1024)(128)(4,1)}), s8[1572864]{0:T(1024)(128)(4,1)S(1)}, s32[]{:S(2)}) async-start(s8[5767168]{0:T(1024)(128)(4,1)} %bitcast.88), calls=%async_computation.11 | async-start | bytes 3145728
  99.9 5.6 %copy-start.7 = (bf16[128,2]{0,1:T(2,128)(2,1)S(1)}, bf16[128,2]{0,1:T(2,128)(2,1)}, u32[]{:S(2)}) copy-start(bf16[128,2]{0,1:T(2,128)(2,1)} %param.9) | copy-start | bytes 1540
  99.9 43.2 %all-to-all-start.1 = ((bf16[8,48,4096]{2,1,0:T(8,128)(2,1)}), bf16[8,48,4096]{2,1,0:T(8,128)(2,1)}, u32[]{:S(2)}, u32[]{:S(2)}) async-start(bf16[8,48,4096]{2,1,0:T(8,128)(2,1)} %bitcast.73), calls=%async_computation.1 | async-start | bytes 6291456 | tf_op jit(solution)/shard_map/all_to_all | solution.py:167
  155.8 2.6 %copy-start.3 = (bf16[256,2048]{1,0:T(8,128)(2,1)S(1)}, bf16[256,2048]{1,0:T(8,128)(2,1)}, u32[]{:S(2)}) copy-start(bf16[256,2048]{1,0:T(8,128)(2,1)} %get-tuple-element.9) | copy-start | bytes 3145732
  160.0 4.3 %copy-start.2 = (f32[128,2,2048]{2,1,0:T(2,128)S(1)}, f32[128,2,2048]{2,1,0:T(2,128)}, u32[]{:S(2)}) copy-start(f32[128,2,2048]{2,1,0:T(2,128)} %reshape.145) | copy-start | bytes 6291460
Sparse Core Ops, SparseCore 0:
  83.6 112.5 reduce-scatter.3

commit v9 on v7

--- a/solution.py
+++ b/solution.py
@@ -79,21 +79,35 @@
     )(recv, gate_delta, up_delta, hidden, recv)
 
 
+def _unpack_kernel(red_ref, g_ref, u_ref, d_ref):
+    rows, ff = g_ref.shape
+    width = red_ref.shape[2]
+    over = 2 * ff - width
+    extra = rows * over // width
+    g_ref[...] = red_ref[0, :rows, :ff].astype(g_ref.dtype)
+    u_ref[:, : width - ff] = red_ref[0, :rows, ff:].astype(u_ref.dtype)
+    col_tiles = over // LANES
+    for i in range(rows // TILE_ROWS):
+        for j in range(col_tiles):
+            q, p = divmod(i * col_tiles + j, width // LANES)
+            col = width - ff + j * LANES
+            u_ref[i * TILE_ROWS : (i + 1) * TILE_ROWS, col : col + LANES] = red_ref[
+                0, rows + q * TILE_ROWS : rows + (q + 1) * TILE_ROWS, p * LANES : (p + 1) * LANES
+            ].astype(u_ref.dtype)
+    d_ref[...] = red_ref[0, rows + extra :, :].astype(d_ref.dtype)
+
+
 def unpack_weight_grads(red, gu_rows, ff):
-    width = red.shape[1]
-    over = 2 * ff - width
-    extra = gu_rows * over // width
-    gate = red[:gu_rows, :ff]
-    up_head = red[:gu_rows, ff:]
-    tiles = red[gu_rows : gu_rows + extra].reshape(
-        extra // TILE_ROWS, TILE_ROWS, width // LANES, LANES
-    )
-    tiles = tiles.transpose(0, 2, 1, 3).reshape(
-        gu_rows // TILE_ROWS, over // LANES, TILE_ROWS, LANES
-    )
-    up_tail = tiles.transpose(0, 2, 1, 3).reshape(gu_rows, over)
-    up = jnp.concatenate([up_head, up_tail], axis=1)
-    return gate, up, red[gu_rows + extra :]
+    _, chunk, width = red.shape
+    extra = gu_rows * (2 * ff - width) // width
+    return pl.pallas_call(
+        _unpack_kernel,
+        out_shape=(
+            jax.ShapeDtypeStruct((gu_rows, ff), jnp.float32),
+            jax.ShapeDtypeStruct((gu_rows, ff), jnp.float32),
+            jax.ShapeDtypeStruct((chunk - gu_rows - extra, width), jnp.float32),
+        ),
+    )(red)
 
 
 def body(tokens, experts, gates, w_gate, w_up, w_down, cotangent):
@@ -151,10 +165,8 @@
     packed = packed_weight_grads(recv, gate_delta, up_delta, hidden, n_rep)
     reduced = lax.optimization_barrier(
         lax.psum_scatter(packed, "rep", scatter_dimension=0, tiled=True)
-    )[0]
-    grad_gate, grad_up, grad_down = (
-        part.astype(jnp.float32) for part in unpack_weight_grads(reduced, gu_rows, ff_width)
-    )
+    )
+    grad_gate, grad_up, grad_down = unpack_weight_grads(reduced, gu_rows, ff_width)
 
     expert_out = jnp.dot(hidden, down_mat, preferred_element_type=jnp.float32).astype(jnp.bfloat16)
     row_grads = (

time: 210 us -> 205 us (0.976)
  other arithmetic: 18.4 us -> 13.7 us
  Pallas kernels: 15.3 us -> 17.9 us
  local copies, waits for them, and re-layouts: 21.4 us -> 19.2 us
    convert_element_type x2 -> x0, other arithmetic: 2.81 us -> none  [body(): part.astype(jnp.float32)]
    pallas_call x0 -> x1, Pallas kernels: none -> 2.62 us  [unpack_weight_grads(): pl.pallas_call(_unpack_kernel, out_shape=(jax.ShapeDtypeStruct((gu_rows,...]
where the time goes in v9:
time: 205 us
  waiting for transfers between devices  60.8 us (30%)
  blocking collectives  44.3 us (22%)
  matrix products  28.8 us (14%)
  local copies, waits for them, and re-layouts  19.2 us (9%)
  Pallas kernels  17.9 us (9%)
  between operations  14.4 us (7%)
  other arithmetic  13.7 us (7%)
  starting transfers between devices  5.61 us (3%)
    all_to_all x1, blocking collectives, body(): lax.all_to_all(disp, 'ep', split_axis=0, concat_axis=0, tiled=True)  44.3 us
    all_to_all x1, waiting for transfers between devices, body(): lax.all_to_all(back, 'ep', split_axis=0, concat_axis=0, tiled=True)  37.1 us
    unnamed x2, waiting for transfers between devices  23.7 us
    pallas_call x1, Pallas kernels, packed_weight_grads(): pl.pallas_call(_pack_kernel, grid=(n_rep // group,), in_specs=[pl.BlockSp...  15.3 us
    gather x1, local copies, waits for them, and re-layouts, body(): pair_back = returned[slot_index]  6.18 us
    all_to_all x1, starting transfers between devices, body(): lax.all_to_all(back, 'ep', split_axis=0, concat_axis=0, tiled=True)  5.58 us
    dot_general x1, matrix products, body(): jnp.dot(hidden, down_mat, preferred_element_type=jnp.float32)  5.48 us
    dot_general x1, matrix products, body(): lax.dot_general(up_delta, up_mat, contract, preferred_element_type=jnp.fl...  5 us
  transfers between devices with their start and end apart: 2, of which 2 were waited for; matrix products, arithmetic and copies ran while one was open for 22% of the time, Pallas kernels for 0%

profile of v9, /device:TPU:1, one launch (start us, length us, event | category | flops | bytes accessed | tf_op | source)
XLA Modules:
  0.0 204.7 jit_solution(12089464092800077595)
XLA Ops:
  7.2 0.0 copy-start
  7.2 0.0 reduce-scatter.4.cloned.1.call-start
  7.2 0.8 copy.26
  8.1 0.1 eq.42
  8.2 0.1 eq.38
  8.4 0.6 reduce-window.6
  8.9 0.2 slice_reduce_fusion
  9.2 0.1 fusion.27
  9.3 0.1 reduce_sum.53
  9.5 0.1 copy.29
  9.5 0.1 convert_reduce_fusion
  9.7 0.8 fusion.24
  10.5 1.6 convolution_convert_fusion.1
  12.1 0.0 copy-done
  12.1 0.0 slice-start.2
  12.1 0.6 convolution_convert_fusion
  12.7 0.0 slice-start.3
  12.7 0.2 pad_maximum_fusion
  12.9 0.0 slice-start.4
  13.0 44.3 %all_to_all.10 = bf16[8,48,4096]{2,1,0:T(8,128)(2,1)S(1)} all-to-all(bf16[8,48,4096]{2,1,0:T(8,128)(2,1)S(1)} %bitcast.57), channel_id=1, replica_groups=mesh['rep'=16,'ep'=8] {'ep'}, dimensions={0} | all-to-all | bytes 6291456 | tf_op jit(solution)/shard_map/all_to_all | solution.py:146
  57.2 0.0 slice-done.2
  57.2 0.0 slice-done.3
  57.2 0.0 slice-start.5
  57.3 0.0 slice-start
  57.3 2.6 %fusion = f32[384,1408]{1,0:T(8,128)S(1)} fusion(bf16[1,1408,2048]{2,1,0:T(8,128)(2,1)S(1)} %bitcast.64, bf16[384,4096]{1,0:T(8,128)(2,1)S(1)} %bitcast.51), kind=kOutput, calls=%fused_computation.1 | convolution fusion | flops 2214592512 | bytes 9502720 | tf_op jit(solution)/shard_map/dot_general | solution.py:158
  59.9 0.0 slice-done.4
  59.9 0.0 slice-done.5
  59.9 0.0 slice-start.1
  60.0 2.6 %fusion.10 = f32[384,1408]{1,0:T(8,128)S(1)} fusion(bf16[1,2048,1408]{2,1,0:T(8,128)(2,1)S(1)} %bitcast.66, bf16[384,4096]{1,0:T(8,128)(2,1)S(1)} %bitcast.52), kind=kOutput, calls=%fused_computation.11 | convolution fusion | flops 2214592512 | bytes 9502720 | tf_op jit(solution)/shard_map/dot_general | solution.py:153
  62.6 0.0 copy-done.1
  62.6 0.0 slice-done
  62.6 0.0 slice-done.1
  62.6 4.5 %multiply_convert_fusion.2 = (bf16[384,1408]{1,0:T(8,128)(2,1)}, bf16[384,1408]{1,0:T(8,128)(2,1)}, bf16[384,1408]{1,0:T(8,128)(2,1)}) fusion(f32[384,1408]{1,0:T(8,128)S(1)} %fusion.10, f32[384,1408]{1,0:T(8,128)S(1)} %fusion, bf16[1,2048,1408]{2,1,0:T(8,128)(2,1)S(1)} %bitcast.62, bf16[384,4096]{1,0:T(8,128)(2,1)S(1)} %bitcast.53), kind=kOutput, calls=%fused_computation.21 | convolution fusion | flops 2222702592 | bytes 14909440 | tf_op jit(solution)/shard_map/dot_general | solution.py:154
  67.1 15.3 %shard_map.118 = bf16[16,264,2048]{2,1,0:T(8,128)(2,1)} custom-call(bf16[384,4096]{1,0:T(8,128)(2,1)} %bitcast.54, bf16[384,1408]{1,0:T(8,128)(2,1)} %get-tuple-element.13.gd_ref, bf16[384,1408]{1,0:T(8,128)(2,1)} %get-tuple-element.14.ud_ref, bf16[384,1408]{1,0:T(8,128)(2,1)} %get-tuple-element.12.h_ref, bf16[384,4096]{1,0:T(8,128)(2,1)} %bitcast.55), custom_call_target="tpu_custom_call" | custom-call | flops 6643777536 | bytes 17301504 | tf_op jit(solution)/shard_map/pallas_call | solution.py:62
  82.5 0.0 reduce-scatter.4.cloned.1.call-update
  82.5 1.2 copy-done.6
  83.7 5.0 %fusion.4 = f32[384,2048]{1,0:T(8,128)S(1)} fusion(bf16[384,1408]{1,0:T(8,128)(2,1)S(1)} %copy-done.6, bf16[1,2048,1408]{2,1,0:T(8,128)(2,1)} %param.11), kind=kOutput, calls=%fused_computation.5 | convolution fusion | flops 2214592512 | bytes 9994240 | tf_op jit(solution)/shard_map/dot_general | solution.py:174
  88.7 0.0 copy-done.5
  88.7 0.0 copy-start.4
  88.7 0.0 slice-start.7
  88.7 5.5 %fusion.14 = bf16[384,2048]{1,0:T(8,128)(2,1)S(1)} fusion(bf16[384,1408]{1,0:T(8,128)(2,1)S(1)} %copy-done.5, bf16[1,1408,2048]{2,1,0:T(8,128)(2,1)} %param.12), kind=kOutput, calls=%fused_computation.16 | convolution fusion | flops 2215378944 | bytes 8421376 | tf_op jit(solution)/shard_map/dot_general | solution.py:171
  94.2 0.0 slice-done.6
  94.2 0.0 copy-done.4
  94.2 0.0 slice-done.7
  94.3 2.6 %add_convert_fusion = bf16[384,2048]{1,0:T(8,128)(2,1)S(1)} fusion(f32[384,2048]{1,0:T(8,128)S(1)} %fusion.4, bf16[384,1408]{1,0:T(8,128)(2,1)S(1)} %copy-done.4, bf16[1,2048,1408]{2,1,0:T(8,128)(2,1)S(1)} %bitcast.68), kind=kOutput, calls=%fused_computation.15 | convolution fusion | flops 2216165376 | bytes 11567104 | tf_op jit(solution)/shard_map/dot_general | solution.py:173
  96.9 2.0 pad_maximum_fusion.1
  98.9 5.6 %all-to-all-start.1 = ((bf16[8,48,4096]{2,1,0:T(8,128)(2,1)}), bf16[8,48,4096]{2,1,0:T(8,128)(2,1)}, u32[]{:S(2)}, u32[]{:S(2)}) async-start(bf16[8,48,4096]{2,1,0:T(8,128)(2,1)} %bitcast.56), calls=%async_computation.1 | async-start | bytes 6291456 | tf_op jit(solution)/shard_map/all_to_all | solution.py:179
  104.5 0.1 copy.25
  104.6 0.1 mul.61
  104.7 0.1 reshape.109
  104.9 37.1 %all-to-all-done.1 = bf16[8,48,4096]{2,1,0:T(8,128)(2,1)} async-done(((bf16[8,48,4096]{2,1,0:T(8,128)(2,1)}), bf16[8,48,4096]{2,1,0:T(8,128)(2,1)}, u32[]{:S(2)}, u32[]{:S(2)}) %all-to-all-start.1) | async-done | bytes 3145760 | tf_op jit(solution)/shard_map/all_to_all | solution.py:179
  142.0 6.2 %gather_fusion = bf16[256,4096]{1,0:T(8,128)(2,1)S(1)} fusion(bf16[384,4096]{1,0:T(8,128)(2,1)} %bitcast.8, s32[1024]{0:T(1024)S(1)} %pad_clamp_fusion), kind=kCustom, calls=%fused_computation | custom fusion | bytes 4195328 | tf_op jit(solution)/shard_map/gather | solution.py:182
  148.2 1.5 convert_multiply_fusion
  149.8 3.5 %reshape.105 = f32[128,2,2048]{2,1,0:T(2,128)} reshape(f32[256,2048]{1,0:T(8,128)} %convert_multiply_fusion) | data formatting | bytes 4194304 | tf_op jit(solution)/shard_map/reshape | solution.py:186
  153.2 1.5 fusion.30
  154.8 2.7 %reshape.106 = bf16[128,2,2048]{2,1,0:T(2,128)(2,1)} reshape(bf16[256,2048]{1,0:T(8,128)(2,1)} %get-tuple-element.16) | data formatting | bytes 2097152 | tf_op jit(solution)/shard_map/reshape | solution.py:195
  157.4 0.0 copy-done.3
  157.4 1.5 reshape.108
  158.9 3.7 %fusion.21 = bf16[128,1,2]{2,1,0:T(2,128)(2,1)S(1)} fusion(bf16[128,2,2048]{2,1,0:T(2,128)(2,1)} %reshape.108, bf16[128,2048,1]{1,0,2:T(8,128)(2,1)S(1)} %bitcast.50), kind=kOutput, calls=%fused_computation.28 | convolution fusion | flops 1048576 | bytes 1573376 | tf_op jit(solution)/shard_map/tkd,td->tk/dot_general | solution.py:188
  162.6 0.6 copy.31
  163.2 3.8 %reduce_sum.57 = bf16[128,2048]{1,0:T(8,128)(2,1)} reduce(f32[128,2,2048]{2,1,0:T(2,128)S(1)} %copy-done.2, f32[]{:T(128)} %constant.17.clone.1), dimensions={1}, to_apply=%region_5.6 | reduce | flops 262144 | bytes 2621444 | tf_op jit(solution)/shard_map/reduce_sum | solution.py:185
  167.0 4.6 %reduce.1 = bf16[128,2048]{1,0:T(8,128)(2,1)} reduce(bf16[128,2,2048]{2,1,0:T(2,128)(2,1)} %reshape.106, bf16[]{:T(256)} %constant.14.clone.1), dimensions={1}, to_apply=%region_6.7.clone | reduce | flops 262144 | bytes 1572866 | tf_op jit(solution)/shard_map/reduce_sum | solution.py:194
  171.6 23.6 %reduce-scatter.4.cloned.1.call-done.red_ref = bf16[1,264,2048]{2,1,0:T(8,128)(2,1)} async-done(((bf16[16,264,2048]{2,1,0:T(8,128)(2,1)}), bf16[1,264,2048]{2,1,0:T(8,128)(2,1)}) %reduce-scatter.4.cloned.1.call-update) | async-done | bytes 1081360
  195.2 2.6 %shard_map.119 = (f32[128,1408]{1,0:T(8,128)}, f32[128,1408]{1,0:T(8,128)}, f32[88,2048]{1,0:T(8,128)}) custom-call(bf16[1,264,2048]{2,1,0:T(8,128)(2,1)} %reduce-scatter.4.cloned.1.call-done.red_ref), custom_call_target="tpu_custom_call" | custom-call | tf_op jit(solution)/shard_map/pallas_call | solution.py:103
  (19 shorter events, 0.1 us)
Async XLA Ops:
  7.2 4.9 %copy-start = (bf16[128,2048]{1,0:T(8,128)(2,1)S(1)}, bf16[128,2048]{1,0:T(8,128)(2,1)}, u32[]{:S(2)}) copy-start(bf16[128,2048]{1,0:T(8,128)(2,1)} %param.13) | copy-start | bytes 1572868
  7.2 188.0 %reduce-scatter.4.cloned.1.call-start = ((), (), s32[]{:S(2)}) async-start(), calls=%async_computation.3 | async-start | bytes 18382848
  12.1 45.1 %slice-start.2 = ((s8[5767168]{0:T(1024)(128)(4,1)}), s8[4194304]{0:T(1024)(128)(4,1)S(1)}, s32[]{:S(2)}) async-start(s8[5767168]{0:T(1024)(128)(4,1)} %bitcast.63), calls=%async_computation.6 | async-start | bytes 8388608
  12.7 44.5 %slice-start.3 = ((s8[5767168]{0:T(1024)(128)(4,1)}), s8[1572864]{0:T(1024)(128)(4,1)S(1)}, s32[]{:S(2)}) async-start(s8[5767168]{0:T(1024)(128)(4,1)} %bitcast.63), calls=%async_computation.7 | async-start | bytes 3145728
  12.9 47.0 %slice-start.4 = ((s8[5767168]{0:T(1024)(128)(4,1)}), s8[4194304]{0:T(1024)(128)(4,1)S(1)}, s32[]{:S(2)}) async-start(s8[5767168]{0:T(1024)(128)(4,1)} %bitcast.65), calls=%async_computation.8 | async-start | bytes 8388608
  57.2 5.3 %copy-start.1 = (bf16[8,48,4096]{2,1,0:T(8,128)(2,1)}, bf16[8,48,4096]{2,1,0:T(8,128)(2,1)S(1)}, u32[]{:S(2)}) copy-start(bf16[8,48,4096]{2,1,0:T(8,128)(2,1)S(1)} %all_to_all.10) | copy-start | bytes 9437188
  57.2 2.7 %slice-start.5 = ((s8[5767168]{0:T(1024)(128)(4,1)}), s8[1572864]{0:T(1024)(128)(4,1)S(1)}, s32[]{:S(2)}) async-start(s8[5767168]{0:T(1024)(128)(4,1)} %bitcast.65), calls=%async_computation.9 | async-start | bytes 3145728
  57.3 5.3 %slice-start = ((s8[5767168]{0:T(1024)(128)(4,1)}), s8[4194304]{0:T(1024)(128)(4,1)S(1)}, s32[]{:S(2)}) async-start(s8[5767168]{0:T(1024)(128)(4,1)} %bitcast.61), calls=%async_computation.4 | async-start | bytes 8388608
  59.9 2.6 %slice-start.1 = ((s8[5767168]{0:T(1024)(128)(4,1)}), s8[1572864]{0:T(1024)(128)(4,1)S(1)}, s32[]{:S(2)}) async-start(s8[5767168]{0:T(1024)(128)(4,1)} %bitcast.61), calls=%async_computation.5 | async-start | bytes 3145728
  82.4 1.2 copy-start.6
  83.7 5.0 %copy-start.5 = (bf16[384,1408]{1,0:T(8,128)(2,1)S(1)}, bf16[384,1408]{1,0:T(8,128)(2,1)}, u32[]{:S(2)}) copy-start(bf16[384,1408]{1,0:T(8,128)(2,1)} %get-tuple-element.12.h_ref) | copy-start | bytes 3244036
  83.7 10.5 %slice-start.6 = ((s8[5767168]{0:T(1024)(128)(4,1)}), s8[4194304]{0:T(1024)(128)(4,1)S(1)}, s32[]{:S(2)}) async-start(s8[5767168]{0:T(1024)(128)(4,1)} %bitcast.67), calls=%async_computation.10 | async-start | bytes 8388608
  88.7 5.5 %copy-start.4 = (bf16[384,1408]{1,0:T(8,128)(2,1)S(1)}, bf16[384,1408]{1,0:T(8,128)(2,1)}, u32[]{:S(2)}) copy-start(bf16[384,1408]{1,0:T(8,128)(2,1)} %get-tuple-element.13.gd_ref) | copy-start | bytes 3244036
  88.7 5.5 %slice-start.7 = ((s8[5767168]{0:T(1024)(128)(4,1)}), s8[1572864]{0:T(1024)(128)(4,1)S(1)}, s32[]{:S(2)}) async-start(s8[5767168]{0:T(1024)(128)(4,1)} %bitcast.67), calls=%async_computation.11 | async-start | bytes 3145728
  98.9 5.6 %copy-start.7 = (bf16[128,2]{0,1:T(2,128)(2,1)S(1)}, bf16[128,2]{0,1:T(2,128)(2,1)}, u32[]{:S(2)}) copy-start(bf16[128,2]{0,1:T(2,128)(2,1)} %param.9) | copy-start | bytes 1540
  98.9 43.2 %all-to-all-start.1 = ((bf16[8,48,4096]{2,1,0:T(8,128)(2,1)}), bf16[8,48,4096]{2,1,0:T(8,128)(2,1)}, u32[]{:S(2)}, u32[]{:S(2)}) async-start(bf16[8,48,4096]{2,1,0:T(8,128)(2,1)} %bitcast.56), calls=%async_computation.1 | async-start | bytes 6291456 | tf_op jit(solution)/shard_map/all_to_all | solution.py:179
  154.8 2.7 %copy-start.3 = (bf16[256,2048]{1,0:T(8,128)(2,1)S(1)}, bf16[256,2048]{1,0:T(8,128)(2,1)}, u32[]{:S(2)}) copy-start(bf16[256,2048]{1,0:T(8,128)(2,1)} %get-tuple-element.15) | copy-start | bytes 3145732
  158.9 4.3 %copy-start.2 = (f32[128,2,2048]{2,1,0:T(2,128)S(1)}, f32[128,2,2048]{2,1,0:T(2,128)}, u32[]{:S(2)}) copy-start(f32[128,2,2048]{2,1,0:T(2,128)} %reshape.105) | copy-start | bytes 6291460
Sparse Core Ops, SparseCore 0:
  82.6 112.5 reduce-scatter.3

commit v10 on v9

--- a/solution.py
+++ b/solution.py
@@ -10,8 +10,8 @@
 LANES = 128
 
 
-def _pack_kernel(x_ref, gd_ref, ud_ref, h_ref, og_ref, o_ref, down_ref):
-    ff = gd_ref.shape[1]
+def _pack_kernel(x_ref, dl_ref, h_ref, og_ref, o_ref, down_ref):
+    ff = dl_ref.shape[1] // 2
     width = og_ref.shape[1]
     group, chunk, _ = o_ref.shape
     rows = x_ref.shape[1] // group
@@ -27,13 +27,12 @@
         )
 
     x = x_ref[...]
-    g_all = lax.dot_general(x, gd_ref[...], first, preferred_element_type=jnp.float32)
-    u_all = lax.dot_general(x, ud_ref[...], first, preferred_element_type=jnp.float32)
+    gu_all = lax.dot_general(x, dl_ref[...], first, preferred_element_type=jnp.float32)
     col_tiles = over // LANES
     extra = rows * over // width
     for c in range(group):
-        g = g_all[c * rows : (c + 1) * rows]
-        u = u_all[c * rows : (c + 1) * rows]
+        g = gu_all[c * rows : (c + 1) * rows, :ff]
+        u = gu_all[c * rows : (c + 1) * rows, ff:]
         o_ref[c, :rows, :ff] = g.astype(o_ref.dtype)
         o_ref[c, :rows, ff:] = u[:, : width - ff].astype(o_ref.dtype)
         for i in range(rows // TILE_ROWS):
@@ -50,8 +49,8 @@
 GROUP = 4
 
 
-def packed_weight_grads(recv, gate_delta, up_delta, hidden, n_rep):
-    slots, ff = gate_delta.shape
+def packed_weight_grads(recv, deltas, hidden, n_rep):
+    slots, ff = hidden.shape
     model_width = recv.shape[1] // 2
     gu_rows = model_width // n_rep
     down_rows = ff // n_rep
@@ -64,8 +63,7 @@
         grid=(n_rep // group,),
         in_specs=[
             pl.BlockSpec((slots, group * gu_rows), lambda r: (0, r)),
-            pl.BlockSpec((slots, ff), lambda r: (0, 0)),
-            pl.BlockSpec((slots, ff), lambda r: (0, 0)),
+            pl.BlockSpec((slots, 2 * ff), lambda r: (0, 0)),
             pl.BlockSpec((slots, ff), lambda r: (0, 0)),
             pl.BlockSpec((slots, model_width), lambda r: (0, 1)),
         ],
@@ -76,7 +74,7 @@
         cost_estimate=pl.CostEstimate(
             flops=flops, transcendentals=0, bytes_accessed=2 * n_rep * chunk * model_width
         ),
-    )(recv, gate_delta, up_delta, hidden, recv)
+    )(recv, deltas, hidden, recv)
 
 
 def _unpack_kernel(red_ref, g_ref, u_ref, d_ref):
@@ -162,7 +160,8 @@
     up_delta = (hidden_grad * activated).astype(jnp.bfloat16)
 
     gu_rows = model_width // n_rep
-    packed = packed_weight_grads(recv, gate_delta, up_delta, hidden, n_rep)
+    deltas = jnp.concatenate([gate_delta, up_delta], axis=1)
+    packed = packed_weight_grads(recv, deltas, hidden, n_rep)
     reduced = lax.optimization_barrier(
         lax.psum_scatter(packed, "rep", scatter_dimension=0, tiled=True)
     )

time: 205 us -> 206 us (level)
    dot_general x1, matrix products: 2.63 us -> 5.31 us  [body(): lax.dot_general(gate_delta, gate_mat, contract, preferred_element_type=jn...]
where the time goes in v10:
time: 206 us
  waiting for transfers between devices  59.7 us (29%)
  blocking collectives  44.3 us (22%)
  matrix products  29.3 us (14%)
  local copies, waits for them, and re-layouts  19.5 us (9%)
  Pallas kernels  17.7 us (9%)
  other arithmetic  15.5 us (8%)
  between operations  14.3 us (7%)
  starting transfers between devices  5.53 us (3%)
    all_to_all x1, blocking collectives, body(): lax.all_to_all(disp, 'ep', split_axis=0, concat_axis=0, tiled=True)  44.3 us
    all_to_all x1, waiting for transfers between devices, body(): lax.all_to_all(back, 'ep', split_axis=0, concat_axis=0, tiled=True)  37.1 us
    unnamed x2, waiting for transfers between devices  22.6 us
    pallas_call x1, Pallas kernels, packed_weight_grads(): pl.pallas_call(_pack_kernel, grid=(n_rep // group,), in_specs=[pl.BlockSp...  15 us
    gather x1, local copies, waits for them, and re-layouts, body(): pair_back = returned[slot_index]  6.28 us
    all_to_all x1, starting transfers between devices, body(): lax.all_to_all(back, 'ep', split_axis=0, concat_axis=0, tiled=True)  5.49 us
    dot_general x1, matrix products, body(): jnp.dot(hidden, down_mat, preferred_element_type=jnp.float32)  5.32 us
    dot_general x1, matrix products, body(): lax.dot_general(gate_delta, gate_mat, contract, preferred_element_type=jn...  5.31 us
  transfers between devices with their start and end apart: 2, of which 2 were waited for; matrix products, arithmetic and copies ran while one was open for 22% of the time, Pallas kernels for 0%

profile of v10, /device:TPU:1, one launch (start us, length us, event | category | flops | bytes accessed | tf_op | source)
XLA Modules:
  0.0 205.7 jit_solution(15334289627776044896)
XLA Ops:
  7.2 0.0 copy-start
  7.2 0.0 reduce-scatter.4.cloned.1.call-start
  7.2 0.8 copy.26
  8.1 0.1 eq.42
  8.2 0.1 eq.38
  8.4 0.6 reduce-window.6
  8.9 0.2 slice_reduce_fusion
  9.2 0.1 fusion.27
  9.3 0.1 reduce_sum.53
  9.5 0.1 copy.29
  9.5 0.1 convert_reduce_fusion
  9.7 0.8 fusion.24
  10.5 1.6 convolution_convert_fusion.1
  12.1 0.0 copy-done
  12.1 0.0 slice-start
  12.1 0.6 convolution_convert_fusion
  12.7 0.0 slice-start.1
  12.7 0.2 pad_maximum_fusion
  12.9 0.0 slice-start.4
  13.0 44.3 %all_to_all.10 = bf16[8,48,4096]{2,1,0:T(8,128)(2,1)S(1)} all-to-all(bf16[8,48,4096]{2,1,0:T(8,128)(2,1)S(1)} %bitcast.57), channel_id=1, replica_groups=mesh['rep'=16,'ep'=8] {'ep'}, dimensions={0} | all-to-all | bytes 6291456 | tf_op jit(solution)/shard_map/all_to_all | solution.py:144
  57.2 0.0 copy-start.1
  57.2 0.0 slice-done
  57.2 0.0 slice-done.1
  57.2 0.0 slice-start.5
  57.3 0.0 slice-start.2
  57.3 2.6 %fusion = f32[384,1408]{1,0:T(8,128)S(1)} fusion(bf16[1,1408,2048]{2,1,0:T(8,128)(2,1)S(1)} %bitcast.62, bf16[384,4096]{1,0:T(8,128)(2,1)S(1)} %bitcast.51), kind=kOutput, calls=%fused_computation.1 | convolution fusion | flops 2214592512 | bytes 9502720 | tf_op jit(solution)/shard_map/dot_general | solution.py:156
  59.9 0.0 slice-done.4
  59.9 0.0 slice-done.5
  59.9 0.0 slice-start.3
  60.0 2.6 %fusion.10 = f32[384,1408]{1,0:T(8,128)S(1)} fusion(bf16[1,2048,1408]{2,1,0:T(8,128)(2,1)S(1)} %bitcast.66, bf16[384,4096]{1,0:T(8,128)(2,1)S(1)} %bitcast.52), kind=kOutput, calls=%fused_computation.11 | convolution fusion | flops 2214592512 | bytes 9502720 | tf_op jit(solution)/shard_map/dot_general | solution.py:151
  62.6 0.0 copy-done.1
  62.6 0.0 slice-done.2
  62.6 0.0 slice-done.3
  62.6 4.2 %multiply_convert_fusion.2 = (bf16[384,1408]{1,0:T(8,128)(2,1)}, bf16[384,1408]{1,0:T(8,128)(2,1)S(1)}, bf16[384,1408]{1,0:T(8,128)(2,1)S(1)}) fusion(f32[384,1408]{1,0:T(8,128)S(1)} %fusion.10, f32[384,1408]{1,0:T(8,128)S(1)} %fusion, bf16[1,2048,1408]{2,1,0:T(8,128)(2,1)S(1)} %bitcast.64, bf16[384,4096]{1,0:T(8,128)(2,1)S(1)} %bitcast.53), kind=kOutput, calls=%fused_computation.22 | convolution fusion | flops 2222702592 | bytes 14909440 | tf_op jit(solution)/shard_map/dot_general | solution.py:152
  66.8 0.0 copy-start.4
  66.8 1.7 pad_maximum_fusion.2.dl_ref
  68.5 0.1 copy-done.4
  68.5 15.0 %shard_map.118 = bf16[16,264,2048]{2,1,0:T(8,128)(2,1)} custom-call(bf16[384,4096]{1,0:T(8,128)(2,1)} %bitcast.54, bf16[384,2816]{1,0:T(8,128)(2,1)} %pad_maximum_fusion.2.dl_ref, bf16[384,1408]{1,0:T(8,128)(2,1)} %get-tuple-element.12.h_ref, bf16[384,4096]{1,0:T(8,128)(2,1)} %bitcast.55), custom_call_target="tpu_custom_call" | custom-call | flops 6643777536 | bytes 17301504 | tf_op jit(solution)/shard_map/pallas_call | solution.py:61
  83.6 0.0 reduce-scatter.4.cloned.1.call-update
  83.6 1.2 copy-done.3
  84.8 5.3 %fusion.14 = bf16[384,2048]{1,0:T(8,128)(2,1)S(1)} fusion(bf16[384,1408]{1,0:T(8,128)(2,1)S(1)} %copy-done.3, bf16[1,1408,2048]{2,1,0:T(8,128)(2,1)} %param.12), kind=kOutput, calls=%fused_computation.16 | convolution fusion | flops 2215378944 | bytes 8421376 | tf_op jit(solution)/shard_map/dot_general | solution.py:170
  90.1 0.0 copy-done.5
  90.1 4.7 %fusion.4 = f32[384,2048]{1,0:T(8,128)S(1)} fusion(bf16[384,1408]{1,0:T(8,128)(2,1)S(1)} %copy-done.5, bf16[1,2048,1408]{2,1,0:T(8,128)(2,1)} %param.11), kind=kOutput, calls=%fused_computation.5 | convolution fusion | flops 2214592512 | bytes 9994240 | tf_op jit(solution)/shard_map/dot_general | solution.py:173
  94.8 5.3 %add_convert_fusion = bf16[384,2048]{1,0:T(8,128)(2,1)S(1)} fusion(f32[384,2048]{1,0:T(8,128)S(1)} %fusion.4, bf16[384,1408]{1,0:T(8,128)(2,1)S(1)} %get-tuple-element.13, bf16[1,2048,1408]{2,1,0:T(8,128)(2,1)} %param.10), kind=kOutput, calls=%fused_computation.15 | convolution fusion | flops 2216165376 | bytes 11567104 | tf_op jit(solution)/shard_map/dot_general | solution.py:172
  100.2 2.0 pad_maximum_fusion.1
  102.2 5.5 %all-to-all-start.1 = ((bf16[8,48,4096]{2,1,0:T(8,128)(2,1)}), bf16[8,48,4096]{2,1,0:T(8,128)(2,1)}, u32[]{:S(2)}, u32[]{:S(2)}) async-start(bf16[8,48,4096]{2,1,0:T(8,128)(2,1)} %bitcast.56), calls=%async_computation.1 | async-start | bytes 6291456 | tf_op jit(solution)/shard_map/all_to_all | solution.py:178
  107.7 0.0 copy-done.6
  107.7 0.1 copy.25
  107.8 0.1 mul.61
  107.9 0.1 reshape.109
  108.1 37.1 %all-to-all-done.1 = bf16[8,48,4096]{2,1,0:T(8,128)(2,1)} async-done(((bf16[8,48,4096]{2,1,0:T(8,128)(2,1)}), bf16[8,48,4096]{2,1,0:T(8,128)(2,1)}, u32[]{:S(2)}, u32[]{:S(2)}) %all-to-all-start.1) | async-done | bytes 3145760 | tf_op jit(solution)/shard_map/all_to_all | solution.py:178
  145.2 6.3 %gather_fusion = bf16[256,4096]{1,0:T(8,128)(2,1)S(1)} fusion(bf16[384,4096]{1,0:T(8,128)(2,1)} %bitcast.8, s32[1024]{0:T(1024)S(1)} %pad_clamp_fusion), kind=kCustom, calls=%fused_computation | custom fusion | bytes 4195328 | tf_op jit(solution)/shard_map/gather | solution.py:181
  151.5 1.6 convert_multiply_fusion
  153.1 3.5 %reshape.105 = f32[128,2,2048]{2,1,0:T(2,128)} reshape(f32[256,2048]{1,0:T(8,128)} %convert_multiply_fusion) | data formatting | bytes 4194304 | tf_op jit(solution)/shard_map/reshape | solution.py:185
  156.6 1.5 fusion.30
  158.1 1.8 reshape.108
  159.8 2.3 %fusion.21 = bf16[128,1,2]{2,1,0:T(2,128)(2,1)S(1)} fusion(bf16[128,2,2048]{2,1,0:T(2,128)(2,1)S(1)} %reshape.108, bf16[128,2048,1]{1,0,2:T(8,128)(2,1)S(1)} %bitcast.50), kind=kOutput, calls=%fused_computation.29 | convolution fusion | flops 1048576 | bytes 1573376 | tf_op jit(solution)/shard_map/tkd,td->tk/dot_general | solution.py:187
  162.1 0.6 copy.31
  162.8 2.6 %reshape.106 = bf16[128,2,2048]{2,1,0:T(2,128)(2,1)} reshape(bf16[256,2048]{1,0:T(8,128)(2,1)} %get-tuple-element.16) | data formatting | bytes 2097152 | tf_op jit(solution)/shard_map/reshape | solution.py:194
  165.4 0.0 copy-done.2
  165.4 3.8 %reduce_sum.57 = bf16[128,2048]{1,0:T(8,128)(2,1)} reduce(f32[128,2,2048]{2,1,0:T(2,128)S(1)} %copy-done.2, f32[]{:T(128)} %constant.17.clone.1), dimensions={1}, to_apply=%region_5.6 | reduce | flops 262144 | bytes 2621444 | tf_op jit(solution)/shard_map/reduce_sum | solution.py:184
  169.1 4.6 %reduce.1 = bf16[128,2048]{1,0:T(8,128)(2,1)} reduce(bf16[128,2,2048]{2,1,0:T(2,128)(2,1)} %reshape.106, bf16[]{:T(256)} %constant.14.clone.1), dimensions={1}, to_apply=%region_6.7.clone | reduce | flops 262144 | bytes 1572866 | tf_op jit(solution)/shard_map/reduce_sum | solution.py:193
  173.7 22.5 %reduce-scatter.4.cloned.1.call-done.red_ref = bf16[1,264,2048]{2,1,0:T(8,128)(2,1)} async-done(((bf16[16,264,2048]{2,1,0:T(8,128)(2,1)}), bf16[1,264,2048]{2,1,0:T(8,128)(2,1)}) %reduce-scatter.4.cloned.1.call-update) | async-done | bytes 1081360
  196.3 2.6 %shard_map.119 = (f32[128,1408]{1,0:T(8,128)}, f32[128,1408]{1,0:T(8,128)}, f32[88,2048]{1,0:T(8,128)}) custom-call(bf16[1,264,2048]{2,1,0:T(8,128)(2,1)} %reduce-scatter.4.cloned.1.call-done.red_ref), custom_call_target="tpu_custom_call" | custom-call | tf_op jit(solution)/shard_map/pallas_call | solution.py:101
  (13 shorter events, 0.1 us)
Async XLA Ops:
  7.2 4.9 %copy-start = (bf16[128,2048]{1,0:T(8,128)(2,1)S(1)}, bf16[128,2048]{1,0:T(8,128)(2,1)}, u32[]{:S(2)}) copy-start(bf16[128,2048]{1,0:T(8,128)(2,1)} %param.13) | copy-start | bytes 1572868
  7.2 189.1 %reduce-scatter.4.cloned.1.call-start = ((), (), s32[]{:S(2)}) async-start(), calls=%async_computation.3 | async-start | bytes 18382848
  12.1 45.1 %slice-start = ((s8[5767168]{0:T(1024)(128)(4,1)}), s8[4194304]{0:T(1024)(128)(4,1)S(1)}, s32[]{:S(2)}) async-start(s8[5767168]{0:T(1024)(128)(4,1)} %bitcast.61), calls=%async_computation.4 | async-start | bytes 8388608
  12.7 44.5 %slice-start.1 = ((s8[5767168]{0:T(1024)(128)(4,1)}), s8[1572864]{0:T(1024)(128)(4,1)S(1)}, s32[]{:S(2)}) async-start(s8[5767168]{0:T(1024)(128)(4,1)} %bitcast.61), calls=%async_computation.5 | async-start | bytes 3145728
  12.9 47.0 %slice-start.4 = ((s8[5767168]{0:T(1024)(128)(4,1)}), s8[4194304]{0:T(1024)(128)(4,1)S(1)}, s32[]{:S(2)}) async-start(s8[5767168]{0:T(1024)(128)(4,1)} %bitcast.65), calls=%async_computation.8 | async-start | bytes 8388608
  57.2 5.3 %copy-start.1 = (bf16[8,48,4096]{2,1,0:T(8,128)(2,1)}, bf16[8,48,4096]{2,1,0:T(8,128)(2,1)S(1)}, u32[]{:S(2)}) copy-start(bf16[8,48,4096]{2,1,0:T(8,128)(2,1)S(1)} %all_to_all.10) | copy-start | bytes 9437188
  57.2 2.7 %slice-start.5 = ((s8[5767168]{0:T(1024)(128)(4,1)}), s8[1572864]{0:T(1024)(128)(4,1)S(1)}, s32[]{:S(2)}) async-start(s8[5767168]{0:T(1024)(128)(4,1)} %bitcast.65), calls=%async_computation.9 | async-start | bytes 3145728
  57.3 5.3 %slice-start.2 = ((s8[5767168]{0:T(1024)(128)(4,1)}), s8[1572864]{0:T(1024)(128)(4,1)S(1)}, s32[]{:S(2)}) async-start(s8[5767168]{0:T(1024)(128)(4,1)} %bitcast.63), calls=%async_computation.6 | async-start | bytes 3145728
  59.9 2.6 %slice-start.3 = ((s8[5767168]{0:T(1024)(128)(4,1)}), s8[4194304]{0:T(1024)(128)(4,1)S(1)}, s32[]{:S(2)}) async-start(s8[5767168]{0:T(1024)(128)(4,1)} %bitcast.63), calls=%async_computation.7 | async-start | bytes 8388608
  66.8 1.7 copy-start.4
  83.6 1.2 copy-start.3
  84.8 5.3 %copy-start.5 = (bf16[384,1408]{1,0:T(8,128)(2,1)S(1)}, bf16[384,1408]{1,0:T(8,128)(2,1)}, u32[]{:S(2)}) copy-start(bf16[384,1408]{1,0:T(8,128)(2,1)} %copy-done.4) | copy-start | bytes 3244036
  102.2 5.5 %copy-start.6 = (bf16[128,2]{0,1:T(2,128)(2,1)S(1)}, bf16[128,2]{0,1:T(2,128)(2,1)}, u32[]{:S(2)}) copy-start(bf16[128,2]{0,1:T(2,128)(2,1)} %param.9) | copy-start | bytes 1540
  102.2 43.1 %all-to-all-start.1 = ((bf16[8,48,4096]{2,1,0:T(8,128)(2,1)}), bf16[8,48,4096]{2,1,0:T(8,128)(2,1)}, u32[]{:S(2)}, u32[]{:S(2)}) async-start(bf16[8,48,4096]{2,1,0:T(8,128)(2,1)} %bitcast.56), calls=%async_computation.1 | async-start | bytes 6291456 | tf_op jit(solution)/shard_map/all_to_all | solution.py:178
  162.1 3.2 %copy-start.2 = (f32[128,2,2048]{2,1,0:T(2,128)S(1)}, f32[128,2,2048]{2,1,0:T(2,128)}, u32[]{:S(2)}) copy-start(f32[128,2,2048]{2,1,0:T(2,128)} %reshape.105) | copy-start | bytes 6291460
Sparse Core Ops, SparseCore 0:
  83.7 112.4 reduce-scatter.3

commit v11 on v9

--- a/solution.py
+++ b/solution.py
@@ -36,13 +36,16 @@
         u = u_all[c * rows : (c + 1) * rows]
         o_ref[c, :rows, :ff] = g.astype(o_ref.dtype)
         o_ref[c, :rows, ff:] = u[:, : width - ff].astype(o_ref.dtype)
-        for i in range(rows // TILE_ROWS):
-            for j in range(col_tiles):
-                q, p = divmod(i * col_tiles + j, width // LANES)
-                src = u[i * TILE_ROWS : (i + 1) * TILE_ROWS, width - ff + j * LANES :][:, :LANES]
-                o_ref[
-                    c, rows + q * TILE_ROWS : rows + (q + 1) * TILE_ROWS, p * LANES : (p + 1) * LANES
-                ] = src.astype(o_ref.dtype)
+        per_row = width // LANES
+        for q in range(extra // TILE_ROWS):
+            pieces = []
+            for p in range(per_row):
+                i, j = divmod(q * per_row + p, col_tiles)
+                col = width - ff + j * LANES
+                pieces.append(u[i * TILE_ROWS : (i + 1) * TILE_ROWS, col : col + LANES])
+            o_ref[c, rows + q * TILE_ROWS : rows + (q + 1) * TILE_ROWS, :] = jnp.concatenate(
+                pieces, axis=1
+            ).astype(o_ref.dtype)
         start = pl.multiple_of((r * group + c) * down_rows, 8)
         o_ref[c, rows + extra :, :] = down_ref[pl.ds(start, down_rows), :].astype(o_ref.dtype)
 

time: 205 us -> 205 us (level)
  no operation moved by 1% of the time
where the time goes in v11:
time: 205 us
  waiting for transfers between devices  60.8 us (30%)
  blocking collectives  44.3 us (22%)
  matrix products  28.8 us (14%)
  local copies, waits for them, and re-layouts  19.2 us (9%)
  Pallas kernels  17.9 us (9%)
  between operations  14.4 us (7%)
  other arithmetic  13.7 us (7%)
  starting transfers between devices  5.61 us (3%)
    all_to_all x1, blocking collectives, body(): lax.all_to_all(disp, 'ep', split_axis=0, concat_axis=0, tiled=True)  44.3 us
    all_to_all x1, waiting for transfers between devices, body(): lax.all_to_all(back, 'ep', split_axis=0, concat_axis=0, tiled=True)  37.1 us
    unnamed x2, waiting for transfers between devices  23.7 us
    pallas_call x1, Pallas kernels, packed_weight_grads(): pl.pallas_call(_pack_kernel, grid=(n_rep // group,), in_specs=[pl.BlockSp...  15.3 us
    gather x1, local copies, waits for them, and re-layouts, body(): pair_back = returned[slot_index]  6.18 us
    all_to_all x1, starting transfers between devices, body(): lax.all_to_all(back, 'ep', split_axis=0, concat_axis=0, tiled=True)  5.58 us
    dot_general x1, matrix products, body(): jnp.dot(hidden, down_mat, preferred_element_type=jnp.float32)  5.48 us
    dot_general x1, matrix products, body(): lax.dot_general(up_delta, up_mat, contract, preferred_element_type=jnp.fl...  5 us
  transfers between devices with their start and end apart: 2, of which 2 were waited for; matrix products, arithmetic and copies ran while one was open for 22% of the time, Pallas kernels for 0%

profile of v11, /device:TPU:1, one launch (start us, length us, event | category | flops | bytes accessed | tf_op | source)
XLA Modules:
  0.0 204.7 jit_solution(12089464092800077595)
XLA Ops:
  7.2 0.0 copy-start
  7.2 0.0 reduce-scatter.4.cloned.1.call-start
  7.2 0.8 copy.26
  8.1 0.1 eq.42
  8.2 0.1 eq.38
  8.4 0.6 reduce-window.6
  8.9 0.2 slice_reduce_fusion
  9.2 0.1 fusion.27
  9.3 0.1 reduce_sum.53
  9.5 0.1 copy.29
  9.5 0.1 convert_reduce_fusion
  9.7 0.8 fusion.24
  10.5 1.6 convolution_convert_fusion.1
  12.1 0.0 copy-done
  12.1 0.0 slice-start.2
  12.1 0.6 convolution_convert_fusion
  12.7 0.0 slice-start.3
  12.7 0.2 pad_maximum_fusion
  12.9 0.0 slice-start.4
  13.0 44.3 %all_to_all.10 = bf16[8,48,4096]{2,1,0:T(8,128)(2,1)S(1)} all-to-all(bf16[8,48,4096]{2,1,0:T(8,128)(2,1)S(1)} %bitcast.57), channel_id=1, replica_groups=mesh['rep'=16,'ep'=8] {'ep'}, dimensions={0} | all-to-all | bytes 6291456 | tf_op jit(solution)/shard_map/all_to_all | solution.py:149
  57.2 0.0 slice-done.2
  57.2 0.0 slice-done.3
  57.2 0.0 slice-start.5
  57.3 0.0 slice-start
  57.3 2.6 %fusion = f32[384,1408]{1,0:T(8,128)S(1)} fusion(bf16[1,1408,2048]{2,1,0:T(8,128)(2,1)S(1)} %bitcast.64, bf16[384,4096]{1,0:T(8,128)(2,1)S(1)} %bitcast.51), kind=kOutput, calls=%fused_computation.1 | convolution fusion | flops 2214592512 | bytes 9502720 | tf_op jit(solution)/shard_map/dot_general | solution.py:161
  59.9 0.0 slice-done.4
  59.9 0.0 slice-done.5
  59.9 0.0 slice-start.1
  60.0 2.6 %fusion.10 = f32[384,1408]{1,0:T(8,128)S(1)} fusion(bf16[1,2048,1408]{2,1,0:T(8,128)(2,1)S(1)} %bitcast.66, bf16[384,4096]{1,0:T(8,128)(2,1)S(1)} %bitcast.52), kind=kOutput, calls=%fused_computation.11 | convolution fusion | flops 2214592512 | bytes 9502720 | tf_op jit(solution)/shard_map/dot_general | solution.py:156
  62.6 0.0 copy-done.1
  62.6 0.0 slice-done
  62.6 0.0 slice-done.1
  62.6 4.5 %multiply_convert_fusion.2 = (bf16[384,1408]{1,0:T(8,128)(2,1)}, bf16[384,1408]{1,0:T(8,128)(2,1)}, bf16[384,1408]{1,0:T(8,128)(2,1)}) fusion(f32[384,1408]{1,0:T(8,128)S(1)} %fusion.10, f32[384,1408]{1,0:T(8,128)S(1)} %fusion, bf16[1,2048,1408]{2,1,0:T(8,128)(2,1)S(1)} %bitcast.62, bf16[384,4096]{1,0:T(8,128)(2,1)S(1)} %bitcast.53), kind=kOutput, calls=%fused_computation.21 | convolution fusion | flops 2222702592 | bytes 14909440 | tf_op jit(solution)/shard_map/dot_general | solution.py:157
  67.1 15.3 %shard_map.118 = bf16[16,264,2048]{2,1,0:T(8,128)(2,1)} custom-call(bf16[384,4096]{1,0:T(8,128)(2,1)} %bitcast.54, bf16[384,1408]{1,0:T(8,128)(2,1)} %get-tuple-element.13.gd_ref, bf16[384,1408]{1,0:T(8,128)(2,1)} %get-tuple-element.14.ud_ref, bf16[384,1408]{1,0:T(8,128)(2,1)} %get-tuple-element.12.h_ref, bf16[384,4096]{1,0:T(8,128)(2,1)} %bitcast.55), custom_call_target="tpu_custom_call" | custom-call | flops 6643777536 | bytes 17301504 | tf_op jit(solution)/shard_map/pallas_call | solution.py:65
  82.5 0.0 reduce-scatter.4.cloned.1.call-update
  82.5 1.2 copy-done.6
  83.7 5.0 %fusion.4 = f32[384,2048]{1,0:T(8,128)S(1)} fusion(bf16[384,1408]{1,0:T(8,128)(2,1)S(1)} %copy-done.6, bf16[1,2048,1408]{2,1,0:T(8,128)(2,1)} %param.11), kind=kOutput, calls=%fused_computation.5 | convolution fusion | flops 2214592512 | bytes 9994240 | tf_op jit(solution)/shard_map/dot_general | solution.py:177
  88.7 0.0 copy-done.5
  88.7 0.0 copy-start.4
  88.7 0.0 slice-start.7
  88.7 5.5 %fusion.14 = bf16[384,2048]{1,0:T(8,128)(2,1)S(1)} fusion(bf16[384,1408]{1,0:T(8,128)(2,1)S(1)} %copy-done.5, bf16[1,1408,2048]{2,1,0:T(8,128)(2,1)} %param.12), kind=kOutput, calls=%fused_computation.16 | convolution fusion | flops 2215378944 | bytes 8421376 | tf_op jit(solution)/shard_map/dot_general | solution.py:174
  94.2 0.0 slice-done.6
  94.2 0.0 copy-done.4
  94.2 0.0 slice-done.7
  94.3 2.6 %add_convert_fusion = bf16[384,2048]{1,0:T(8,128)(2,1)S(1)} fusion(f32[384,2048]{1,0:T(8,128)S(1)} %fusion.4, bf16[384,1408]{1,0:T(8,128)(2,1)S(1)} %copy-done.4, bf16[1,2048,1408]{2,1,0:T(8,128)(2,1)S(1)} %bitcast.68), kind=kOutput, calls=%fused_computation.15 | convolution fusion | flops 2216165376 | bytes 11567104 | tf_op jit(solution)/shard_map/dot_general | solution.py:176
  96.9 2.0 pad_maximum_fusion.1
  98.9 5.6 %all-to-all-start.1 = ((bf16[8,48,4096]{2,1,0:T(8,128)(2,1)}), bf16[8,48,4096]{2,1,0:T(8,128)(2,1)}, u32[]{:S(2)}, u32[]{:S(2)}) async-start(bf16[8,48,4096]{2,1,0:T(8,128)(2,1)} %bitcast.56), calls=%async_computation.1 | async-start | bytes 6291456 | tf_op jit(solution)/shard_map/all_to_all | solution.py:182
  104.5 0.1 copy.25
  104.6 0.1 mul.61
  104.7 0.1 reshape.109
  104.9 37.1 %all-to-all-done.1 = bf16[8,48,4096]{2,1,0:T(8,128)(2,1)} async-done(((bf16[8,48,4096]{2,1,0:T(8,128)(2,1)}), bf16[8,48,4096]{2,1,0:T(8,128)(2,1)}, u32[]{:S(2)}, u32[]{:S(2)}) %all-to-all-start.1) | async-done | bytes 3145760 | tf_op jit(solution)/shard_map/all_to_all | solution.py:182
  142.0 6.2 %gather_fusion = bf16[256,4096]{1,0:T(8,128)(2,1)S(1)} fusion(bf16[384,4096]{1,0:T(8,128)(2,1)} %bitcast.8, s32[1024]{0:T(1024)S(1)} %pad_clamp_fusion), kind=kCustom, calls=%fused_computation | custom fusion | bytes 4195328 | tf_op jit(solution)/shard_map/gather | solution.py:185
  148.2 1.5 convert_multiply_fusion
  149.8 3.5 %reshape.105 = f32[128,2,2048]{2,1,0:T(2,128)} reshape(f32[256,2048]{1,0:T(8,128)} %convert_multiply_fusion) | data formatting | bytes 4194304 | tf_op jit(solution)/shard_map/reshape | solution.py:189
  153.2 1.5 fusion.30
  154.8 2.7 %reshape.106 = bf16[128,2,2048]{2,1,0:T(2,128)(2,1)} reshape(bf16[256,2048]{1,0:T(8,128)(2,1)} %get-tuple-element.16) | data formatting | bytes 2097152 | tf_op jit(solution)/shard_map/reshape | solution.py:198
  157.4 0.0 copy-done.3
  157.4 1.5 reshape.108
  158.9 3.7 %fusion.21 = bf16[128,1,2]{2,1,0:T(2,128)(2,1)S(1)} fusion(bf16[128,2,2048]{2,1,0:T(2,128)(2,1)} %reshape.108, bf16[128,2048,1]{1,0,2:T(8,128)(2,1)S(1)} %bitcast.50), kind=kOutput, calls=%fused_computation.28 | convolution fusion | flops 1048576 | bytes 1573376 | tf_op jit(solution)/shard_map/tkd,td->tk/dot_general | solution.py:191
  162.6 0.6 copy.31
  163.2 3.8 %reduce_sum.57 = bf16[128,2048]{1,0:T(8,128)(2,1)} reduce(f32[128,2,2048]{2,1,0:T(2,128)S(1)} %copy-done.2, f32[]{:T(128)} %constant.17.clone.1), dimensions={1}, to_apply=%region_5.6 | reduce | flops 262144 | bytes 2621444 | tf_op jit(solution)/shard_map/reduce_sum | solution.py:188
  167.0 4.6 %reduce.1 = bf16[128,2048]{1,0:T(8,128)(2,1)} reduce(bf16[128,2,2048]{2,1,0:T(2,128)(2,1)} %reshape.106, bf16[]{:T(256)} %constant.14.clone.1), dimensions={1}, to_apply=%region_6.7.clone | reduce | flops 262144 | bytes 1572866 | tf_op jit(solution)/shard_map/reduce_sum | solution.py:197
  171.6 23.6 %reduce-scatter.4.cloned.1.call-done.red_ref = bf16[1,264,2048]{2,1,0:T(8,128)(2,1)} async-done(((bf16[16,264,2048]{2,1,0:T(8,128)(2,1)}), bf16[1,264,2048]{2,1,0:T(8,128)(2,1)}) %reduce-scatter.4.cloned.1.call-update) | async-done | bytes 1081360
  195.2 2.6 %shard_map.119 = (f32[128,1408]{1,0:T(8,128)}, f32[128,1408]{1,0:T(8,128)}, f32[88,2048]{1,0:T(8,128)}) custom-call(bf16[1,264,2048]{2,1,0:T(8,128)(2,1)} %reduce-scatter.4.cloned.1.call-done.red_ref), custom_call_target="tpu_custom_call" | custom-call | tf_op jit(solution)/shard_map/pallas_call | solution.py:106
  (19 shorter events, 0.1 us)
Async XLA Ops:
  7.2 4.9 %copy-start = (bf16[128,2048]{1,0:T(8,128)(2,1)S(1)}, bf16[128,2048]{1,0:T(8,128)(2,1)}, u32[]{:S(2)}) copy-start(bf16[128,2048]{1,0:T(8,128)(2,1)} %param.13) | copy-start | bytes 1572868
  7.2 188.0 %reduce-scatter.4.cloned.1.call-start = ((), (), s32[]{:S(2)}) async-start(), calls=%async_computation.3 | async-start | bytes 18382848
  12.1 45.1 %slice-start.2 = ((s8[5767168]{0:T(1024)(128)(4,1)}), s8[4194304]{0:T(1024)(128)(4,1)S(1)}, s32[]{:S(2)}) async-start(s8[5767168]{0:T(1024)(128)(4,1)} %bitcast.63), calls=%async_computation.6 | async-start | bytes 8388608
  12.7 44.5 %slice-start.3 = ((s8[5767168]{0:T(1024)(128)(4,1)}), s8[1572864]{0:T(1024)(128)(4,1)S(1)}, s32[]{:S(2)}) async-start(s8[5767168]{0:T(1024)(128)(4,1)} %bitcast.63), calls=%async_computation.7 | async-start | bytes 3145728
  12.9 47.0 %slice-start.4 = ((s8[5767168]{0:T(1024)(128)(4,1)}), s8[4194304]{0:T(1024)(128)(4,1)S(1)}, s32[]{:S(2)}) async-start(s8[5767168]{0:T(1024)(128)(4,1)} %bitcast.65), calls=%async_computation.8 | async-start | bytes 8388608
  57.2 5.3 %copy-start.1 = (bf16[8,48,4096]{2,1,0:T(8,128)(2,1)}, bf16[8,48,4096]{2,1,0:T(8,128)(2,1)S(1)}, u32[]{:S(2)}) copy-start(bf16[8,48,4096]{2,1,0:T(8,128)(2,1)S(1)} %all_to_all.10) | copy-start | bytes 9437188
  57.2 2.7 %slice-start.5 = ((s8[5767168]{0:T(1024)(128)(4,1)}), s8[1572864]{0:T(1024)(128)(4,1)S(1)}, s32[]{:S(2)}) async-start(s8[5767168]{0:T(1024)(128)(4,1)} %bitcast.65), calls=%async_computation.9 | async-start | bytes 3145728
  57.3 5.3 %slice-start = ((s8[5767168]{0:T(1024)(128)(4,1)}), s8[4194304]{0:T(1024)(128)(4,1)S(1)}, s32[]{:S(2)}) async-start(s8[5767168]{0:T(1024)(128)(4,1)} %bitcast.61), calls=%async_computation.4 | async-start | bytes 8388608
  59.9 2.6 %slice-start.1 = ((s8[5767168]{0:T(1024)(128)(4,1)}), s8[1572864]{0:T(1024)(128)(4,1)S(1)}, s32[]{:S(2)}) async-start(s8[5767168]{0:T(1024)(128)(4,1)} %bitcast.61), calls=%async_computation.5 | async-start | bytes 3145728
  82.4 1.2 copy-start.6
  83.7 5.0 %copy-start.5 = (bf16[384,1408]{1,0:T(8,128)(2,1)S(1)}, bf16[384,1408]{1,0:T(8,128)(2,1)}, u32[]{:S(2)}) copy-start(bf16[384,1408]{1,0:T(8,128)(2,1)} %get-tuple-element.12.h_ref) | copy-start | bytes 3244036
  83.7 10.5 %slice-start.6 = ((s8[5767168]{0:T(1024)(128)(4,1)}), s8[4194304]{0:T(1024)(128)(4,1)S(1)}, s32[]{:S(2)}) async-start(s8[5767168]{0:T(1024)(128)(4,1)} %bitcast.67), calls=%async_computation.10 | async-start | bytes 8388608
  88.7 5.5 %copy-start.4 = (bf16[384,1408]{1,0:T(8,128)(2,1)S(1)}, bf16[384,1408]{1,0:T(8,128)(2,1)}, u32[]{:S(2)}) copy-start(bf16[384,1408]{1,0:T(8,128)(2,1)} %get-tuple-element.13.gd_ref) | copy-start | bytes 3244036
  88.7 5.5 %slice-start.7 = ((s8[5767168]{0:T(1024)(128)(4,1)}), s8[1572864]{0:T(1024)(128)(4,1)S(1)}, s32[]{:S(2)}) async-start(s8[5767168]{0:T(1024)(128)(4,1)} %bitcast.67), calls=%async_computation.11 | async-start | bytes 3145728
  98.9 5.6 %copy-start.7 = (bf16[128,2]{0,1:T(2,128)(2,1)S(1)}, bf16[128,2]{0,1:T(2,128)(2,1)}, u32[]{:S(2)}) copy-start(bf16[128,2]{0,1:T(2,128)(2,1)} %param.9) | copy-start | bytes 1540
  98.9 43.2 %all-to-all-start.1 = ((bf16[8,48,4096]{2,1,0:T(8,128)(2,1)}), bf16[8,48,4096]{2,1,0:T(8,128)(2,1)}, u32[]{:S(2)}, u32[]{:S(2)}) async-start(bf16[8,48,4096]{2,1,0:T(8,128)(2,1)} %bitcast.56), calls=%async_computation.1 | async-start | bytes 6291456 | tf_op jit(solution)/shard_map/all_to_all | solution.py:182
  154.8 2.7 %copy-start.3 = (bf16[256,2048]{1,0:T(8,128)(2,1)S(1)}, bf16[256,2048]{1,0:T(8,128)(2,1)}, u32[]{:S(2)}) copy-start(bf16[256,2048]{1,0:T(8,128)(2,1)} %get-tuple-element.15) | copy-start | bytes 3145732
  158.9 4.3 %copy-start.2 = (f32[128,2,2048]{2,1,0:T(2,128)S(1)}, f32[128,2,2048]{2,1,0:T(2,128)}, u32[]{:S(2)}) copy-start(f32[128,2,2048]{2,1,0:T(2,128)} %reshape.105) | copy-start | bytes 6291460
Sparse Core Ops, SparseCore 0:
  82.6 112.5 reduce-scatter.3

commit v12 on v9

--- a/solution.py
+++ b/solution.py
@@ -47,7 +47,7 @@
         o_ref[c, rows + extra :, :] = down_ref[pl.ds(start, down_rows), :].astype(o_ref.dtype)
 
 
-GROUP = 4
+GROUP = 2
 
 
 def packed_weight_grads(recv, gate_delta, up_delta, hidden, n_rep):

time: 205 us -> 206 us (level)
  no operation moved by 1% of the time
where the time goes in v12:
time: 206 us
  waiting for transfers between devices  60.8 us (30%)
  blocking collectives  44.3 us (22%)
  matrix products  28.8 us (14%)
  local copies, waits for them, and re-layouts  19.2 us (9%)
  Pallas kernels  18.9 us (9%)
  between operations  14.4 us (7%)
  other arithmetic  13.7 us (7%)
  starting transfers between devices  5.62 us (3%)
    all_to_all x1, blocking collectives, body(): lax.all_to_all(disp, 'ep', split_axis=0, concat_axis=0, tiled=True)  44.3 us
    all_to_all x1, waiting for transfers between devices, body(): lax.all_to_all(back, 'ep', split_axis=0, concat_axis=0, tiled=True)  37.1 us
    unnamed x2, waiting for transfers between devices  23.7 us
    pallas_call x1, Pallas kernels, packed_weight_grads(): pl.pallas_call(_pack_kernel, grid=(n_rep // group,), in_specs=[pl.BlockSp...  16.3 us
    gather x1, local copies, waits for them, and re-layouts, body(): pair_back = returned[slot_index]  6.18 us
    all_to_all x1, starting transfers between devices, body(): lax.all_to_all(back, 'ep', split_axis=0, concat_axis=0, tiled=True)  5.58 us
    dot_general x1, matrix products, body(): jnp.dot(hidden, down_mat, preferred_element_type=jnp.float32)  5.48 us
    dot_general x1, matrix products, body(): lax.dot_general(up_delta, up_mat, contract, preferred_element_type=jnp.fl...  5 us
  transfers between devices with their start and end apart: 2, of which 2 were waited for; matrix products, arithmetic and copies ran while one was open for 22% of the time, Pallas kernels for 0%

profile of v12, /device:TPU:1, one launch (start us, length us, event | category | flops | bytes accessed | tf_op | source)
XLA Modules:
  0.0 205.7 jit_solution(11860588651711657631)
XLA Ops:
  7.2 0.0 copy-start
  7.2 0.0 reduce-scatter.4.cloned.1.call-start
  7.2 0.8 copy.26
  8.1 0.1 eq.42
  8.2 0.1 eq.38
  8.4 0.6 reduce-window.6
  8.9 0.2 slice_reduce_fusion
  9.2 0.1 fusion.27
  9.3 0.1 reduce_sum.53
  9.5 0.1 copy.29
  9.5 0.1 convert_reduce_fusion
  9.7 0.8 fusion.24
  10.5 1.6 convolution_convert_fusion.1
  12.1 0.0 copy-done
  12.1 0.0 slice-start.2
  12.1 0.6 convolution_convert_fusion
  12.7 0.0 slice-start.3
  12.7 0.2 pad_maximum_fusion
  12.9 0.0 slice-start.4
  13.0 44.3 %all_to_all.10 = bf16[8,48,4096]{2,1,0:T(8,128)(2,1)S(1)} all-to-all(bf16[8,48,4096]{2,1,0:T(8,128)(2,1)S(1)} %bitcast.57), channel_id=1, replica_groups=mesh['rep'=16,'ep'=8] {'ep'}, dimensions={0} | all-to-all | bytes 6291456 | tf_op jit(solution)/shard_map/all_to_all | solution.py:146
  57.2 0.0 slice-done.2
  57.2 0.0 slice-done.3
  57.2 0.0 slice-start.5
  57.3 0.0 slice-start
  57.3 2.6 %fusion = f32[384,1408]{1,0:T(8,128)S(1)} fusion(bf16[1,1408,2048]{2,1,0:T(8,128)(2,1)S(1)} %bitcast.64, bf16[384,4096]{1,0:T(8,128)(2,1)S(1)} %bitcast.51), kind=kOutput, calls=%fused_computation.1 | convolution fusion | flops 2214592512 | bytes 9502720 | tf_op jit(solution)/shard_map/dot_general | solution.py:158
  59.9 0.0 slice-done.4
  59.9 0.0 slice-done.5
  59.9 0.0 slice-start.1
  60.0 2.6 %fusion.10 = f32[384,1408]{1,0:T(8,128)S(1)} fusion(bf16[1,2048,1408]{2,1,0:T(8,128)(2,1)S(1)} %bitcast.66, bf16[384,4096]{1,0:T(8,128)(2,1)S(1)} %bitcast.52), kind=kOutput, calls=%fused_computation.11 | convolution fusion | flops 2214592512 | bytes 9502720 | tf_op jit(solution)/shard_map/dot_general | solution.py:153
  62.6 0.0 copy-done.1
  62.6 0.0 slice-done
  62.6 0.0 slice-done.1
  62.6 4.5 %multiply_convert_fusion.2 = (bf16[384,1408]{1,0:T(8,128)(2,1)}, bf16[384,1408]{1,0:T(8,128)(2,1)}, bf16[384,1408]{1,0:T(8,128)(2,1)}) fusion(f32[384,1408]{1,0:T(8,128)S(1)} %fusion.10, f32[384,1408]{1,0:T(8,128)S(1)} %fusion, bf16[1,2048,1408]{2,1,0:T(8,128)(2,1)S(1)} %bitcast.62, bf16[384,4096]{1,0:T(8,128)(2,1)S(1)} %bitcast.53), kind=kOutput, calls=%fused_computation.21 | convolution fusion | flops 2222702592 | bytes 14909440 | tf_op jit(solution)/shard_map/dot_general | solution.py:154
  67.1 16.3 %shard_map.118 = bf16[16,264,2048]{2,1,0:T(8,128)(2,1)} custom-call(bf16[384,4096]{1,0:T(8,128)(2,1)} %bitcast.54, bf16[384,1408]{1,0:T(8,128)(2,1)} %get-tuple-element.13.gd_ref, bf16[384,1408]{1,0:T(8,128)(2,1)} %get-tuple-element.14.ud_ref, bf16[384,1408]{1,0:T(8,128)(2,1)} %get-tuple-element.12.h_ref, bf16[384,4096]{1,0:T(8,128)(2,1)} %bitcast.55), custom_call_target="tpu_custom_call" | custom-call | flops 6643777536 | bytes 17301504 | tf_op jit(solution)/shard_map/pallas_call | solution.py:62
  83.4 0.0 reduce-scatter.4.cloned.1.call-update
  83.4 1.2 copy-done.6
  84.7 5.0 %fusion.4 = f32[384,2048]{1,0:T(8,128)S(1)} fusion(bf16[384,1408]{1,0:T(8,128)(2,1)S(1)} %copy-done.6, bf16[1,2048,1408]{2,1,0:T(8,128)(2,1)} %param.11), kind=kOutput, calls=%fused_computation.5 | convolution fusion | flops 2214592512 | bytes 9994240 | tf_op jit(solution)/shard_map/dot_general | solution.py:174
  89.7 0.0 copy-done.5
  89.7 0.0 copy-start.4
  89.7 0.0 slice-start.7
  89.7 5.5 %fusion.14 = bf16[384,2048]{1,0:T(8,128)(2,1)S(1)} fusion(bf16[384,1408]{1,0:T(8,128)(2,1)S(1)} %copy-done.5, bf16[1,1408,2048]{2,1,0:T(8,128)(2,1)} %param.12), kind=kOutput, calls=%fused_computation.16 | convolution fusion | flops 2215378944 | bytes 8421376 | tf_op jit(solution)/shard_map/dot_general | solution.py:171
  95.2 0.0 slice-done.6
  95.2 0.0 copy-done.4
  95.2 0.0 slice-done.7
  95.2 2.6 %add_convert_fusion = bf16[384,2048]{1,0:T(8,128)(2,1)S(1)} fusion(f32[384,2048]{1,0:T(8,128)S(1)} %fusion.4, bf16[384,1408]{1,0:T(8,128)(2,1)S(1)} %copy-done.4, bf16[1,2048,1408]{2,1,0:T(8,128)(2,1)S(1)} %bitcast.68), kind=kOutput, calls=%fused_computation.15 | convolution fusion | flops 2216165376 | bytes 11567104 | tf_op jit(solution)/shard_map/dot_general | solution.py:173
  97.9 2.0 pad_maximum_fusion.1
  99.8 5.6 %all-to-all-start.1 = ((bf16[8,48,4096]{2,1,0:T(8,128)(2,1)}), bf16[8,48,4096]{2,1,0:T(8,128)(2,1)}, u32[]{:S(2)}, u32[]{:S(2)}) async-start(bf16[8,48,4096]{2,1,0:T(8,128)(2,1)} %bitcast.56), calls=%async_computation.1 | async-start | bytes 6291456 | tf_op jit(solution)/shard_map/all_to_all | solution.py:179
  105.4 0.1 copy.25
  105.6 0.1 mul.61
  105.7 0.1 reshape.109
  105.9 37.1 %all-to-all-done.1 = bf16[8,48,4096]{2,1,0:T(8,128)(2,1)} async-done(((bf16[8,48,4096]{2,1,0:T(8,128)(2,1)}), bf16[8,48,4096]{2,1,0:T(8,128)(2,1)}, u32[]{:S(2)}, u32[]{:S(2)}) %all-to-all-start.1) | async-done | bytes 3145760 | tf_op jit(solution)/shard_map/all_to_all | solution.py:179
  143.0 6.2 %gather_fusion = bf16[256,4096]{1,0:T(8,128)(2,1)S(1)} fusion(bf16[384,4096]{1,0:T(8,128)(2,1)} %bitcast.8, s32[1024]{0:T(1024)S(1)} %pad_clamp_fusion), kind=kCustom, calls=%fused_computation | custom fusion | bytes 4195328 | tf_op jit(solution)/shard_map/gather | solution.py:182
  149.2 1.5 convert_multiply_fusion
  150.7 3.5 %reshape.105 = f32[128,2,2048]{2,1,0:T(2,128)} reshape(f32[256,2048]{1,0:T(8,128)} %convert_multiply_fusion) | data formatting | bytes 4194304 | tf_op jit(solution)/shard_map/reshape | solution.py:186
  154.2 1.5 fusion.30
  155.7 2.6 %reshape.106 = bf16[128,2,2048]{2,1,0:T(2,128)(2,1)} reshape(bf16[256,2048]{1,0:T(8,128)(2,1)} %get-tuple-element.16) | data formatting | bytes 2097152 | tf_op jit(solution)/shard_map/reshape | solution.py:195
  158.4 0.0 copy-done.3
  158.4 1.5 reshape.108
  159.9 3.7 %fusion.21 = bf16[128,1,2]{2,1,0:T(2,128)(2,1)S(1)} fusion(bf16[128,2,2048]{2,1,0:T(2,128)(2,1)} %reshape.108, bf16[128,2048,1]{1,0,2:T(8,128)(2,1)S(1)} %bitcast.50), kind=kOutput, calls=%fused_computation.28 | convolution fusion | flops 1048576 | bytes 1573376 | tf_op jit(solution)/shard_map/tkd,td->tk/dot_general | solution.py:188
  163.6 0.6 copy.31
  164.2 3.8 %reduce_sum.57 = bf16[128,2048]{1,0:T(8,128)(2,1)} reduce(f32[128,2,2048]{2,1,0:T(2,128)S(1)} %copy-done.2, f32[]{:T(128)} %constant.17.clone.1), dimensions={1}, to_apply=%region_5.6 | reduce | flops 262144 | bytes 2621444 | tf_op jit(solution)/shard_map/reduce_sum | solution.py:185
  168.0 4.6 %reduce.1 = bf16[128,2048]{1,0:T(8,128)(2,1)} reduce(bf16[128,2,2048]{2,1,0:T(2,128)(2,1)} %reshape.106, bf16[]{:T(256)} %constant.14.clone.1), dimensions={1}, to_apply=%region_6.7.clone | reduce | flops 262144 | bytes 1572866 | tf_op jit(solution)/shard_map/reduce_sum | solution.py:194
  172.5 23.7 %reduce-scatter.4.cloned.1.call-done.red_ref = bf16[1,264,2048]{2,1,0:T(8,128)(2,1)} async-done(((bf16[16,264,2048]{2,1,0:T(8,128)(2,1)}), bf16[1,264,2048]{2,1,0:T(8,128)(2,1)}) %reduce-scatter.4.cloned.1.call-update) | async-done | bytes 1081360
  196.2 2.6 %shard_map.119 = (f32[128,1408]{1,0:T(8,128)}, f32[128,1408]{1,0:T(8,128)}, f32[88,2048]{1,0:T(8,128)}) custom-call(bf16[1,264,2048]{2,1,0:T(8,128)(2,1)} %reduce-scatter.4.cloned.1.call-done.red_ref), custom_call_target="tpu_custom_call" | custom-call | tf_op jit(solution)/shard_map/pallas_call | solution.py:103
  (19 shorter events, 0.1 us)
Async XLA Ops:
  7.2 4.9 %copy-start = (bf16[128,2048]{1,0:T(8,128)(2,1)S(1)}, bf16[128,2048]{1,0:T(8,128)(2,1)}, u32[]{:S(2)}) copy-start(bf16[128,2048]{1,0:T(8,128)(2,1)} %param.13) | copy-start | bytes 1572868
  7.2 189.0 %reduce-scatter.4.cloned.1.call-start = ((), (), s32[]{:S(2)}) async-start(), calls=%async_computation.3 | async-start | bytes 18382848
  12.1 45.1 %slice-start.2 = ((s8[5767168]{0:T(1024)(128)(4,1)}), s8[4194304]{0:T(1024)(128)(4,1)S(1)}, s32[]{:S(2)}) async-start(s8[5767168]{0:T(1024)(128)(4,1)} %bitcast.63), calls=%async_computation.6 | async-start | bytes 8388608
  12.7 44.5 %slice-start.3 = ((s8[5767168]{0:T(1024)(128)(4,1)}), s8[1572864]{0:T(1024)(128)(4,1)S(1)}, s32[]{:S(2)}) async-start(s8[5767168]{0:T(1024)(128)(4,1)} %bitcast.63), calls=%async_computation.7 | async-start | bytes 3145728
  12.9 47.0 %slice-start.4 = ((s8[5767168]{0:T(1024)(128)(4,1)}), s8[4194304]{0:T(1024)(128)(4,1)S(1)}, s32[]{:S(2)}) async-start(s8[5767168]{0:T(1024)(128)(4,1)} %bitcast.65), calls=%async_computation.8 | async-start | bytes 8388608
  57.2 5.3 %copy-start.1 = (bf16[8,48,4096]{2,1,0:T(8,128)(2,1)}, bf16[8,48,4096]{2,1,0:T(8,128)(2,1)S(1)}, u32[]{:S(2)}) copy-start(bf16[8,48,4096]{2,1,0:T(8,128)(2,1)S(1)} %all_to_all.10) | copy-start | bytes 9437188
  57.2 2.7 %slice-start.5 = ((s8[5767168]{0:T(1024)(128)(4,1)}), s8[1572864]{0:T(1024)(128)(4,1)S(1)}, s32[]{:S(2)}) async-start(s8[5767168]{0:T(1024)(128)(4,1)} %bitcast.65), calls=%async_computation.9 | async-start | bytes 3145728
  57.3 5.3 %slice-start = ((s8[5767168]{0:T(1024)(128)(4,1)}), s8[4194304]{0:T(1024)(128)(4,1)S(1)}, s32[]{:S(2)}) async-start(s8[5767168]{0:T(1024)(128)(4,1)} %bitcast.61), calls=%async_computation.4 | async-start | bytes 8388608
  59.9 2.6 %slice-start.1 = ((s8[5767168]{0:T(1024)(128)(4,1)}), s8[1572864]{0:T(1024)(128)(4,1)S(1)}, s32[]{:S(2)}) async-start(s8[5767168]{0:T(1024)(128)(4,1)} %bitcast.61), calls=%async_computation.5 | async-start | bytes 3145728
  83.4 1.2 copy-start.6
  84.7 5.0 %copy-start.5 = (bf16[384,1408]{1,0:T(8,128)(2,1)S(1)}, bf16[384,1408]{1,0:T(8,128)(2,1)}, u32[]{:S(2)}) copy-start(bf16[384,1408]{1,0:T(8,128)(2,1)} %get-tuple-element.12.h_ref) | copy-start | bytes 3244036
  84.7 10.5 %slice-start.6 = ((s8[5767168]{0:T(1024)(128)(4,1)}), s8[4194304]{0:T(1024)(128)(4,1)S(1)}, s32[]{:S(2)}) async-start(s8[5767168]{0:T(1024)(128)(4,1)} %bitcast.67), calls=%async_computation.10 | async-start | bytes 8388608
  89.7 5.5 %copy-start.4 = (bf16[384,1408]{1,0:T(8,128)(2,1)S(1)}, bf16[384,1408]{1,0:T(8,128)(2,1)}, u32[]{:S(2)}) copy-start(bf16[384,1408]{1,0:T(8,128)(2,1)} %get-tuple-element.13.gd_ref) | copy-start | bytes 3244036
  89.7 5.5 %slice-start.7 = ((s8[5767168]{0:T(1024)(128)(4,1)}), s8[1572864]{0:T(1024)(128)(4,1)S(1)}, s32[]{:S(2)}) async-start(s8[5767168]{0:T(1024)(128)(4,1)} %bitcast.67), calls=%async_computation.11 | async-start | bytes 3145728
  99.8 5.6 %copy-start.7 = (bf16[128,2]{0,1:T(2,128)(2,1)S(1)}, bf16[128,2]{0,1:T(2,128)(2,1)}, u32[]{:S(2)}) copy-start(bf16[128,2]{0,1:T(2,128)(2,1)} %param.9) | copy-start | bytes 1540
  99.8 43.2 %all-to-all-start.1 = ((bf16[8,48,4096]{2,1,0:T(8,128)(2,1)}), bf16[8,48,4096]{2,1,0:T(8,128)(2,1)}, u32[]{:S(2)}, u32[]{:S(2)}) async-start(bf16[8,48,4096]{2,1,0:T(8,128)(2,1)} %bitcast.56), calls=%async_computation.1 | async-start | bytes 6291456 | tf_op jit(solution)/shard_map/all_to_all | solution.py:179
  155.7 2.6 %copy-start.3 = (bf16[256,2048]{1,0:T(8,128)(2,1)S(1)}, bf16[256,2048]{1,0:T(8,128)(2,1)}, u32[]{:S(2)}) copy-start(bf16[256,2048]{1,0:T(8,128)(2,1)} %get-tuple-element.15) | copy-start | bytes 3145732
  159.9 4.3 %copy-start.2 = (f32[128,2,2048]{2,1,0:T(2,128)S(1)}, f32[128,2,2048]{2,1,0:T(2,128)}, u32[]{:S(2)}) copy-start(f32[128,2,2048]{2,1,0:T(2,128)} %reshape.105) | copy-start | bytes 6291460
Sparse Core Ops, SparseCore 0:
  83.6 112.5 reduce-scatter.3
